TPU v7x, 512 devices: a whole 4x8x8 slice. The times are simulated.
512 devices in a mesh: section: 32 (over z, x), et: 16 (over y, core).
Axes of the slice: x: 4, y: 8, z: 8, core: 2. Of those that a mesh axis runs over, the one named last changes fastest.
Arguments:
- x_fwd: bfloat16 [32, 256, 3072], P('section', 'et'), may hold values from -6 to 6
- act_fwd: bfloat16 [32, 256, 8192], P('section', None, 'et'), may hold values from -6 to 6
- ids_fwd: int32 [32, 256, 2], P('section'), may hold values from 0 to 7, as said below
- x_bwd: bfloat16 [32, 256, 3072], P('section', 'et'), may hold values from -6 to 6
- act_bwd: bfloat16 [32, 256, 8192], P('section', None, 'et'), may hold values from -6 to 6
- ids_bwd: int32 [32, 256, 2], P('section'), may hold values from 0 to 7, as said below
- grad_out: bfloat16 [32, 256, 3072], P('section', 'et'), may hold values from -6 to 6
- gain: bfloat16 [32, 3072], P('section'), may hold values from 0.099609375 to 1.8984375
- w_router: bfloat16 [32, 3072, 8], P('section'), may hold values from -0.21875 to 0.21875
- w_down: bfloat16 [32, 8192, 3072], P('section', 'et'), may hold values from -0.0625 to 0.0625
Outputs:
- fwd_in: bfloat16 [32, 256, 3072], P('section', 'et')
- incoming_gradient: bfloat16 [32, 256, 3072], P('section', 'et')
- dact: bfloat16 [32, 256, 8192], P('section', None, 'et')
Inputs may be any that keep to these rules, and one draw needn't show every extreme that they name: `ids_fwd`: each token names 2 different experts; in each section's micro-batch exactly 128 tokens name expert 0. `ids_bwd`: each token names 2 different experts; in each section's micro-batch exactly 128 tokens name expert 0.
All inputs are finite; a program needn't handle non-finite values.
Results may differ from a plain program's by a relative error of at most 0.014.
Values may be sent and summed in bfloat16 or wider, within the bound.
No kernel may reach another device: no remote copies, remote signals or barrier semaphores. Data moves between devices by JAX's collectives and lax.ppermute only.
A program may use at most 64 MiB of HBM per device.

v0:
```python
import jax
import jax.numpy as jnp
from jax import lax
from jax.sharding import PartitionSpec as P


def from_behind(value, axis, steps):
    count = lax.axis_size(axis)
    first, last = (max(0, -steps), min(count, count - steps))
    return lax.ppermute(value, axis, [(source, source + steps) for source in range(first, last)])


def norm_logits(inputs, gain, w_router):
    wide = inputs.astype(jnp.float32)
    inverse = lax.rsqrt(jnp.mean(wide * wide, axis=-1, keepdims=True) + 1e-05)
    normed = (wide * inverse * gain.astype(jnp.float32)).astype(jnp.bfloat16)
    logits = jnp.dot(normed, w_router, preferred_element_type=jnp.float32).astype(jnp.bfloat16)
    return (wide, inverse, logits)


def routing(logits, chosen, experts):
    route = jnp.sum((chosen == 0).astype(jnp.float32), axis=1)
    partner = jnp.minimum(jnp.sum(chosen, axis=1), experts - 1)
    labels = jnp.arange(experts, dtype=jnp.int32)
    onehot = (partner[:, None] == labels[None, :]).astype(jnp.float32)
    wide_logits = logits.astype(jnp.float32)
    sigma = jax.nn.sigmoid(wide_logits[:, 0] - jnp.sum(wide_logits * onehot, axis=1))
    return (route, onehot, sigma, route * sigma)


def arrange(chosen):
    member = jnp.sum((chosen == 0).astype(jnp.int32), axis=1)
    tally = jnp.sum(member)
    before = jnp.cumsum(member) - member
    after = jnp.cumsum(1 - member) - (1 - member)
    place = jnp.where(member == 1, before, tally + after)
    ordering = jnp.zeros_like(member).at[place].set(jnp.arange(member.shape[0], dtype=jnp.int32))
    return (member, place, ordering)


def spread_back(compact, member, place, capacity):
    safe = jnp.minimum(place, capacity - 1)
    return jnp.where(member[:, None] == 1, compact[safe], 0.0)


def shards(x_fwd, act_fwd, ids_fwd, x_bwd, act_bwd, ids_bwd, grad_out, gain, w_router, w_down):
    x_fwd, act_fwd, ids_fwd, x_bwd, act_bwd = (
        x_fwd[0],
        act_fwd[0],
        ids_fwd[0],
        x_bwd[0],
        act_bwd[0],
    )
    ids_bwd, grad_out, gain, w_router, w_down = (
        ids_bwd[0],
        grad_out[0],
        gain[0],
        w_router[0],
        w_down[0],
    )
    experts = w_router.shape[1]
    tokens = ids_fwd.shape[0]
    capacity = tokens // 2
    own_rows = x_fwd.shape[0]
    first_row = lax.axis_index("et") * own_rows
    wide_f, inverse_f, logit_f = norm_logits(x_fwd, gain, w_router)
    backward_wide_rows, backward_inverse_norm, logit_b = norm_logits(x_bwd, gain, w_router)
    full_f, full_b, full_g = (
        lax.all_gather(logit_f, "et", axis=0, tiled=True),
        lax.all_gather(logit_b, "et", axis=0, tiled=True),
        lax.all_gather(grad_out, "et", axis=0, tiled=True),
    )
    route_f, onehot_f, sigma_f, coef_f = routing(full_f, ids_fwd, experts)
    member_f, place_f, order_f = arrange(ids_fwd)
    chosen_f = order_f[:capacity]
    compact = (
        jnp.dot(act_fwd[chosen_f], w_down, preferred_element_type=jnp.float32)
        * coef_f[chosen_f][:, None]
    )
    summed = lax.psum(compact.astype(jnp.bfloat16), "et").astype(jnp.float32)
    member_own = lax.dynamic_slice_in_dim(member_f, first_row, own_rows, 0)
    place_own = lax.dynamic_slice_in_dim(place_f, first_row, own_rows, 0)
    y_mine = spread_back(summed, member_own, place_own, capacity)
    layer_out = (wide_f + y_mine).astype(jnp.bfloat16)
    route_b, onehot_b, sigma_b, backward_coefficient = routing(full_b, ids_bwd, experts)
    member_b, place_b, order_b = arrange(ids_bwd)
    chosen_b = order_b[:capacity]
    up_compact = lax.dot_general(
        full_g[chosen_b], w_down, (((1,), (1,)), ((), ())), preferred_element_type=jnp.float32
    )
    back_up = spread_back(up_compact, member_b, place_b, capacity)
    dact = (backward_coefficient[:, None] * back_up).astype(jnp.bfloat16)
    dprob_part = jnp.sum(act_bwd.astype(jnp.float32) * back_up, axis=1)
    dprob_all = lax.psum(dprob_part, "et")
    dprob_mine = lax.dynamic_slice_in_dim(dprob_all, first_row, own_rows, 0)
    route_mine = lax.dynamic_slice_in_dim(route_b, first_row, own_rows, 0)
    sigma_mine = lax.dynamic_slice_in_dim(sigma_b, first_row, own_rows, 0)
    onehot_mine = lax.dynamic_slice_in_dim(onehot_b, first_row, own_rows, 0)
    slope = route_mine * dprob_mine * sigma_mine * (1.0 - sigma_mine)
    router_wide = w_router.astype(jnp.float32)
    spread = router_wide[:, 0][None, :] - jnp.dot(
        onehot_mine, router_wide.T, precision=lax.Precision.HIGHEST
    )
    dnormed = slope[:, None] * spread
    scaled_rows = dnormed * gain.astype(jnp.float32)
    normalized_input = backward_wide_rows * backward_inverse_norm
    norm_input_gradient = backward_inverse_norm * (
        scaled_rows
        - normalized_input * jnp.mean(scaled_rows * normalized_input, axis=-1, keepdims=True)
    )
    input_grad = (grad_out.astype(jnp.float32) + norm_input_gradient).astype(jnp.bfloat16)
    fwd_in = from_behind(layer_out, "section", 1)
    incoming_gradient = from_behind(input_grad, "section", -1)
    return (fwd_in[None], incoming_gradient[None], dact[None])


def solution(mesh):
    placed = (
        P("section", "et", None),
        P("section", None, "et"),
        P("section", None, None),
        P("section", "et", None),
        P("section", None, "et"),
        P("section", None, None),
        P("section", "et", None),
        P("section", None),
        P("section", None, None),
        P("section", "et", None),
    )
    return jax.shard_map(
        shards,
        mesh=mesh,
        in_specs=placed,
        out_specs=(P("section", "et", None), P("section", "et", None), P("section", None, "et")),
        check_vma=False,
    )
```

profile of v0, /device:TPU:6, one launch (start us, length us, event | category | flops | bytes accessed | tf_op | source)
XLA Modules:
  0.0 256.7 jit_solution(1746351903962819599)
XLA Ops:
  7.2 0.9 convert_reduce_fusion.5
  8.1 1.4 convert_reduce_fusion
  11.9 1.4 scatter_custom_fusion
  14.1 1.0 fusion.22
  15.1 1.1 fusion.6
  16.3 17.6 %all-gather.1 = bf16[16,16,8]{1,2,0:T(8,128)(2,1)S(1)} all-gather(bf16[1,16,8]{1,2,0:T(8,128)(2,1)S(1)} %fusion.6), channel_id=1, replica_groups=mesh['section'=32,'et'=16] {'et'}, dimensions={0}, use_global_device_ids=true | all-gather | bytes 4352 | tf_op jit(solution)/shard_map/all_gather | solution.py:69
  34.1 1.9 gather_fusion
  36.0 1.3 gather_fusion.1
  37.3 1.5 fusion
  40.4 1.0 fusion.7
  42.6 1.2 compare_select_fusion
  43.8 1.4 scatter_custom_fusion.1
  45.9 15.0 %all-gather.2 = bf16[16,16,8]{1,2,0:T(8,128)(2,1)S(1)} all-gather(bf16[1,16,8]{1,2,0:T(8,128)(2,1)S(1)} %fusion.7), channel_id=1, replica_groups=mesh['section'=32,'et'=16] {'et'}, dimensions={0}, use_global_device_ids=true | all-gather | bytes 4352 | tf_op jit(solution)/shard_map/all_gather | solution.py:70
  63.9 1.4 slice_convert_fusion
  65.3 92.2 %all-reduce.2.cloned.1.call-done = bf16[128,3072]{1,0:T(8,128)(2,1)} async-done(((bf16[128,3072]{1,0:T(8,128)(2,1)}), bf16[128,3072]{1,0:T(8,128)(2,1)}) %all-reduce.2.cloned.1.call-update) | async-done | bytes 786448 | tf_op jit(solution)/shard_map/psum | solution.py:80
  157.6 2.4 convert_element_type.106
  160.0 2.2 gather_fusion.2
  162.2 0.8 fusion.23
  163.0 3.5 %collective-permute-start = (bf16[16,3072]{1,0:T(8,128)(2,1)S(1)}, bf16[16,3072]{1,0:T(8,128)(2,1)}, u32[]{:S(2)}, u32[]{:S(2)}) collective-permute-start(bf16[16,3072]{1,0:T(8,128)(2,1)S(1)} %fusion.23), channel_id=1, source_target_pairs={{0,16},{16,32},{32,48},{48,64},{64,80},{80,96},{96,112},{112,128},... | collective-permute-start | bytes 294920 | tf_op jit(solution)/shard_map/ppermute | solution.py:10
  167.2 2.4 collective-permute-done
  169.6 32.3 %all-gather.5.cloned.1.call-done = bf16[1,256,3072]{2,1,0:T(8,128)(2,1)} async-done(((bf16[1,16,3072]{2,1,0:T(8,128)(2,1)}), bf16[1,256,3072]{2,1,0:T(8,128)(2,1)}) %all-gather.5.cloned.1.call-update) | async-done | bytes 1572880 | tf_op jit(solution)/shard_map/all_gather | solution.py:71
  201.9 4.5 %gather_fusion.3 = bf16[128,3072]{1,0:T(8,128)(2,1)} fusion(bf16[256,3072]{1,0:T(8,128)(2,1)} %bitcast.108, s32[1024]{0:T(1024)} %pad_clamp_fusion.1), kind=kCustom, calls=%fused_computation.3 | custom fusion | bytes 1573376 | tf_op jit(solution)/shard_map/gather | solution.py:89
  206.3 2.3 fusion.3
  208.7 1.8 gather_fusion.4
  210.5 1.3 fusion.8
  211.8 24.9 %psum.15 = f32[256]{0:T(256)S(1)} all-reduce(f32[256]{0:T(256)S(1)} %fusion.8), channel_id=1, replica_groups=mesh['section'=32,'et'=16] {'et'}, use_global_device_ids=true, to_apply=%region_22.23 | all-reduce | flops 256 | bytes 2048 | tf_op jit(solution)/shard_map/psum | solution.py:94
  236.8 1.2 fusion.17
  238.0 1.0 fusion.21
  239.0 2.8 %collective-permute-start.1 = (bf16[16,3072]{1,0:T(8,128)(2,1)S(1)}, bf16[16,3072]{1,0:T(8,128)(2,1)S(1)}, u32[]{:S(2)}, u32[]{:S(2)}) collective-permute-start(bf16[16,3072]{1,0:T(8,128)(2,1)S(1)} %fusion.21), channel_id=1, source_target_pairs={{16,0},{32,16},{48,32},{64,48},{80,64},{96,80},{112,96},{128,112},... | collective-permute-start | bytes 294920 | tf_op jit(solution)/shard_map/ppermute | solution.py:10
  241.8 1.9 fusion.10
  243.7 4.0 %collective-permute-done.1 = bf16[16,3072]{1,0:T(8,128)(2,1)S(1)} collective-permute-done((bf16[16,3072]{1,0:T(8,128)(2,1)S(1)}, bf16[16,3072]{1,0:T(8,128)(2,1)S(1)}, u32[]{:S(2)}, u32[]{:S(2)}) %collective-permute-start.1) | collective-permute-done | bytes 98336 | tf_op jit(solution)/shard_map/ppermute | solution.py:10
  247.6 1.5 copy.20
  (79 shorter events, 11.3 us)
Async XLA Ops:
  7.2 30.1 %copy-start = (bf16[1,512,3072]{2,1,0:T(8,128)(2,1)S(1)}, bf16[1,512,3072]{2,1,0:T(8,128)(2,1)}, u32[]{:S(2)}) copy-start(bf16[1,512,3072]{2,1,0:T(8,128)(2,1)} %param.19) | copy-start | bytes 9437188
  7.2 150.4 %all-reduce.2.cloned.1.call-start = ((), (), s32[]{:S(2)}) async-start(), calls=%async_computation | async-start | bytes 1572864 | tf_op jit(solution)/shard_map/psum | solution.py:80
  34.0 6.2 %copy-start.2 = (bf16[1,16,3072]{2,1,0:T(8,128)(2,1)S(1)}, bf16[1,16,3072]{2,1,0:T(8,128)(2,1)}, u32[]{:S(2)}) copy-start(bf16[1,16,3072]{2,1,0:T(8,128)(2,1)} %param.13) | copy-start | bytes 294916
  35.9 25.7 %copy-start.4 = (s32[1,256,2]{1,2,0:T(2,128)S(1)}, s32[1,256,2]{1,2,0:T(2,128)}, u32[]{:S(2)}) copy-start(s32[1,256,2]{1,2,0:T(2,128)} %param.15) | copy-start | bytes 6148
  38.8 123.5 %copy-start.1 = (bf16[1,16,3072]{2,1,0:T(8,128)(2,1)S(1)}, bf16[1,16,3072]{2,1,0:T(8,128)(2,1)}, u32[]{:S(2)}) copy-start(bf16[1,16,3072]{2,1,0:T(8,128)(2,1)} %param.10) | copy-start | bytes 294916
  38.8 163.1 %all-gather.5.cloned.1.call-start = ((), (), s32[]{:S(2)}) async-start(), calls=%async_computation.1 | async-start | bytes 1671168 | tf_op jit(solution)/shard_map/all_gather | solution.py:71
  40.4 1.0 copy-start.9
  163.0 6.6 %collective-permute-start = (bf16[16,3072]{1,0:T(8,128)(2,1)S(1)}, bf16[16,3072]{1,0:T(8,128)(2,1)}, u32[]{:S(2)}, u32[]{:S(2)}) collective-permute-start(bf16[16,3072]{1,0:T(8,128)(2,1)S(1)} %fusion.23), channel_id=1, source_target_pairs={{0,16},{16,32},{32,48},{48,64},{64,80},{80,96},{96,112},{112,128},... | collective-permute-start | bytes 294920 | tf_op jit(solution)/shard_map/ppermute | solution.py:10
  208.7 1.8 copy-start.8
  208.7 28.0 %copy-start.6 = (f32[256]{0:T(256)S(1)}, f32[256]{0:T(256)}, u32[]{:S(2)}) copy-start(f32[256]{0:T(256)} %add_divide_fusion) | copy-start | bytes 3076
  208.7 28.1 %copy-start.3 = (f32[3072,1]{0,1:T(1,128)S(1)}, f32[3072,1]{0,1:T(1,128)}, u32[]{:S(2)}) copy-start(f32[3072,1]{0,1:T(1,128)} %slice_convert_fusion) | copy-start | bytes 36868
  208.7 28.1 %copy-start.7 = (pred[256,8]{0,1:T(8,128)(4,1)S(1)}, pred[256,8]{0,1:T(8,128)(4,1)}, u32[]{:S(2)}) copy-start(pred[256,8]{0,1:T(8,128)(4,1)} %iota_compare_fusion) | copy-start | bytes 6148
  208.7 33.1 %copy-start.5 = (f32[256,1]{0,1:T(1,128)S(1)}, f32[256,1]{0,1:T(1,128)}, u32[]{:S(2)}) copy-start(f32[256,1]{0,1:T(1,128)} %get-tuple-element.14) | copy-start | bytes 3076
  239.0 8.6 %collective-permute-start.1 = (bf16[16,3072]{1,0:T(8,128)(2,1)S(1)}, bf16[16,3072]{1,0:T(8,128)(2,1)S(1)}, u32[]{:S(2)}, u32[]{:S(2)}) collective-permute-start(bf16[16,3072]{1,0:T(8,128)(2,1)S(1)} %fusion.21), channel_id=1, source_target_pairs={{16,0},{32,16},{48,32},{64,48},{80,64},{96,80},{112,96},{128,112},... | collective-permute-start | bytes 294920 | tf_op jit(solution)/shard_map/ppermute | solution.py:10
Sparse Core Ops, SparseCore 0:
  38.9 118.5 all-reduce.1
  159.7 42.1 all-gather.4
where the time goes:
time: 257 us
  waiting for transfers between devices  132 us (51%)
  blocking collectives  57.5 us (22%)
  other arithmetic  22.1 us (9%)
  local copies, waits for them, and re-layouts  17.6 us (7%)
  between operations  14.3 us (6%)
  matrix products  7.15 us (3%)
  starting transfers between devices  6.38 us (2%)
    psum x1, waiting for transfers between devices, shards(): summed = lax.psum(compact.astype(jnp.bfloat16), 'et').astype(jnp.float32)  92.2 us
    all_gather x1, waiting for transfers between devices, shards(): lax.all_gather(grad_out, 'et', axis=0, tiled=True)  32.3 us
    psum x1, blocking collectives, shards(): dprob_all = lax.psum(dprob_part, 'et')  24.9 us
    all_gather x1, blocking collectives, shards(): lax.all_gather(logit_f, 'et', axis=0, tiled=True)  17.6 us
    all_gather x1, blocking collectives, shards(): lax.all_gather(logit_b, 'et', axis=0, tiled=True)  15 us
    ppermute x2, waiting for transfers between devices, from_behind(): lax.ppermute(value, axis, [(source, source + steps) for source in range(f...  6.38 us
    ppermute x2, starting transfers between devices, from_behind(): lax.ppermute(value, axis, [(source, source + steps) for source in range(f...  6.3 us
  transfers between devices with their start and end apart: 4, of which 4 were waited for; matrix products, arithmetic and copies ran while one was open for 7% of the time, Pallas kernels for 0%

commit v1 on v0

v1 whole, which is shorter than its diff:
```python
import jax
import jax.numpy as jnp
from jax import lax
from jax.sharding import PartitionSpec as P


def from_behind(value, axis, steps):
    count = lax.axis_size(axis)
    first, last = (max(0, -steps), min(count, count - steps))
    return lax.ppermute(value, axis, [(source, source + steps) for source in range(first, last)])


def norm_logits(inputs, gain, w_router):
    wide = inputs.astype(jnp.float32)
    inverse = lax.rsqrt(jnp.mean(wide * wide, axis=-1, keepdims=True) + 1e-05)
    normed = (wide * inverse * gain.astype(jnp.float32)).astype(jnp.bfloat16)
    logits = jnp.dot(normed, w_router, preferred_element_type=jnp.float32).astype(jnp.bfloat16)
    return (wide, inverse, logits)


def routing(logits, chosen, experts):
    route = jnp.sum((chosen == 0).astype(jnp.float32), axis=1)
    partner = jnp.minimum(jnp.sum(chosen, axis=1), experts - 1)
    labels = jnp.arange(experts, dtype=jnp.int32)
    onehot = (partner[:, None] == labels[None, :]).astype(jnp.float32)
    wide_logits = logits.astype(jnp.float32)
    sigma = jax.nn.sigmoid(wide_logits[:, 0] - jnp.sum(wide_logits * onehot, axis=1))
    return (route, onehot, sigma, route * sigma)


def shards(x_fwd, act_fwd, ids_fwd, x_bwd, act_bwd, ids_bwd, grad_out, gain, w_router, w_down):
    x_fwd, act_fwd, ids_fwd, x_bwd, act_bwd = (x_fwd[0], act_fwd[0], ids_fwd[0], x_bwd[0], act_bwd[0])
    ids_bwd, grad_out, gain, w_router, w_down = (ids_bwd[0], grad_out[0], gain[0], w_router[0], w_down[0])
    experts = w_router.shape[1]
    width = x_fwd.shape[1]
    own_rows = x_fwd.shape[0]
    groups = lax.axis_size("et")
    first_row = lax.axis_index("et") * own_rows
    pad = 128

    wide_f, inverse_f, logit_f = norm_logits(x_fwd, gain, w_router)
    backward_wide_rows, backward_inverse_norm, logit_b = norm_logits(x_bwd, gain, w_router)

    packed = jnp.concatenate(
        [grad_out, jnp.pad(logit_b, ((0, 0), (0, pad - experts)))], axis=1
    )
    tiled = jnp.broadcast_to(packed[None], (groups,) + packed.shape).reshape(groups * own_rows, -1)
    full = lax.all_to_all(tiled, "et", 0, 0, tiled=True)
    full_g = full[:, :width]
    full_b = full[:, width : width + experts]

    route_b, onehot_b, sigma_b, coef_b = routing(full_b, ids_bwd, experts)
    back_up = lax.dot_general(
        full_g, w_down, (((1,), (1,)), ((), ())), preferred_element_type=jnp.float32
    )
    dact = (coef_b[:, None] * back_up).astype(jnp.bfloat16)
    dprob_part = jnp.sum(act_bwd.astype(jnp.float32) * back_up, axis=1)
    dprob_hi = dprob_part.astype(jnp.bfloat16)
    dprob_lo = (dprob_part - dprob_hi.astype(jnp.float32)).astype(jnp.bfloat16)

    z_fwd = jnp.dot(act_fwd, w_down, preferred_element_type=jnp.float32).astype(jnp.bfloat16)
    extra = jnp.zeros((z_fwd.shape[0], pad), jnp.bfloat16)
    extra = extra.at[:, 0].set(dprob_hi).at[:, 1].set(dprob_lo)
    sent = jnp.concatenate([z_fwd, extra], axis=1)
    got = lax.all_to_all(sent, "et", 0, 0, tiled=True).reshape(groups, own_rows, -1)
    got = got.astype(jnp.float32)
    z_sum = jnp.sum(got[:, :, :width], axis=0)
    dprob_mine = jnp.sum(got[:, :, width] + got[:, :, width + 1], axis=0)

    ids_f_own = lax.dynamic_slice_in_dim(ids_fwd, first_row, own_rows, 0)
    _, _, _, coef_f = routing(logit_f, ids_f_own, experts)
    layer_out = (wide_f + coef_f[:, None] * z_sum).astype(jnp.bfloat16)

    ids_b_own = lax.dynamic_slice_in_dim(ids_bwd, first_row, own_rows, 0)
    route_mine, onehot_mine, sigma_mine, _ = routing(logit_b, ids_b_own, experts)
    slope = route_mine * dprob_mine * sigma_mine * (1.0 - sigma_mine)
    router_wide = w_router.astype(jnp.float32)
    spread = router_wide[:, 0][None, :] - jnp.dot(
        onehot_mine, router_wide.T, precision=lax.Precision.HIGHEST
    )
    dnormed = slope[:, None] * spread
    scaled_rows = dnormed * gain.astype(jnp.float32)
    normalized_input = backward_wide_rows * backward_inverse_norm
    norm_input_gradient = backward_inverse_norm * (
        scaled_rows
        - normalized_input * jnp.mean(scaled_rows * normalized_input, axis=-1, keepdims=True)
    )
    input_grad = (grad_out.astype(jnp.float32) + norm_input_gradient).astype(jnp.bfloat16)
    fwd_in = from_behind(layer_out, "section", 1)
    incoming_gradient = from_behind(input_grad, "section", -1)
    return (fwd_in[None], incoming_gradient[None], dact[None])


def solution(mesh):
    placed = (
        P("section", "et", None),
        P("section", None, "et"),
        P("section", None, None),
        P("section", "et", None),
        P("section", None, "et"),
        P("section", None, None),
        P("section", "et", None),
        P("section", None),
        P("section", None, None),
        P("section", "et", None),
    )
    return jax.shard_map(
        shards,
        mesh=mesh,
        in_specs=placed,
        out_specs=(P("section", "et", None), P("section", "et", None), P("section", None, "et")),
        check_vma=False,
    )
```

time: 257 us -> 125 us (0.49)
  the two profiles are of different devices: /device:TPU:6 before, /device:TPU:257 now
where the time goes in v1:
time: 125 us
  waiting for transfers between devices  83.6 us (67%)
  starting transfers between devices  17.5 us (14%)
  other arithmetic  11.6 us (9%)
  matrix products  7.09 us (6%)
  local copies, waits for them, and re-layouts  4.15 us (3%)
    all_to_all x1, waiting for transfers between devices, shards(): lax.all_to_all(sent, 'et', 0, 0, tiled=True).reshape(groups, own_rows, -1)  39.3 us
    all_to_all x1, waiting for transfers between devices, shards(): full = lax.all_to_all(tiled, 'et', 0, 0, tiled=True)  36.5 us
    ppermute x2, waiting for transfers between devices, from_behind(): lax.ppermute(value, axis, [(source, source + steps) for source in range(f...  7.84 us
    all_to_all x1, starting transfers between devices, shards(): full = lax.all_to_all(tiled, 'et', 0, 0, tiled=True)  7.79 us
    ppermute x2, starting transfers between devices, from_behind(): lax.ppermute(value, axis, [(source, source + steps) for source in range(f...  5.4 us
    all_to_all x1, starting transfers between devices, shards(): lax.all_to_all(sent, 'et', 0, 0, tiled=True).reshape(groups, own_rows, -1)  4.32 us
    dot_general x1, matrix products, shards(): lax.dot_general(full_g, w_down, (((1,), (1,)), ((), ())), preferred_eleme...  3.25 us
    concatenate x1, other arithmetic, shards(): sent = jnp.concatenate([z_fwd, extra], axis=1)  2.75 us
  transfers between devices with their start and end apart: 4, of which 4 were waited for; matrix products, arithmetic and copies ran while one was open for 3% of the time, Pallas kernels for 0%

profile of v1, /device:TPU:257, one launch (start us, length us, event | category | flops | bytes accessed | tf_op | source)
XLA Modules:
  0.0 124.8 jit_solution(17442643203819891960)
XLA Ops:
  0.7 0.9 dynamic-slice_reduce_fusion
  1.6 0.8 mul.190
  2.4 1.0 fusion.22
  3.5 1.1 select_reduce_fusion.1
  4.7 0.9 fusion.30
  5.6 1.3 %broadcast_in_dim.8 = bf16[16,16,3200]{2,1,0:T(8,128)(2,1)} broadcast(bf16[16,3200]{1,0:T(8,128)(2,1)S(1)} %fusion.30), dimensions={1,2} | broadcast | bytes 1740800 | tf_op jit(solution)/shard_map/broadcast_in_dim | solution.py:47
  6.9 7.8 %all-to-all-start = ((bf16[16,16,3200]{2,1,0:T(8,128)(2,1)}), bf16[16,16,3200]{2,1,0:T(8,128)(2,1)}, u32[]{:S(2)}, u32[]{:S(2)}) async-start(bf16[16,16,3200]{2,1,0:T(8,128)(2,1)} %broadcast_in_dim.8), calls=%async_computation | async-start | bytes 3276800 | tf_op jit(solution)/shard_map/all_to_all | solution.py:48
  14.7 0.6 compare_reduce_fusion
  15.3 0.6 compare_reduce_fusion.1
  16.0 2.1 %convolution_convert_fusion = bf16[256,3072]{1,0:T(8,128)(2,1)} fusion(bf16[1,512,3072]{2,1,0:T(8,128)(2,1)S(1)} %copy-done, bf16[1,256,512]{2,1,0:T(8,128)(2,1)S(1)} %copy-done.4), kind=kOutput, calls=%fused_computation | convolution fusion | flops 806092800 | bytes 4980736 | tf_op jit(solution)/shard_map/dot_general | solution.py:61
  18.2 36.5 %all-to-all-done = bf16[16,16,3200]{2,1,0:T(8,128)(2,1)} async-done(((bf16[16,16,3200]{2,1,0:T(8,128)(2,1)}), bf16[16,16,3200]{2,1,0:T(8,128)(2,1)}, u32[]{:S(2)}, u32[]{:S(2)}) %all-to-all-start) | async-done | bytes 1638432 | tf_op jit(solution)/shard_map/all_to_all | solution.py:48
  54.6 0.8 slice.71
  55.6 3.2 %fusion.8 = (bf16[1,256,512]{2,1,0:T(8,128)(2,1)}, f32[256]{0:T(256)S(1)}) fusion(f32[256]{0:T(256)S(1)} %bitcast.126, bf16[1,256,512]{2,1,0:T(8,128)(2,1)} %param.18, bf16[1,512,3072]{2,1,0:T(8,128)(2,1)S(1)} %copy-done, bf16[256,3200]{1,0:T(8,128)(2,1)} %bitcast.13), kind=kOutput, calls=%fused_computation.16 | convolution fusion | flops 805961472 | bytes 5244928 | tf_op jit(solution)/shard_map/dot_general | solution.py:53
  58.8 0.1 copy.24
  59.0 1.3 %fusion.39 = (bf16[256,1]{1,0:T(8,128)(2,1)S(1)}, bf16[256,1]{1,0:T(8,128)(2,1)S(1)}) fusion(f32[256,1]{1,0:T(8,128)S(1)} %copy.24, pred[]{:T(512)} %compare_reduce_fusion, pred[]{:T(512)} %compare_reduce_fusion.1), kind=kLoop, calls=%fused_computation.52 | loop fusion | flops 1536 | bytes 2050 | tf_op jit(solution)/shard_map/select.16
  60.3 0.3 scatter.9
  60.6 2.7 %pad_maximum_fusion = bf16[256,3200]{1,0:T(8,128)(2,1)} fusion(bf16[256,128]{1,0:T(8,128)(2,1)S(1)} %scatter.9, bf16[256,3072]{1,0:T(8,128)(2,1)} %convolution_convert_fusion), kind=kLoop, calls=%fused_computation.8 | loop fusion | flops 3276800 | bytes 3276800 | tf_op jit(solution)/shard_map/concatenate | solution.py:64
  63.4 4.3 %all-to-all-start.1 = ((bf16[16,16,3200]{2,1,0:T(8,128)(2,1)}), bf16[16,16,3200]{2,1,0:T(8,128)(2,1)}, u32[]{:S(2)}, u32[]{:S(2)}) async-start(bf16[16,16,3200]{2,1,0:T(8,128)(2,1)} %bitcast.114), calls=%async_computation.1 | async-start | bytes 3276800 | tf_op jit(solution)/shard_map/all_to_all | solution.py:65
  67.8 0.1 fusion.25
  68.0 0.2 select_reduce_fusion.2
  68.3 39.3 %all-to-all-done.1 = bf16[16,16,3200]{2,1,0:T(8,128)(2,1)} async-done(((bf16[16,16,3200]{2,1,0:T(8,128)(2,1)}), bf16[16,16,3200]{2,1,0:T(8,128)(2,1)}, u32[]{:S(2)}, u32[]{:S(2)}) %all-to-all-start.1) | async-done | bytes 1638432 | tf_op jit(solution)/shard_map/all_to_all | solution.py:65
  107.5 1.6 %convert_element_type.138 = f32[16,16,3200]{2,1,0:T(8,128)S(1)} convert(bf16[16,16,3200]{2,1,0:T(8,128)(2,1)} %all-to-all-done.1) | non-fusion elementwise | flops 819200 | bytes 4915200 | tf_op jit(solution)/shard_map/convert_element_type | solution.py:66
  109.2 0.2 fusion.29
  109.4 0.1 slice_reduce_fusion
  109.6 0.3 fusion.17
  109.9 0.1 copy-done.3
  110.2 3.5 %collective-permute-start.1 = (bf16[16,3072]{1,0:T(8,128)(2,1)S(1)}, bf16[16,3072]{1,0:T(8,128)(2,1)S(1)}, u32[]{:S(2)}, u32[]{:S(2)}) collective-permute-start(bf16[16,3072]{1,0:T(8,128)(2,1)S(1)} %fusion.21), channel_id=1, source_target_pairs={{16,0},{32,16},{48,32},{64,48},{80,64},{96,80},{112,96},{128,112},... | collective-permute-start | bytes 294920 | tf_op jit(solution)/shard_map/ppermute | solution.py:10
  113.8 1.9 %collective-permute-start = (bf16[16,3072]{1,0:T(8,128)(2,1)S(1)}, bf16[16,3072]{1,0:T(8,128)(2,1)S(1)}, u32[]{:S(2)}, u32[]{:S(2)}) collective-permute-start(bf16[16,3072]{1,0:T(8,128)(2,1)S(1)} %fusion.26), channel_id=1, source_target_pairs={{0,16},{16,32},{32,48},{48,64},{64,80},{80,96},{96,112},{112,128},... | collective-permute-start | bytes 294920 | tf_op jit(solution)/shard_map/ppermute | solution.py:10
  115.7 1.1 collective-permute-done.1
  116.9 6.7 %collective-permute-done = bf16[16,3072]{1,0:T(8,128)(2,1)S(1)} collective-permute-done((bf16[16,3072]{1,0:T(8,128)(2,1)S(1)}, bf16[16,3072]{1,0:T(8,128)(2,1)S(1)}, u32[]{:S(2)}, u32[]{:S(2)}) %collective-permute-start) | collective-permute-done | bytes 98336 | tf_op jit(solution)/shard_map/ppermute | solution.py:10
  123.6 0.6 copy.32
  124.2 0.6 copy.33
  (36 shorter events, 0.7 us)
Async XLA Ops:
  0.6 15.4 %copy-start = (bf16[1,512,3072]{2,1,0:T(8,128)(2,1)S(1)}, bf16[1,512,3072]{2,1,0:T(8,128)(2,1)}, u32[]{:S(2)}) copy-start(bf16[1,512,3072]{2,1,0:T(8,128)(2,1)} %param.23) | copy-start | bytes 9437188
  0.6 14.0 %copy-start.5 = (s32[1,256,2]{1,2,0:T(2,128)S(1)}, s32[1,256,2]{1,2,0:T(2,128)}, u32[]{:S(2)}) copy-start(s32[1,256,2]{1,2,0:T(2,128)} %param.19) | copy-start | bytes 6148
  0.7 15.3 %copy-start.4 = (bf16[1,256,512]{2,1,0:T(8,128)(2,1)S(1)}, bf16[1,256,512]{2,1,0:T(8,128)(2,1)}, u32[]{:S(2)}) copy-start(bf16[1,256,512]{2,1,0:T(8,128)(2,1)} %param.15) | copy-start | bytes 786436
  6.9 47.7 %all-to-all-start = ((bf16[16,16,3200]{2,1,0:T(8,128)(2,1)}), bf16[16,16,3200]{2,1,0:T(8,128)(2,1)}, u32[]{:S(2)}, u32[]{:S(2)}) async-start(bf16[16,16,3200]{2,1,0:T(8,128)(2,1)} %broadcast_in_dim.8), calls=%async_computation | async-start | bytes 3276800 | tf_op jit(solution)/shard_map/all_to_all | solution.py:48
  60.6 7.1 %copy-start.7 = (s32[1,256,2]{1,2,0:T(2,128)S(1)}, s32[1,256,2]{1,2,0:T(2,128)}, u32[]{:S(2)}) copy-start(s32[1,256,2]{1,2,0:T(2,128)} %param.16) | copy-start | bytes 6148
  60.6 7.2 %copy-start.1 = (bf16[1,16,3072]{2,1,0:T(8,128)(2,1)S(1)}, bf16[1,16,3072]{2,1,0:T(8,128)(2,1)}, u32[]{:S(2)}) copy-start(bf16[1,16,3072]{2,1,0:T(8,128)(2,1)} %param.14) | copy-start | bytes 294916
  60.6 7.4 %copy-start.6 = (bf16[1,3072,8]{1,2,0:T(8,128)(2,1)S(1)}, bf16[1,3072,8]{1,2,0:T(8,128)(2,1)}, u32[]{:S(2)}) copy-start(bf16[1,3072,8]{1,2,0:T(8,128)(2,1)} %param.22) | copy-start | bytes 147460
  63.4 44.2 %all-to-all-start.1 = ((bf16[16,16,3200]{2,1,0:T(8,128)(2,1)}), bf16[16,16,3200]{2,1,0:T(8,128)(2,1)}, u32[]{:S(2)}, u32[]{:S(2)}) async-start(bf16[16,16,3200]{2,1,0:T(8,128)(2,1)} %bitcast.114), calls=%async_computation.1 | async-start | bytes 3276800 | tf_op jit(solution)/shard_map/all_to_all | solution.py:65
  68.3 41.3 %copy-start.2 = (bf16[1,16,3072]{2,1,0:T(8,128)(2,1)S(1)}, bf16[1,16,3072]{2,1,0:T(8,128)(2,1)}, u32[]{:S(2)}) copy-start(bf16[1,16,3072]{2,1,0:T(8,128)(2,1)} %param.17) | copy-start | bytes 294916
  109.2 0.9 copy-start.3
  110.2 6.7 %collective-permute-start.1 = (bf16[16,3072]{1,0:T(8,128)(2,1)S(1)}, bf16[16,3072]{1,0:T(8,128)(2,1)S(1)}, u32[]{:S(2)}, u32[]{:S(2)}) collective-permute-start(bf16[16,3072]{1,0:T(8,128)(2,1)S(1)} %fusion.21), channel_id=1, source_target_pairs={{16,0},{32,16},{48,32},{64,48},{80,64},{96,80},{112,96},{128,112},... | collective-permute-start | bytes 294920 | tf_op jit(solution)/shard_map/ppermute | solution.py:10
  113.8 9.8 %collective-permute-start = (bf16[16,3072]{1,0:T(8,128)(2,1)S(1)}, bf16[16,3072]{1,0:T(8,128)(2,1)S(1)}, u32[]{:S(2)}, u32[]{:S(2)}) collective-permute-start(bf16[16,3072]{1,0:T(8,128)(2,1)S(1)} %fusion.26), channel_id=1, source_target_pairs={{0,16},{16,32},{32,48},{48,64},{64,80},{80,96},{96,112},{112,128},... | collective-permute-start | bytes 294920 | tf_op jit(solution)/shard_map/ppermute | solution.py:10

commit v2 on v1

--- a/solution.py
+++ b/solution.py
@@ -34,8 +34,8 @@
     experts = w_router.shape[1]
     width = x_fwd.shape[1]
     own_rows = x_fwd.shape[0]
-    groups = lax.axis_size("et")
-    first_row = lax.axis_index("et") * own_rows
+    groups = lax.axis_size("ety") * lax.axis_size("etc")
+    first_row = (lax.axis_index("ety") * lax.axis_size("etc") + lax.axis_index("etc")) * own_rows
     pad = 128
 
     wide_f, inverse_f, logit_f = norm_logits(x_fwd, gain, w_router)
@@ -44,8 +44,16 @@
     packed = jnp.concatenate(
         [grad_out, jnp.pad(logit_b, ((0, 0), (0, pad - experts)))], axis=1
     )
-    tiled = jnp.broadcast_to(packed[None], (groups,) + packed.shape).reshape(groups * own_rows, -1)
-    full = lax.all_to_all(tiled, "et", 0, 0, tiled=True)
+    chips = lax.axis_size("ety")
+    core = lax.axis_index("etc")
+    tiled = jnp.broadcast_to(packed[None], (chips,) + packed.shape).reshape(chips * own_rows, -1)
+    same_core = lax.all_to_all(tiled, "ety", 0, 0, tiled=True).reshape(chips, 1, own_rows, -1)
+    other_core = lax.ppermute(same_core, "etc", [(0, 1), (1, 0)])
+    full = jnp.where(
+        core == 0,
+        jnp.concatenate([same_core, other_core], axis=1),
+        jnp.concatenate([other_core, same_core], axis=1),
+    ).reshape(groups * own_rows, -1)
     full_g = full[:, :width]
     full_b = full[:, width : width + experts]
 
@@ -59,10 +67,29 @@
     dprob_lo = (dprob_part - dprob_hi.astype(jnp.float32)).astype(jnp.bfloat16)
 
     z_fwd = jnp.dot(act_fwd, w_down, preferred_element_type=jnp.float32).astype(jnp.bfloat16)
-    extra = jnp.zeros((z_fwd.shape[0], pad), jnp.bfloat16)
-    extra = extra.at[:, 0].set(dprob_hi).at[:, 1].set(dprob_lo)
-    sent = jnp.concatenate([z_fwd, extra], axis=1)
-    got = lax.all_to_all(sent, "et", 0, 0, tiled=True).reshape(groups, own_rows, -1)
+    z_fwd = z_fwd.reshape(chips, 2, own_rows, width)
+    d_split = jnp.stack([dprob_hi, dprob_lo], axis=-1).reshape(chips, 2, own_rows, 2)
+    mine_z = jnp.where(core == 0, z_fwd[:, 0], z_fwd[:, 1])
+    give_z = jnp.where(core == 0, z_fwd[:, 1], z_fwd[:, 0])
+    mine_d = jnp.where(core == 0, d_split[:, 0], d_split[:, 1])
+    give_d = jnp.where(core == 0, d_split[:, 1], d_split[:, 0])
+    given = lax.ppermute(
+        jnp.concatenate([give_z, jnp.pad(give_d, ((0, 0), (0, 0), (0, pad - 2)))], axis=-1),
+        "etc",
+        [(0, 1), (1, 0)],
+    )
+    pair_z = (mine_z.astype(jnp.float32) + given[..., :width].astype(jnp.float32)).astype(jnp.bfloat16)
+    pair_d = jnp.sum(mine_d.astype(jnp.float32), axis=-1) + jnp.sum(
+        given[..., width : width + 2].astype(jnp.float32), axis=-1
+    )
+    pair_hi = pair_d.astype(jnp.bfloat16)
+    pair_lo = (pair_d - pair_hi.astype(jnp.float32)).astype(jnp.bfloat16)
+    extra = jnp.concatenate(
+        [pair_hi[..., None], pair_lo[..., None], jnp.zeros((chips, own_rows, pad - 2), jnp.bfloat16)],
+        axis=-1,
+    )
+    sent = jnp.concatenate([pair_z, extra], axis=-1).reshape(chips * own_rows, -1)
+    got = lax.all_to_all(sent, "ety", 0, 0, tiled=True).reshape(chips, own_rows, -1)
     got = got.astype(jnp.float32)
     z_sum = jnp.sum(got[:, :, :width], axis=0)
     dprob_mine = jnp.sum(got[:, :, width] + got[:, :, width + 1], axis=0)
@@ -92,22 +119,25 @@
 
 
 def solution(mesh):
+    sections, ets = mesh.devices.shape
+    mesh = jax.sharding.Mesh(mesh.devices.reshape(sections, ets // 2, 2), ("section", "ety", "etc"))
+    et = ("ety", "etc")
     placed = (
-        P("section", "et", None),
-        P("section", None, "et"),
+        P("section", et, None),
+        P("section", None, et),
         P("section", None, None),
-        P("section", "et", None),
-        P("section", None, "et"),
+        P("section", et, None),
+        P("section", None, et),
         P("section", None, None),
-        P("section", "et", None),
+        P("section", et, None),
         P("section", None),
         P("section", None, None),
-        P("section", "et", None),
+        P("section", et, None),
     )
     return jax.shard_map(
         shards,
         mesh=mesh,
         in_specs=placed,
-        out_specs=(P("section", "et", None), P("section", "et", None), P("section", None, "et")),
+        out_specs=(P("section", et, None), P("section", et, None), P("section", None, et)),
         check_vma=False,
     )

time: 125 us -> 109 us (0.87)
  the two profiles are of different devices: /device:TPU:257 before, /device:TPU:198 now
where the time goes in v2:
time: 109 us; the launch traced here: 108 us
  waiting for transfers between devices  55.8 us (51%)
  starting transfers between devices  22.8 us (21%)
  other arithmetic  14.1 us (13%)
  local copies, waits for them, and re-layouts  7.14 us (7%)
  matrix products  7.09 us (7%)
    all_to_all x1, waiting for transfers between devices, shards(): lax.all_to_all(sent, 'ety', 0, 0, tiled=True).reshape(chips, own_rows, -1)  24.2 us
    all_to_all x1, waiting for transfers between devices, shards(): lax.all_to_all(tiled, 'ety', 0, 0, tiled=True)  21.7 us
    ppermute x2, waiting for transfers between devices, from_behind(): lax.ppermute(value, axis, [(source, source + steps) for source in range(f...  7.89 us
    ppermute x2, starting transfers between devices, from_behind(): lax.ppermute(value, axis, [(source, source + steps) for source in range(f...  7.33 us
    all_to_all x1, starting transfers between devices, shards(): lax.all_to_all(tiled, 'ety', 0, 0, tiled=True)  7.1 us
    all_to_all x1, starting transfers between devices, shards(): lax.all_to_all(sent, 'ety', 0, 0, tiled=True).reshape(chips, own_rows, -1)  4.23 us
    unnamed x25, local copies, waits for them, and re-layouts  3.67 us
    dot_general x1, matrix products, shards(): lax.dot_general(full_g, w_down, (((1,), (1,)), ((), ())), preferred_eleme...  3.25 us
  transfers between devices with their start and end apart: 6, of which 5 were waited for; matrix products, arithmetic and copies ran while one was open for 5% of the time, Pallas kernels for 0%

profile of v2, /device:TPU:198, one launch (start us, length us, event | category | flops | bytes accessed | tf_op | source)
XLA Modules:
  0.0 107.9 jit_solution(960737604878143567)
XLA Ops:
  0.7 0.9 dynamic-slice_reduce_fusion
  1.6 1.1 %fusion.27 = f32[16]{0:T(128)S(1)} fusion(bf16[1,16,3072]{2,1,0:T(8,128)(2,1)} %param.13), kind=kLoop, calls=%fused_computation.44 | loop fusion | flops 147440 | bytes 98368 | tf_op jit(solution)/shard_map/reduce_sum | solution.py:15
  2.7 0.7 mul.194
  3.5 1.1 %select_reduce_fusion.1 = (f32[16]{0:T(128)S(1)}, bf16[16,8]{0,1:T(8,128)(2,1)S(1)}) fusion(s32[16]{0:T(128)S(1)} %broadcast_minimum_fusion.1, bf16[1,3072,8]{1,2,0:T(8,128)(2,1)} %param.18, bf16[1,16,3072]{2,1,0:T(8,128)(2,1)} %param.13, f32[16]{0:T(128)S(1)} %add_rsqrt_fusion, f32[3072]{0:T(1024)S(1)} %bitcast.152), kind=kOutput, calls=%fused_computation.74 | convolution fusion | flops 983664 | bytes 160192 | tf_op jit(solution)/shard_map/dot_general | solution.py:17
  4.7 0.9 fusion.34
  5.6 1.0 broadcast_in_dim.10
  6.5 7.1 %all-to-all-start = ((bf16[8,16,3200]{2,1,0:T(8,128)(2,1)}), bf16[8,16,3200]{2,1,0:T(8,128)(2,1)}, u32[]{:S(2)}, u32[]{:S(2)}) async-start(bf16[8,16,3200]{2,1,0:T(8,128)(2,1)} %broadcast_in_dim.10), calls=%async_computation | async-start | bytes 1638400 | tf_op jit(solution)/shard_map/all_to_all | solution.py:50
  13.7 2.1 %convolution_convert_fusion = bf16[256,3072]{1,0:T(8,128)(2,1)} fusion(bf16[1,512,3072]{2,1,0:T(8,128)(2,1)S(1)} %copy-done, bf16[1,256,512]{2,1,0:T(8,128)(2,1)S(1)} %copy-done.6), kind=kOutput, calls=%fused_computation | convolution fusion | flops 806092800 | bytes 4980736 | tf_op jit(solution)/shard_map/dot_general | solution.py:69
  15.9 21.7 %all-to-all-done = bf16[8,16,3200]{2,1,0:T(8,128)(2,1)} async-done(((bf16[8,16,3200]{2,1,0:T(8,128)(2,1)}), bf16[8,16,3200]{2,1,0:T(8,128)(2,1)}, u32[]{:S(2)}, u32[]{:S(2)}) %all-to-all-start) | async-done | bytes 819232 | tf_op jit(solution)/shard_map/all_to_all | solution.py:50
  37.6 1.9 %collective-permute-start = (bf16[8,1,16,3200]{3,2,0,1:T(8,128)(2,1)}, bf16[8,1,16,3200]{3,2,0,1:T(8,128)(2,1)S(1)}, u32[]{:S(2)}, u32[]{:S(2)}) collective-permute-start(bf16[8,1,16,3200]{3,2,0,1:T(8,128)(2,1)} %bitcast.19), channel_id=1, source_target_pairs={{0,1},{1,0},{2,3},{3,2},{4,5},{5,4},{6,7},{7,6},{8,9},{9,8},{10,11... | collective-permute-start | bytes 2457608 | tf_op jit(solution)/shard_map/ppermute | solution.py:51
  39.5 2.3 %fusion.10 = bf16[8,16,3072]{2,1,0:T(8,128)(2,1)} fusion(pred[]{:T(512)S(6)} %eq.65, bf16[8,2,16,3072]{3,2,1,0:T(8,128)(2,1)} %bitcast.144), kind=kLoop, calls=%fused_computation.19 | loop fusion | flops 393216 | bytes 2359297 | tf_op jit(solution)/shard_map/jit(_where)/select_n | solution.py:73
  41.8 0.1 collective-permute-done
  42.0 1.7 %maximum_select_fusion = bf16[8,2,16,3200]{3,2,0,1:T(8,128)(2,1)S(1)} fusion(bf16[8,1,16,3200]{3,2,0,1:T(8,128)(2,1)S(1)} %collective-permute-done, bf16[8,1,16,3200]{3,2,0,1:T(8,128)(2,1)} %bitcast.19, pred[]{:T(512)S(6)} %eq.65), kind=kLoop, calls=%fused_computation.8 | loop fusion | flops 2457600 | bytes 3276801 | tf_op jit(solution)/shard_map/jit(_where)/select_n | solution.py:52
  43.8 1.2 %copy-done.1 = bf16[8,2,16,3200]{3,2,1,0:T(8,128)(2,1)} copy-done((bf16[8,2,16,3200]{3,2,1,0:T(8,128)(2,1)}, bf16[8,2,16,3200]{3,2,1,0:T(8,128)(2,1)S(1)}, u32[]{:S(2)}) %copy-start.1) | copy-done | bytes 1638424
  45.1 3.2 %fusion.13 = (bf16[1,256,512]{2,1,0:T(8,128)(2,1)}, f32[256]{0:T(256)S(1)}) fusion(f32[256]{0:T(256)S(1)} %bitcast.159, bf16[1,256,512]{2,1,0:T(8,128)(2,1)} %param.14, bf16[1,512,3072]{2,1,0:T(8,128)(2,1)S(1)} %copy-done, bf16[256,3200]{1,0:T(8,128)(2,1)} %bitcast.147), kind=kOutput, calls=%fused_computation.25 | convolution fusion | flops 805961472 | bytes 5244928 | tf_op jit(solution)/shard_map/dot_general | solution.py:61
  48.7 1.2 %fusion.9 = bf16[8,16,3200]{2,1,0:T(8,128)(2,1)S(1)} fusion(bf16[8,16,2]{2,1,0:T(8,128)(2,1)S(1)} %bitcast.149, bf16[8,16,3072]{2,1,0:T(8,128)(2,1)} %fusion.10), kind=kLoop, calls=%fused_computation.18 | loop fusion | flops 2457600 | bytes 1606144 | tf_op jit(solution)/shard_map/concatenate | solution.py:77
  49.9 2.3 %collective-permute-start.1 = (bf16[8,16,3200]{2,1,0:T(8,128)(2,1)S(1)}, bf16[8,16,3200]{2,1,0:T(8,128)(2,1)S(1)}, u32[]{:S(2)}, u32[]{:S(2)}) collective-permute-start(bf16[8,16,3200]{2,1,0:T(8,128)(2,1)S(1)} %fusion.9), channel_id=1, source_target_pairs={{0,1},{1,0},{2,3},{3,2},{4,5},{5,4},{6,7},{7,6},{8,9},{9,8},{10,11... | collective-permute-start | bytes 2457608 | tf_op jit(solution)/shard_map/ppermute | solution.py:76
  52.3 1.8 %collective-permute-done.1 = bf16[8,16,3200]{2,1,0:T(8,128)(2,1)S(1)} collective-permute-done((bf16[8,16,3200]{2,1,0:T(8,128)(2,1)S(1)}, bf16[8,16,3200]{2,1,0:T(8,128)(2,1)S(1)}, u32[]{:S(2)}, u32[]{:S(2)}) %collective-permute-start.1) | collective-permute-done | bytes 819232 | tf_op jit(solution)/shard_map/ppermute | solution.py:76
  54.1 0.9 copy-done.2
  55.4 2.9 %fusion.7 = bf16[8,16,3072]{2,1,0:T(8,128)(2,1)} fusion(bf16[8,16,3200]{2,1,0:T(8,128)(2,1)} %copy-done.2, pred[]{:T(512)S(6)} %eq.65, bf16[8,2,16,3072]{3,2,1,0:T(8,128)(2,1)} %bitcast.145), kind=kLoop, calls=%fused_computation.13 | loop fusion | flops 1966080 | bytes 3145729 | tf_op jit(solution)/shard_map/convert_element_type | solution.py:81
  58.3 2.0 %concatenate.22 = bf16[8,16,3200]{2,1,0:T(8,128)(2,1)} concatenate(bf16[8,16,3072]{2,1,0:T(8,128)(2,1)} %fusion.7, bf16[8,16,1]{2,1,0:T(8,128)(2,1)S(1)} %copy.47, bf16[8,16,1]{2,1,0:T(8,128)(2,1)S(1)} %copy.48, bf16[8,16,126]{2,1,0:T(8,128)(2,1)S(1)} %broadcast_in_dim.11), dimensions={2} | concatenate | bytes 1638400 | tf_op jit(solution)/shard_map/concatenate | solution.py:91
  60.3 4.2 %all-to-all-start.1 = ((bf16[8,16,3200]{2,1,0:T(8,128)(2,1)}), bf16[8,16,3200]{2,1,0:T(8,128)(2,1)}, u32[]{:S(2)}, u32[]{:S(2)}) async-start(bf16[8,16,3200]{2,1,0:T(8,128)(2,1)} %concatenate.22), calls=%async_computation.1 | async-start | bytes 1638400 | tf_op jit(solution)/shard_map/all_to_all | solution.py:92
  64.7 0.2 select_reduce_fusion.2
  65.0 24.2 %all-to-all-done.1 = bf16[8,16,3200]{2,1,0:T(8,128)(2,1)} async-done(((bf16[8,16,3200]{2,1,0:T(8,128)(2,1)}), bf16[8,16,3200]{2,1,0:T(8,128)(2,1)}, u32[]{:S(2)}, u32[]{:S(2)}) %all-to-all-start.1) | async-done | bytes 819232 | tf_op jit(solution)/shard_map/all_to_all | solution.py:92
  89.2 1.3 %convert_element_type.221 = f32[8,16,3200]{2,1,0:T(8,128)S(1)} convert(bf16[8,16,3200]{2,1,0:T(8,128)(2,1)} %all-to-all-done.1) | non-fusion elementwise | flops 409600 | bytes 2457600 | tf_op jit(solution)/shard_map/convert_element_type | solution.py:93
  90.6 0.2 fusion.43
  90.9 5.4 %collective-permute-start.2 = (bf16[16,3072]{1,0:T(8,128)(2,1)S(1)}, bf16[16,3072]{1,0:T(8,128)(2,1)S(1)}, u32[]{:S(2)}, u32[]{:S(2)}) collective-permute-start(bf16[16,3072]{1,0:T(8,128)(2,1)S(1)} %fusion.31), channel_id=1, source_target_pairs={{0,16},{16,32},{32,48},{48,64},{64,80},{80,96},{96,112},{112,128},... | collective-permute-start | bytes 294920 | tf_op jit(solution)/shard_map/ppermute | solution.py:10
  96.3 0.3 fusion.22
  96.8 1.9 %collective-permute-start.3 = (bf16[16,3072]{1,0:T(8,128)(2,1)S(1)}, bf16[16,3072]{1,0:T(8,128)(2,1)S(1)}, u32[]{:S(2)}, u32[]{:S(2)}) collective-permute-start(bf16[16,3072]{1,0:T(8,128)(2,1)S(1)} %fusion.26), channel_id=1, source_target_pairs={{16,0},{32,16},{48,32},{64,48},{80,64},{96,80},{112,96},{128,112},... | collective-permute-start | bytes 294920 | tf_op jit(solution)/shard_map/ppermute | solution.py:10
  98.8 7.9 %collective-permute-done.3 = bf16[16,3072]{1,0:T(8,128)(2,1)S(1)} collective-permute-done((bf16[16,3072]{1,0:T(8,128)(2,1)S(1)}, bf16[16,3072]{1,0:T(8,128)(2,1)S(1)}, u32[]{:S(2)}, u32[]{:S(2)}) %collective-permute-start.3) | collective-permute-done | bytes 98336 | tf_op jit(solution)/shard_map/ppermute | solution.py:10
  106.6 0.6 copy.58
  107.3 0.6 copy.59
  (54 shorter events, 1.7 us)
Async XLA Ops:
  0.6 13.1 %copy-start = (bf16[1,512,3072]{2,1,0:T(8,128)(2,1)S(1)}, bf16[1,512,3072]{2,1,0:T(8,128)(2,1)}, u32[]{:S(2)}) copy-start(bf16[1,512,3072]{2,1,0:T(8,128)(2,1)} %param.19) | copy-start | bytes 9437188
  0.6 13.0 %copy-start.7 = (s32[1,256,2]{1,2,0:T(2,128)S(1)}, s32[1,256,2]{1,2,0:T(2,128)}, u32[]{:S(2)}) copy-start(s32[1,256,2]{1,2,0:T(2,128)} %param.15) | copy-start | bytes 6148
  0.7 13.0 %copy-start.6 = (bf16[1,256,512]{2,1,0:T(8,128)(2,1)S(1)}, bf16[1,256,512]{2,1,0:T(8,128)(2,1)}, u32[]{:S(2)}) copy-start(bf16[1,256,512]{2,1,0:T(8,128)(2,1)} %param.11) | copy-start | bytes 786436
  6.5 31.0 %all-to-all-start = ((bf16[8,16,3200]{2,1,0:T(8,128)(2,1)}), bf16[8,16,3200]{2,1,0:T(8,128)(2,1)}, u32[]{:S(2)}, u32[]{:S(2)}) async-start(bf16[8,16,3200]{2,1,0:T(8,128)(2,1)} %broadcast_in_dim.10), calls=%async_computation | async-start | bytes 1638400 | tf_op jit(solution)/shard_map/all_to_all | solution.py:50
  37.6 4.4 %collective-permute-start = (bf16[8,1,16,3200]{3,2,0,1:T(8,128)(2,1)}, bf16[8,1,16,3200]{3,2,0,1:T(8,128)(2,1)S(1)}, u32[]{:S(2)}, u32[]{:S(2)}) collective-permute-start(bf16[8,1,16,3200]{3,2,0,1:T(8,128)(2,1)} %bitcast.19), channel_id=1, source_target_pairs={{0,1},{1,0},{2,3},{3,2},{4,5},{5,4},{6,7},{7,6},{8,9},{9,8},{10,11... | collective-permute-start | bytes 2457608 | tf_op jit(solution)/shard_map/ppermute | solution.py:51
  43.8 1.2 %copy-start.1 = (bf16[8,2,16,3200]{3,2,1,0:T(8,128)(2,1)}, bf16[8,2,16,3200]{3,2,1,0:T(8,128)(2,1)S(1)}, u32[]{:S(2)}) copy-start(bf16[8,2,16,3200]{3,2,1,0:T(8,128)(2,1)S(1)} %copy.45) | copy-start | bytes 4915204
  48.4 3.8 %copy-start.9 = (s32[1,256,2]{1,2,0:T(2,128)S(1)}, s32[1,256,2]{1,2,0:T(2,128)}, u32[]{:S(2)}) copy-start(s32[1,256,2]{1,2,0:T(2,128)} %param.12) | copy-start | bytes 6148
  49.9 4.2 %collective-permute-start.1 = (bf16[8,16,3200]{2,1,0:T(8,128)(2,1)S(1)}, bf16[8,16,3200]{2,1,0:T(8,128)(2,1)S(1)}, u32[]{:S(2)}, u32[]{:S(2)}) collective-permute-start(bf16[8,16,3200]{2,1,0:T(8,128)(2,1)S(1)} %fusion.9), channel_id=1, source_target_pairs={{0,1},{1,0},{2,3},{3,2},{4,5},{5,4},{6,7},{7,6},{8,9},{9,8},{10,11... | collective-permute-start | bytes 2457608 | tf_op jit(solution)/shard_map/ppermute | solution.py:76
  54.1 0.9 copy-start.2
  58.3 6.3 %copy-start.3 = (bf16[1,16,3072]{2,1,0:T(8,128)(2,1)S(1)}, bf16[1,16,3072]{2,1,0:T(8,128)(2,1)}, u32[]{:S(2)}) copy-start(bf16[1,16,3072]{2,1,0:T(8,128)(2,1)} %param.10) | copy-start | bytes 294916
  58.3 6.4 %copy-start.8 = (bf16[1,3072,8]{1,2,0:T(8,128)(2,1)S(1)}, bf16[1,3072,8]{1,2,0:T(8,128)(2,1)}, u32[]{:S(2)}) copy-start(bf16[1,3072,8]{1,2,0:T(8,128)(2,1)} %param.18) | copy-start | bytes 147460
  60.3 28.9 %all-to-all-start.1 = ((bf16[8,16,3200]{2,1,0:T(8,128)(2,1)}), bf16[8,16,3200]{2,1,0:T(8,128)(2,1)}, u32[]{:S(2)}, u32[]{:S(2)}) async-start(bf16[8,16,3200]{2,1,0:T(8,128)(2,1)} %concatenate.22), calls=%async_computation.1 | async-start | bytes 1638400 | tf_op jit(solution)/shard_map/all_to_all | solution.py:92
  90.5 5.8 %copy-start.4 = (bf16[1,16,3072]{2,1,0:T(8,128)(2,1)S(1)}, bf16[1,16,3072]{2,1,0:T(8,128)(2,1)}, u32[]{:S(2)}) copy-start(bf16[1,16,3072]{2,1,0:T(8,128)(2,1)} %param.13) | copy-start | bytes 294916
  90.5 6.2 %copy-start.5 = (bf16[1,16,3072]{2,1,0:T(8,128)(2,1)S(1)}, bf16[1,16,3072]{2,1,0:T(8,128)(2,1)}, u32[]{:S(2)}) copy-start(bf16[1,16,3072]{2,1,0:T(8,128)(2,1)} %param.16) | copy-start | bytes 294916
  90.9 7.9 %collective-permute-start.2 = (bf16[16,3072]{1,0:T(8,128)(2,1)S(1)}, bf16[16,3072]{1,0:T(8,128)(2,1)S(1)}, u32[]{:S(2)}, u32[]{:S(2)}) collective-permute-start(bf16[16,3072]{1,0:T(8,128)(2,1)S(1)} %fusion.31), channel_id=1, source_target_pairs={{0,16},{16,32},{32,48},{48,64},{64,80},{80,96},{96,112},{112,128},... | collective-permute-start | bytes 294920 | tf_op jit(solution)/shard_map/ppermute | solution.py:10
  96.8 9.8 %collective-permute-start.3 = (bf16[16,3072]{1,0:T(8,128)(2,1)S(1)}, bf16[16,3072]{1,0:T(8,128)(2,1)S(1)}, u32[]{:S(2)}, u32[]{:S(2)}) collective-permute-start(bf16[16,3072]{1,0:T(8,128)(2,1)S(1)} %fusion.26), channel_id=1, source_target_pairs={{16,0},{32,16},{48,32},{64,48},{80,64},{96,80},{112,96},{128,112},... | collective-permute-start | bytes 294920 | tf_op jit(solution)/shard_map/ppermute | solution.py:10

commit v3 on v2

--- a/solution.py
+++ b/solution.py
@@ -63,36 +63,17 @@
     )
     dact = (coef_b[:, None] * back_up).astype(jnp.bfloat16)
     dprob_part = jnp.sum(act_bwd.astype(jnp.float32) * back_up, axis=1)
-    dprob_hi = dprob_part.astype(jnp.bfloat16)
-    dprob_lo = (dprob_part - dprob_hi.astype(jnp.float32)).astype(jnp.bfloat16)
+    dprob_got = lax.all_to_all(dprob_part.reshape(groups, own_rows), ("ety", "etc"), 0, 0, tiled=True)
+    dprob_mine = jnp.sum(dprob_got, axis=0)
 
     z_fwd = jnp.dot(act_fwd, w_down, preferred_element_type=jnp.float32).astype(jnp.bfloat16)
     z_fwd = z_fwd.reshape(chips, 2, own_rows, width)
-    d_split = jnp.stack([dprob_hi, dprob_lo], axis=-1).reshape(chips, 2, own_rows, 2)
     mine_z = jnp.where(core == 0, z_fwd[:, 0], z_fwd[:, 1])
     give_z = jnp.where(core == 0, z_fwd[:, 1], z_fwd[:, 0])
-    mine_d = jnp.where(core == 0, d_split[:, 0], d_split[:, 1])
-    give_d = jnp.where(core == 0, d_split[:, 1], d_split[:, 0])
-    given = lax.ppermute(
-        jnp.concatenate([give_z, jnp.pad(give_d, ((0, 0), (0, 0), (0, pad - 2)))], axis=-1),
-        "etc",
-        [(0, 1), (1, 0)],
-    )
-    pair_z = (mine_z.astype(jnp.float32) + given[..., :width].astype(jnp.float32)).astype(jnp.bfloat16)
-    pair_d = jnp.sum(mine_d.astype(jnp.float32), axis=-1) + jnp.sum(
-        given[..., width : width + 2].astype(jnp.float32), axis=-1
-    )
-    pair_hi = pair_d.astype(jnp.bfloat16)
-    pair_lo = (pair_d - pair_hi.astype(jnp.float32)).astype(jnp.bfloat16)
-    extra = jnp.concatenate(
-        [pair_hi[..., None], pair_lo[..., None], jnp.zeros((chips, own_rows, pad - 2), jnp.bfloat16)],
-        axis=-1,
-    )
-    sent = jnp.concatenate([pair_z, extra], axis=-1).reshape(chips * own_rows, -1)
-    got = lax.all_to_all(sent, "ety", 0, 0, tiled=True).reshape(chips, own_rows, -1)
-    got = got.astype(jnp.float32)
-    z_sum = jnp.sum(got[:, :, :width], axis=0)
-    dprob_mine = jnp.sum(got[:, :, width] + got[:, :, width + 1], axis=0)
+    given = lax.ppermute(give_z, "etc", [(0, 1), (1, 0)])
+    pair_z = (mine_z.astype(jnp.float32) + given.astype(jnp.float32)).astype(jnp.bfloat16)
+    got = lax.all_to_all(pair_z.reshape(chips * own_rows, width), "ety", 0, 0, tiled=True)
+    z_sum = jnp.sum(got.reshape(chips, own_rows, width).astype(jnp.float32), axis=0)
 
     ids_f_own = lax.dynamic_slice_in_dim(ids_fwd, first_row, own_rows, 0)
     _, _, _, coef_f = routing(logit_f, ids_f_own, experts)

time: 109 us -> 106 us (0.972)
  waiting for transfers between devices: 55.8 us -> 49.6 us
  starting transfers between devices: 22.8 us -> 26.9 us
  other arithmetic: 14.1 us -> 12.1 us
  local copies, waits for them, and re-layouts: 7.14 us -> 8.85 us
    all_to_all x1 -> x2, starting transfers between devices: 4.23 us -> 7.7 us  [the longest x1 4.21 us: shards(): lax.all_to_all(pair_z.reshape(chips * own_rows, width), 'ety', 0, 0, tile...]
    all_to_all x1 -> x2, waiting for transfers between devices: 24.2 us -> 20.9 us  [the longest x1 19.5 us: shards(): lax.all_to_all(pair_z.reshape(chips * own_rows, width), 'ety', 0, 0, tile...]
    unnamed x25 -> x32, local copies, waits for them, and re-layouts: 3.67 us -> 6.45 us
    concatenate x1 -> x0, local copies, waits for them, and re-layouts: 2.02 us -> none  [shards(): jnp.concatenate([pair_z, extra], axis=-1).reshape(chips * own_rows, -1)]
    ppermute x1, waiting for transfers between devices: 1.83 us -> 0.01 us  [shards(): given = lax.ppermute(give_z, 'etc', [(0, 1), (1, 0)])]
    select_n x1, other arithmetic: 2.34 us -> 0.97 us  [shards(): give_z = jnp.where(core == 0, z_fwd[:, 1], z_fwd[:, 0])]
    convert_element_type x5 -> x1, other arithmetic: 4.15 us -> 2.88 us  [shards(): (mine_z.astype(jnp.float32) + given.astype(jnp.float32)).astype(jnp.bfloa...]
    concatenate x1 -> x0, other arithmetic: 1.19 us -> none  [shards(): jnp.concatenate([give_z, jnp.pad(give_d, ((0, 0), (0, 0), (0, pad - 2)))]...]
  transfers between devices with their start and end apart: 6 -> 7, of which waited for: 5 -> 4; matrix products, arithmetic and copies ran while one was open for 5% -> 11% of each run, Pallas kernels for 0% -> 0%
where the time goes in v3:
time: 106 us
  waiting for transfers between devices  49.6 us (47%)
  starting transfers between devices  26.9 us (25%)
  other arithmetic  12.1 us (11%)
  local copies, waits for them, and re-layouts  8.85 us (8%)
  matrix products  7.32 us (7%)
    all_to_all x1, waiting for transfers between devices, shards(): lax.all_to_all(tiled, 'ety', 0, 0, tiled=True)  21.6 us
    all_to_all x1, waiting for transfers between devices, shards(): lax.all_to_all(pair_z.reshape(chips * own_rows, width), 'ety', 0, 0, tile...  19.5 us
    ppermute x2, starting transfers between devices, from_behind(): lax.ppermute(value, axis, [(source, source + steps) for source in range(f...  8.11 us
    all_to_all x1, starting transfers between devices, shards(): lax.all_to_all(tiled, 'ety', 0, 0, tiled=True)  7.1 us
    ppermute x2, waiting for transfers between devices, from_behind(): lax.ppermute(value, axis, [(source, source + steps) for source in range(f...  7.09 us
    unnamed x32, local copies, waits for them, and re-layouts  6.45 us
    all_to_all x1, starting transfers between devices, shards(): lax.all_to_all(pair_z.reshape(chips * own_rows, width), 'ety', 0, 0, tile...  4.21 us
    all_to_all x1, starting transfers between devices, shards(): lax.all_to_all(dprob_part.reshape(groups, own_rows), ('ety', 'etc'), 0, 0...  3.49 us
  transfers between devices with their start and end apart: 7, of which 4 were waited for; matrix products, arithmetic and copies ran while one was open for 11% of the time, Pallas kernels for 0%

profile of v3, /device:TPU:198, one launch (start us, length us, event | category | flops | bytes accessed | tf_op | source)
XLA Modules:
  0.0 105.8 jit_solution(15313223877343141052)
XLA Ops:
  0.7 1.9 %copy-done = bf16[1,512,3072]{2,1,0:T(8,128)(2,1)S(1)} copy-done((bf16[1,512,3072]{2,1,0:T(8,128)(2,1)S(1)}, bf16[1,512,3072]{2,1,0:T(8,128)(2,1)}, u32[]{:S(2)}) %copy-start) | copy-done | bytes 3145752
  2.5 1.9 %convolution_convert_fusion = bf16[256,3072]{1,0:T(8,128)(2,1)S(1)} fusion(bf16[1,512,3072]{2,1,0:T(8,128)(2,1)S(1)} %copy-done, bf16[1,256,512]{2,1,0:T(8,128)(2,1)} %param.11), kind=kOutput, calls=%fused_computation | convolution fusion | flops 806092800 | bytes 4980736 | tf_op jit(solution)/shard_map/dot_general | solution.py:69
  4.5 1.1 %copy-done.1 = bf16[256,3072]{1,0:T(8,128)(2,1)} copy-done((bf16[256,3072]{1,0:T(8,128)(2,1)}, bf16[256,3072]{1,0:T(8,128)(2,1)S(1)}, u32[]{:S(2)}) %copy-start.1) | copy-done | bytes 1572888
  5.6 1.0 fusion.8
  6.6 2.0 %collective-permute-start = (bf16[8,16,3072]{2,1,0:T(8,128)(2,1)}, bf16[8,16,3072]{2,1,0:T(8,128)(2,1)}, u32[]{:S(2)}, u32[]{:S(2)}) collective-permute-start(bf16[8,16,3072]{2,1,0:T(8,128)(2,1)} %fusion.8), channel_id=1, source_target_pairs={{0,1},{1,0},{2,3},{3,2},{4,5},{5,4},{6,7},{7,6},{8,9},{9,8},{10,11... | collective-permute-start | bytes 2359304 | tf_op jit(solution)/shard_map/ppermute | solution.py:73
  9.0 0.8 select_reduce_fusion.1
  9.9 1.0 broadcast_in_dim.9
  10.8 7.1 %all-to-all-start.1 = ((bf16[8,16,3200]{2,1,0:T(8,128)(2,1)}), bf16[8,16,3200]{2,1,0:T(8,128)(2,1)}, u32[]{:S(2)}, u32[]{:S(2)}) async-start(bf16[8,16,3200]{2,1,0:T(8,128)(2,1)} %broadcast_in_dim.9), calls=%async_computation.1 | async-start | bytes 1638400 | tf_op jit(solution)/shard_map/all_to_all | solution.py:50
  18.1 2.9 %fusion.6 = bf16[8,16,3072]{2,1,0:T(8,128)(2,1)} fusion(bf16[8,16,3072]{2,1,0:T(8,128)(2,1)} %collective-permute-done, pred[]{:T(512)S(6)} %eq.63, bf16[8,2,16,3072]{3,2,1,0:T(8,128)(2,1)} %bitcast.137), kind=kLoop, calls=%fused_computation.10 | loop fusion | flops 1966080 | bytes 3145729 | tf_op jit(solution)/shard_map/convert_element_type | solution.py:74
  21.0 21.6 %all-to-all-done.1 = bf16[8,16,3200]{2,1,0:T(8,128)(2,1)} async-done(((bf16[8,16,3200]{2,1,0:T(8,128)(2,1)}), bf16[8,16,3200]{2,1,0:T(8,128)(2,1)}, u32[]{:S(2)}, u32[]{:S(2)}) %all-to-all-start.1) | async-done | bytes 819232 | tf_op jit(solution)/shard_map/all_to_all | solution.py:50
  42.6 4.2 %all-to-all-start = ((bf16[8,16,3072]{2,1,0:T(8,128)(2,1)}), bf16[8,16,3072]{2,1,0:T(8,128)(2,1)}, u32[]{:S(2)}, u32[]{:S(2)}) async-start(bf16[8,16,3072]{2,1,0:T(8,128)(2,1)} %fusion.6), calls=%async_computation | async-start | bytes 1572864 | tf_op jit(solution)/shard_map/all_to_all | solution.py:75
  48.3 1.9 %collective-permute-start.2 = (bf16[8,1,16,3200]{3,2,0,1:T(8,128)(2,1)}, bf16[8,1,16,3200]{3,2,0,1:T(8,128)(2,1)}, u32[]{:S(2)}, u32[]{:S(2)}) collective-permute-start(bf16[8,1,16,3200]{3,2,0,1:T(8,128)(2,1)} %bitcast.20), channel_id=1, source_target_pairs={{0,1},{1,0},{2,3},{3,2},{4,5},{5,4},{6,7},{7,6},{8,9},{9,8},{10,11... | collective-permute-start | bytes 2457608 | tf_op jit(solution)/shard_map/ppermute | solution.py:51
  50.2 0.6 slice_convert_fusion
  50.8 19.5 %all-to-all-done = bf16[8,16,3072]{2,1,0:T(8,128)(2,1)} async-done(((bf16[8,16,3072]{2,1,0:T(8,128)(2,1)}), bf16[8,16,3072]{2,1,0:T(8,128)(2,1)}, u32[]{:S(2)}, u32[]{:S(2)}) %all-to-all-start) | async-done | bytes 786464 | tf_op jit(solution)/shard_map/all_to_all | solution.py:75
  70.4 1.3 %convert_reduce_fusion = f32[16,3072]{1,0:T(8,128)S(1)} fusion(bf16[8,16,3072]{2,1,0:T(8,128)(2,1)} %all-to-all-done), kind=kLoop, calls=%fused_computation.11 | loop fusion | flops 737280 | bytes 983040 | tf_op jit(solution)/shard_map/reduce_sum | solution.py:76
  71.6 2.3 %maximum_select_fusion = bf16[8,2,16,3200]{3,2,0,1:T(8,128)(2,1)S(1)} fusion(bf16[8,1,16,3200]{3,2,0,1:T(8,128)(2,1)} %collective-permute-done.2, bf16[8,1,16,3200]{3,2,0,1:T(8,128)(2,1)} %bitcast.20, pred[]{:T(512)S(6)} %eq.63), kind=kLoop, calls=%fused_computation.7 | loop fusion | flops 2457600 | bytes 3276801 | tf_op jit(solution)/shard_map/jit(_where)/select_n | solution.py:52
  74.1 1.2 %copy-done.2 = bf16[8,2,16,3200]{3,2,1,0:T(8,128)(2,1)} copy-done((bf16[8,2,16,3200]{3,2,1,0:T(8,128)(2,1)}, bf16[8,2,16,3200]{3,2,1,0:T(8,128)(2,1)S(1)}, u32[]{:S(2)}) %copy-start.2) | copy-done | bytes 1638424
  75.2 0.6 slice.39
  75.9 0.9 copy.58
  76.8 3.2 %fusion.11 = (bf16[1,256,512]{2,1,0:T(8,128)(2,1)}, f32[256]{0:T(256)S(1)}) fusion(f32[256]{0:T(256)S(1)} %bitcast.151, bf16[1,256,512]{2,1,0:T(8,128)(2,1)} %param.14, bf16[1,512,3072]{2,1,0:T(8,128)(2,1)S(1)} %copy-done, bf16[256,3200]{1,0:T(8,128)(2,1)} %bitcast.139), kind=kOutput, calls=%fused_computation.22 | convolution fusion | flops 805961472 | bytes 5244928 | tf_op jit(solution)/shard_map/dot_general | solution.py:61
  80.1 0.7 all_to_all.16
  80.8 3.5 %all-to-all-start.2 = ((f32[16,1,16]{2,1,0:T(1,128)}), f32[16,1,16]{2,1,0:T(1,128)S(1)}, u32[]{:S(2)}, u32[]{:S(2)}) async-start(f32[16,1,16]{2,1,0:T(1,128)} %all_to_all.16), calls=%async_computation.2 | async-start | bytes 16384 | tf_op jit(solution)/shard_map/all_to_all | solution.py:66
  84.3 0.7 fusion.26
  85.0 5.4 %collective-permute-start.1 = (bf16[16,3072]{1,0:T(8,128)(2,1)}, bf16[16,3072]{1,0:T(8,128)(2,1)S(1)}, u32[]{:S(2)}, u32[]{:S(2)}) collective-permute-start(bf16[16,3072]{1,0:T(8,128)(2,1)} %fusion.26), channel_id=1, source_target_pairs={{0,16},{16,32},{32,48},{48,64},{64,80},{80,96},{96,112},{112,128},... | collective-permute-start | bytes 294920 | tf_op jit(solution)/shard_map/ppermute | solution.py:10
  90.4 1.4 %all-to-all-done.2 = f32[16,1,16]{2,1,0:T(1,128)S(1)} async-done(((f32[16,1,16]{2,1,0:T(1,128)}), f32[16,1,16]{2,1,0:T(1,128)S(1)}, u32[]{:S(2)}, u32[]{:S(2)}) %all-to-all-start.2) | async-done | bytes 1056 | tf_op jit(solution)/shard_map/all_to_all | solution.py:66
  91.8 0.6 fusion.49
  92.5 1.2 %fusion.20 = (f32[16]{0:T(128)S(1)}, f32[16,3072]{1,0:T(8,128)S(1)}) fusion(bf16[1,16,3072]{2,1,0:T(8,128)(2,1)S(1)} %copy-done.4, f32[16]{0:T(128)} %copy-done.12, f32[3072]{0:T(1024)} %bitcast.146, bf16[1,3072,8]{1,2,0:T(8,128)(2,1)} %param.18, s32[16]{0:T(128)} %copy-done.13, f32[3072]{0:T(1024)} %bitcast.147, f32[16]{0:T(128)S(1)} %fusion.49), kind=kOutput, calls=%fused_computation.36 | convolution fusion | flops 1130608 | bytes 368896 | tf_op jit(solution)/shard_map/dot_general | solution.py:86
  93.6 1.0 fusion.24
  94.6 2.7 %collective-permute-start.3 = (bf16[16,3072]{1,0:T(8,128)(2,1)S(1)}, bf16[16,3072]{1,0:T(8,128)(2,1)S(1)}, u32[]{:S(2)}, u32[]{:S(2)}) collective-permute-start(bf16[16,3072]{1,0:T(8,128)(2,1)S(1)} %fusion.24), channel_id=1, source_target_pairs={{16,0},{32,16},{48,32},{64,48},{80,64},{96,80},{112,96},{128,112},... | collective-permute-start | bytes 294920 | tf_op jit(solution)/shard_map/ppermute | solution.py:10
  97.4 7.1 %collective-permute-done.3 = bf16[16,3072]{1,0:T(8,128)(2,1)S(1)} collective-permute-done((bf16[16,3072]{1,0:T(8,128)(2,1)S(1)}, bf16[16,3072]{1,0:T(8,128)(2,1)S(1)}, u32[]{:S(2)}, u32[]{:S(2)}) %collective-permute-start.3) | collective-permute-done | bytes 98336 | tf_op jit(solution)/shard_map/ppermute | solution.py:10
  104.5 0.6 copy.62
  105.1 0.6 copy.63
  (52 shorter events, 2.2 us)
Async XLA Ops:
  0.6 1.9 %copy-start = (bf16[1,512,3072]{2,1,0:T(8,128)(2,1)S(1)}, bf16[1,512,3072]{2,1,0:T(8,128)(2,1)}, u32[]{:S(2)}) copy-start(bf16[1,512,3072]{2,1,0:T(8,128)(2,1)} %param.19) | copy-start | bytes 9437188
  4.5 1.2 %copy-start.1 = (bf16[256,3072]{1,0:T(8,128)(2,1)}, bf16[256,3072]{1,0:T(8,128)(2,1)S(1)}, u32[]{:S(2)}) copy-start(bf16[256,3072]{1,0:T(8,128)(2,1)S(1)} %convolution_convert_fusion) | copy-start | bytes 4718596
  4.5 4.2 %copy-start.7 = (bf16[1,3072]{1,0:T(2,128)(2,1)S(1)}, bf16[1,3072]{1,0:T(2,128)(2,1)}, u32[]{:S(2)}) copy-start(bf16[1,3072]{1,0:T(2,128)(2,1)} %param.17) | copy-start | bytes 18436
  4.5 4.2 %copy-start.4 = (bf16[1,16,3072]{2,1,0:T(8,128)(2,1)S(1)}, bf16[1,16,3072]{2,1,0:T(8,128)(2,1)}, u32[]{:S(2)}) copy-start(bf16[1,16,3072]{2,1,0:T(8,128)(2,1)} %param.13) | copy-start | bytes 294916
  4.5 4.4 %copy-start.6 = (s32[1,256,2]{1,2,0:T(2,128)S(1)}, s32[1,256,2]{1,2,0:T(2,128)}, u32[]{:S(2)}) copy-start(s32[1,256,2]{1,2,0:T(2,128)} %param.15) | copy-start | bytes 6148
  4.5 4.4 %copy-start.11 = (s32[1,256,2]{1,2,0:T(2,128)S(1)}, s32[1,256,2]{1,2,0:T(2,128)}, u32[]{:S(2)}) copy-start(s32[1,256,2]{1,2,0:T(2,128)} %param.12) | copy-start | bytes 6148
  4.5 4.5 %copy-start.9 = (bf16[1,3072,8]{1,2,0:T(8,128)(2,1)S(1)}, bf16[1,3072,8]{1,2,0:T(8,128)(2,1)}, u32[]{:S(2)}) copy-start(bf16[1,3072,8]{1,2,0:T(8,128)(2,1)} %param.18) | copy-start | bytes 147460
  4.5 5.3 %copy-start.5 = (bf16[1,16,3072]{2,1,0:T(8,128)(2,1)S(1)}, bf16[1,16,3072]{2,1,0:T(8,128)(2,1)}, u32[]{:S(2)}) copy-start(bf16[1,16,3072]{2,1,0:T(8,128)(2,1)} %param.16) | copy-start | bytes 294916
  6.6 11.3 %copy-start.3 = (bf16[1,16,3072]{2,1,0:T(8,128)(2,1)S(1)}, bf16[1,16,3072]{2,1,0:T(8,128)(2,1)}, u32[]{:S(2)}) copy-start(bf16[1,16,3072]{2,1,0:T(8,128)(2,1)} %param.10) | copy-start | bytes 294916
  6.6 11.5 %collective-permute-start = (bf16[8,16,3072]{2,1,0:T(8,128)(2,1)}, bf16[8,16,3072]{2,1,0:T(8,128)(2,1)}, u32[]{:S(2)}, u32[]{:S(2)}) collective-permute-start(bf16[8,16,3072]{2,1,0:T(8,128)(2,1)} %fusion.8), channel_id=1, source_target_pairs={{0,1},{1,0},{2,3},{3,2},{4,5},{5,4},{6,7},{7,6},{8,9},{9,8},{10,11... | collective-permute-start | bytes 2359304 | tf_op jit(solution)/shard_map/ppermute | solution.py:73
  8.7 38.8 %copy-start.8 = (f32[1,3072]{1,0:T(1,128)}, f32[1,3072]{1,0:T(1,128)S(1)}, u32[]{:S(2)}) copy-start(f32[1,3072]{1,0:T(1,128)S(1)} %mul.194) | copy-start | bytes 36868
  8.9 12.1 %copy-start.12 = (f32[16]{0:T(128)}, f32[16]{0:T(128)S(1)}, u32[]{:S(2)}) copy-start(f32[16]{0:T(128)S(1)} %add_rsqrt_fusion) | copy-start | bytes 196
  9.0 12.0 %copy-start.13 = (s32[16]{0:T(128)}, s32[16]{0:T(128)S(1)}, u32[]{:S(2)}) copy-start(s32[16]{0:T(128)S(1)} %broadcast_minimum_fusion.1) | copy-start | bytes 196
  10.8 31.7 %all-to-all-start.1 = ((bf16[8,16,3200]{2,1,0:T(8,128)(2,1)}), bf16[8,16,3200]{2,1,0:T(8,128)(2,1)}, u32[]{:S(2)}, u32[]{:S(2)}) async-start(bf16[8,16,3200]{2,1,0:T(8,128)(2,1)} %broadcast_in_dim.9), calls=%async_computation.1 | async-start | bytes 1638400 | tf_op jit(solution)/shard_map/all_to_all | solution.py:50
  42.6 27.8 %all-to-all-start = ((bf16[8,16,3072]{2,1,0:T(8,128)(2,1)}), bf16[8,16,3072]{2,1,0:T(8,128)(2,1)}, u32[]{:S(2)}, u32[]{:S(2)}) async-start(bf16[8,16,3072]{2,1,0:T(8,128)(2,1)} %fusion.6), calls=%async_computation | async-start | bytes 1572864 | tf_op jit(solution)/shard_map/all_to_all | solution.py:75
  48.3 23.4 %collective-permute-start.2 = (bf16[8,1,16,3200]{3,2,0,1:T(8,128)(2,1)}, bf16[8,1,16,3200]{3,2,0,1:T(8,128)(2,1)}, u32[]{:S(2)}, u32[]{:S(2)}) collective-permute-start(bf16[8,1,16,3200]{3,2,0,1:T(8,128)(2,1)} %bitcast.20), channel_id=1, source_target_pairs={{0,1},{1,0},{2,3},{3,2},{4,5},{5,4},{6,7},{7,6},{8,9},{9,8},{10,11... | collective-permute-start | bytes 2457608 | tf_op jit(solution)/shard_map/ppermute | solution.py:51
  74.1 1.2 %copy-start.2 = (bf16[8,2,16,3200]{3,2,1,0:T(8,128)(2,1)}, bf16[8,2,16,3200]{3,2,1,0:T(8,128)(2,1)S(1)}, u32[]{:S(2)}) copy-start(bf16[8,2,16,3200]{3,2,1,0:T(8,128)(2,1)S(1)} %copy.54) | copy-start | bytes 4915204
  76.8 7.5 %copy-start.10 = (f32[16]{0:T(128)S(1)}, f32[16]{0:T(128)}, u32[]{:S(2)}) copy-start(f32[16]{0:T(128)} %fusion.52) | copy-start | bytes 196
  80.8 11.0 %all-to-all-start.2 = ((f32[16,1,16]{2,1,0:T(1,128)}), f32[16,1,16]{2,1,0:T(1,128)S(1)}, u32[]{:S(2)}, u32[]{:S(2)}) async-start(f32[16,1,16]{2,1,0:T(1,128)} %all_to_all.16), calls=%async_computation.2 | async-start | bytes 16384 | tf_op jit(solution)/shard_map/all_to_all | solution.py:66
  85.0 12.4 %collective-permute-start.1 = (bf16[16,3072]{1,0:T(8,128)(2,1)}, bf16[16,3072]{1,0:T(8,128)(2,1)S(1)}, u32[]{:S(2)}, u32[]{:S(2)}) collective-permute-start(bf16[16,3072]{1,0:T(8,128)(2,1)} %fusion.26), channel_id=1, source_target_pairs={{0,16},{16,32},{32,48},{48,64},{64,80},{80,96},{96,112},{112,128},... | collective-permute-start | bytes 294920 | tf_op jit(solution)/shard_map/ppermute | solution.py:10
  94.6 9.8 %collective-permute-start.3 = (bf16[16,3072]{1,0:T(8,128)(2,1)S(1)}, bf16[16,3072]{1,0:T(8,128)(2,1)S(1)}, u32[]{:S(2)}, u32[]{:S(2)}) collective-permute-start(bf16[16,3072]{1,0:T(8,128)(2,1)S(1)} %fusion.24), channel_id=1, source_target_pairs={{16,0},{32,16},{48,32},{64,48},{80,64},{96,80},{112,96},{128,112},... | collective-permute-start | bytes 294920 | tf_op jit(solution)/shard_map/ppermute | solution.py:10

commit v4 on v3

--- a/solution.py
+++ b/solution.py
@@ -48,6 +48,16 @@
     core = lax.axis_index("etc")
     tiled = jnp.broadcast_to(packed[None], (chips,) + packed.shape).reshape(chips * own_rows, -1)
     same_core = lax.all_to_all(tiled, "ety", 0, 0, tiled=True).reshape(chips, 1, own_rows, -1)
+    z_fwd = jnp.dot(act_fwd, w_down, preferred_element_type=jnp.float32).astype(jnp.bfloat16)
+    z_fwd = z_fwd.reshape(chips, 2, own_rows, width)
+    mine_z = jnp.where(core == 0, z_fwd[:, 0], z_fwd[:, 1])
+    give_z = jnp.where(core == 0, z_fwd[:, 1], z_fwd[:, 0])
+    given = lax.ppermute(give_z, "etc", [(0, 1), (1, 0)])
+    pair_z = (mine_z.astype(jnp.float32) + given.astype(jnp.float32)).astype(jnp.bfloat16)
+    pair_z, same_core = lax.optimization_barrier((pair_z, same_core))
+    got = lax.all_to_all(pair_z.reshape(chips * own_rows, width), "ety", 0, 0, tiled=True)
+    z_sum = jnp.sum(got.reshape(chips, own_rows, width).astype(jnp.float32), axis=0)
+
     other_core = lax.ppermute(same_core, "etc", [(0, 1), (1, 0)])
     full = jnp.where(
         core == 0,
@@ -63,17 +73,9 @@
     )
     dact = (coef_b[:, None] * back_up).astype(jnp.bfloat16)
     dprob_part = jnp.sum(act_bwd.astype(jnp.float32) * back_up, axis=1)
+    dprob_part, z_sum = lax.optimization_barrier((dprob_part, z_sum))
     dprob_got = lax.all_to_all(dprob_part.reshape(groups, own_rows), ("ety", "etc"), 0, 0, tiled=True)
     dprob_mine = jnp.sum(dprob_got, axis=0)
-
-    z_fwd = jnp.dot(act_fwd, w_down, preferred_element_type=jnp.float32).astype(jnp.bfloat16)
-    z_fwd = z_fwd.reshape(chips, 2, own_rows, width)
-    mine_z = jnp.where(core == 0, z_fwd[:, 0], z_fwd[:, 1])
-    give_z = jnp.where(core == 0, z_fwd[:, 1], z_fwd[:, 0])
-    given = lax.ppermute(give_z, "etc", [(0, 1), (1, 0)])
-    pair_z = (mine_z.astype(jnp.float32) + given.astype(jnp.float32)).astype(jnp.bfloat16)
-    got = lax.all_to_all(pair_z.reshape(chips * own_rows, width), "ety", 0, 0, tiled=True)
-    z_sum = jnp.sum(got.reshape(chips, own_rows, width).astype(jnp.float32), axis=0)
 
     ids_f_own = lax.dynamic_slice_in_dim(ids_fwd, first_row, own_rows, 0)
     _, _, _, coef_f = routing(logit_f, ids_f_own, experts)

time: 106 us -> 96.5 us (0.910)
  waiting for transfers between devices: 49.6 us -> 40.3 us
  local copies, waits for them, and re-layouts: 8.85 us -> 5.53 us
  other arithmetic: 12.1 us -> 14.9 us
    all_to_all x1, waiting for transfers between devices: 21.6 us -> 13.4 us  [shards(): lax.all_to_all(tiled, 'ety', 0, 0, tiled=True)]
    all_to_all x1, waiting for transfers between devices: 19.5 us -> 16.4 us  [shards(): lax.all_to_all(pair_z.reshape(chips * own_rows, width), 'ety', 0, 0, tile...]
    unnamed x32 -> x28, local copies, waits for them, and re-layouts: 6.45 us -> 3.77 us
    ppermute x1, waiting for transfers between devices: 0.01 us -> 2.04 us  [shards(): given = lax.ppermute(give_z, 'etc', [(0, 1), (1, 0)])]
  transfers between devices with their start and end apart: 7 -> 7, of which waited for: 4 -> 5; matrix products, arithmetic and copies ran while one was open for 11% -> 17% of each run, Pallas kernels for 0% -> 0%
where the time goes in v4:
time: 96.5 us; the launch traced here: 95.8 us
  waiting for transfers between devices  40.3 us (42%)
  starting transfers between devices  26.8 us (28%)
  other arithmetic  14.9 us (15%)
  matrix products  7.3 us (8%)
  local copies, waits for them, and re-layouts  5.53 us (6%)
    all_to_all x1, waiting for transfers between devices, shards(): lax.all_to_all(pair_z.reshape(chips * own_rows, width), 'ety', 0, 0, tile...  16.4 us
    all_to_all x1, waiting for transfers between devices, shards(): lax.all_to_all(tiled, 'ety', 0, 0, tiled=True)  13.4 us
    ppermute x2, starting transfers between devices, from_behind(): lax.ppermute(value, axis, [(source, source + steps) for source in range(f...  8.13 us
    all_to_all x1, starting transfers between devices, shards(): lax.all_to_all(tiled, 'ety', 0, 0, tiled=True)  7.1 us
    ppermute x2, waiting for transfers between devices, from_behind(): lax.ppermute(value, axis, [(source, source + steps) for source in range(f...  7.08 us
    all_to_all x1, starting transfers between devices, shards(): lax.all_to_all(pair_z.reshape(chips * own_rows, width), 'ety', 0, 0, tile...  4.21 us
    unnamed x28, local copies, waits for them, and re-layouts  3.77 us
    all_to_all x1, starting transfers between devices, shards(): lax.all_to_all(dprob_part.reshape(groups, own_rows), ('ety', 'etc'), 0, 0...  3.49 us
  transfers between devices with their start and end apart: 7, of which 5 were waited for; matrix products, arithmetic and copies ran while one was open for 17% of the time, Pallas kernels for 0%

profile of v4, /device:TPU:198, one launch (start us, length us, event | category | flops | bytes accessed | tf_op | source)
XLA Modules:
  0.0 95.8 jit_solution(13827904486183586491)
XLA Ops:
  0.7 1.2 %fusion.25 = f32[16]{0:T(128)S(1)} fusion(bf16[1,16,3072]{2,1,0:T(8,128)(2,1)} %param.13), kind=kLoop, calls=%fused_computation.41 | loop fusion | flops 147440 | bytes 98368 | tf_op jit(solution)/shard_map/reduce_sum | solution.py:15
  1.9 0.8 dynamic-slice_reduce_fusion
  2.7 0.7 mul.194
  3.4 1.7 %select_reduce_fusion.1 = (f32[16]{0:T(128)}, bf16[16,8]{0,1:T(8,128)(2,1)S(1)}) fusion(s32[16]{0:T(128)S(1)} %broadcast_minimum_fusion.1, bf16[1,3072,8]{1,2,0:T(8,128)(2,1)} %param.18, bf16[1,16,3072]{2,1,0:T(8,128)(2,1)} %param.13, f32[16]{0:T(128)S(1)} %add_rsqrt_fusion, f32[3072]{0:T(1024)S(1)} %bitcast.144), kind=kOutput, calls=%fused_computation.58 | convolution fusion | flops 983664 | bytes 160192 | tf_op jit(solution)/shard_map/dot_general | solution.py:17
  5.1 0.9 fusion.32
  6.1 1.0 %broadcast_in_dim.8 = bf16[8,16,3200]{2,1,0:T(8,128)(2,1)} broadcast(bf16[16,3200]{1,0:T(8,128)(2,1)S(1)} %fusion.32), dimensions={1,2} | broadcast | bytes 921600 | tf_op jit(solution)/shard_map/broadcast_in_dim | solution.py:49
  7.0 7.1 %all-to-all-start = ((bf16[8,16,3200]{2,1,0:T(8,128)(2,1)}), bf16[8,16,3200]{2,1,0:T(8,128)(2,1)}, u32[]{:S(2)}, u32[]{:S(2)}) async-start(bf16[8,16,3200]{2,1,0:T(8,128)(2,1)} %broadcast_in_dim.8), calls=%async_computation | async-start | bytes 1638400 | tf_op jit(solution)/shard_map/all_to_all | solution.py:50
  14.1 1.0 %convolution_convert_fusion = bf16[256,3072]{1,0:T(8,128)(2,1)S(1)} fusion(bf16[1,512,3072]{2,1,0:T(8,128)(2,1)S(1)} %copy-done, bf16[1,256,512]{2,1,0:T(8,128)(2,1)S(1)} %copy-done.5), kind=kOutput, calls=%fused_computation | convolution fusion | flops 806092800 | bytes 4980736 | tf_op jit(solution)/shard_map/dot_general | solution.py:51
  15.2 1.1 %copy-done.1 = bf16[256,3072]{1,0:T(8,128)(2,1)} copy-done((bf16[256,3072]{1,0:T(8,128)(2,1)}, bf16[256,3072]{1,0:T(8,128)(2,1)S(1)}, u32[]{:S(2)}) %copy-start.1) | copy-done | bytes 1572888
  16.3 1.0 %fusion.8 = bf16[8,16,3072]{2,1,0:T(8,128)(2,1)} fusion(pred[]{:T(512)S(6)} %eq.63, bf16[8,2,16,3072]{3,2,1,0:T(8,128)(2,1)S(1)} %bitcast.136), kind=kLoop, calls=%fused_computation.16 | loop fusion | flops 393216 | bytes 2359297 | tf_op jit(solution)/shard_map/jit(_where)/select_n | solution.py:54
  17.3 1.9 %collective-permute-start = (bf16[8,16,3072]{2,1,0:T(8,128)(2,1)}, bf16[8,16,3072]{2,1,0:T(8,128)(2,1)}, u32[]{:S(2)}, u32[]{:S(2)}) collective-permute-start(bf16[8,16,3072]{2,1,0:T(8,128)(2,1)} %fusion.8), channel_id=1, source_target_pairs={{0,1},{1,0},{2,3},{3,2},{4,5},{5,4},{6,7},{7,6},{8,9},{9,8},{10,11... | collective-permute-start | bytes 2359304 | tf_op jit(solution)/shard_map/ppermute | solution.py:55
  19.7 2.0 %collective-permute-done = bf16[8,16,3072]{2,1,0:T(8,128)(2,1)} collective-permute-done((bf16[8,16,3072]{2,1,0:T(8,128)(2,1)}, bf16[8,16,3072]{2,1,0:T(8,128)(2,1)}, u32[]{:S(2)}, u32[]{:S(2)}) %collective-permute-start) | collective-permute-done | bytes 786464 | tf_op jit(solution)/shard_map/ppermute | solution.py:55
  21.8 2.9 %fusion.6 = bf16[8,16,3072]{2,1,0:T(8,128)(2,1)} fusion(bf16[8,16,3072]{2,1,0:T(8,128)(2,1)} %collective-permute-done, pred[]{:T(512)S(6)} %eq.63, bf16[8,2,16,3072]{3,2,1,0:T(8,128)(2,1)} %bitcast.137), kind=kLoop, calls=%fused_computation.10 | loop fusion | flops 1966080 | bytes 3145729 | tf_op jit(solution)/shard_map/convert_element_type | solution.py:56
  24.6 13.4 %all-to-all-done = bf16[8,16,3200]{2,1,0:T(8,128)(2,1)} async-done(((bf16[8,16,3200]{2,1,0:T(8,128)(2,1)}), bf16[8,16,3200]{2,1,0:T(8,128)(2,1)}, u32[]{:S(2)}, u32[]{:S(2)}) %all-to-all-start) | async-done | bytes 819232 | tf_op jit(solution)/shard_map/all_to_all | solution.py:50
  38.0 1.9 %collective-permute-start.1 = (bf16[8,1,16,3200]{3,2,0,1:T(8,128)(2,1)}, bf16[8,1,16,3200]{3,2,0,1:T(8,128)(2,1)}, u32[]{:S(2)}, u32[]{:S(2)}) collective-permute-start(bf16[8,1,16,3200]{3,2,0,1:T(8,128)(2,1)} %bitcast.19), channel_id=1, source_target_pairs={{0,1},{1,0},{2,3},{3,2},{4,5},{5,4},{6,7},{7,6},{8,9},{9,8},{10,11... | collective-permute-start | bytes 2457608 | tf_op jit(solution)/shard_map/ppermute | solution.py:61
  40.6 4.2 %all-to-all-start.1 = ((bf16[8,16,3072]{2,1,0:T(8,128)(2,1)}), bf16[8,16,3072]{2,1,0:T(8,128)(2,1)}, u32[]{:S(2)}, u32[]{:S(2)}) async-start(bf16[8,16,3072]{2,1,0:T(8,128)(2,1)} %fusion.6), calls=%async_computation.1 | async-start | bytes 1572864 | tf_op jit(solution)/shard_map/all_to_all | solution.py:58
  45.4 2.3 %maximum_select_fusion = bf16[8,2,16,3200]{3,2,0,1:T(8,128)(2,1)S(1)} fusion(bf16[8,1,16,3200]{3,2,0,1:T(8,128)(2,1)} %collective-permute-done.1, bf16[8,1,16,3200]{3,2,0,1:T(8,128)(2,1)} %bitcast.19, pred[]{:T(512)S(6)} %eq.63), kind=kLoop, calls=%fused_computation.7 | loop fusion | flops 2457600 | bytes 3276801 | tf_op jit(solution)/shard_map/jit(_where)/select_n | solution.py:62
  47.9 1.2 %copy-done.2 = bf16[8,2,16,3200]{3,2,1,0:T(8,128)(2,1)} copy-done((bf16[8,2,16,3200]{3,2,1,0:T(8,128)(2,1)}, bf16[8,2,16,3200]{3,2,1,0:T(8,128)(2,1)S(1)}, u32[]{:S(2)}) %copy-start.2) | copy-done | bytes 1638424
  49.2 3.3 %fusion.11 = (bf16[1,256,512]{2,1,0:T(8,128)(2,1)}, f32[256]{0:T(256)S(1)}) fusion(f32[256]{0:T(256)S(1)} %bitcast.151, bf16[1,256,512]{2,1,0:T(8,128)(2,1)} %param.14, bf16[1,512,3072]{2,1,0:T(8,128)(2,1)S(1)} %copy-done, bf16[256,3200]{1,0:T(8,128)(2,1)} %bitcast.139), kind=kOutput, calls=%fused_computation.22 | convolution fusion | flops 805961472 | bytes 5244928 | tf_op jit(solution)/shard_map/dot_general | solution.py:71
  52.5 16.4 %all-to-all-done.1 = bf16[8,16,3072]{2,1,0:T(8,128)(2,1)} async-done(((bf16[8,16,3072]{2,1,0:T(8,128)(2,1)}), bf16[8,16,3072]{2,1,0:T(8,128)(2,1)}, u32[]{:S(2)}, u32[]{:S(2)}) %all-to-all-start.1) | async-done | bytes 786464 | tf_op jit(solution)/shard_map/all_to_all | solution.py:58
  68.9 1.3 %convert_reduce_fusion = f32[16,3072]{1,0:T(8,128)S(1)} fusion(bf16[8,16,3072]{2,1,0:T(8,128)(2,1)} %all-to-all-done.1), kind=kLoop, calls=%fused_computation.11 | loop fusion | flops 737280 | bytes 983040 | tf_op jit(solution)/shard_map/reduce_sum | solution.py:59
  70.1 0.7 all_to_all.16
  70.8 3.5 %all-to-all-start.2 = ((f32[16,1,16]{2,1,0:T(1,128)}), f32[16,1,16]{2,1,0:T(1,128)S(1)}, u32[]{:S(2)}, u32[]{:S(2)}) async-start(f32[16,1,16]{2,1,0:T(1,128)} %all_to_all.16), calls=%async_computation.2 | async-start | bytes 16384 | tf_op jit(solution)/shard_map/all_to_all | solution.py:77
  74.3 0.7 fusion.29
  75.0 5.4 %collective-permute-start.2 = (bf16[16,3072]{1,0:T(8,128)(2,1)}, bf16[16,3072]{1,0:T(8,128)(2,1)S(1)}, u32[]{:S(2)}, u32[]{:S(2)}) collective-permute-start(bf16[16,3072]{1,0:T(8,128)(2,1)} %fusion.29), channel_id=1, source_target_pairs={{0,16},{16,32},{32,48},{48,64},{64,80},{80,96},{96,112},{112,128},... | collective-permute-start | bytes 294920 | tf_op jit(solution)/shard_map/ppermute | solution.py:10
  80.5 1.4 %all-to-all-done.2 = f32[16,1,16]{2,1,0:T(1,128)S(1)} async-done(((f32[16,1,16]{2,1,0:T(1,128)}), f32[16,1,16]{2,1,0:T(1,128)S(1)}, u32[]{:S(2)}, u32[]{:S(2)}) %all-to-all-start.2) | async-done | bytes 1056 | tf_op jit(solution)/shard_map/all_to_all | solution.py:77
  82.5 1.1 %fusion.20 = (f32[16]{0:T(128)S(1)}, f32[16,3072]{1,0:T(8,128)S(1)}) fusion(bf16[1,16,3072]{2,1,0:T(8,128)(2,1)S(1)} %copy-done.4, f32[16]{0:T(128)} %copy-done.10, f32[3072]{0:T(1024)} %bitcast.146, bf16[1,3072,8]{1,2,0:T(8,128)(2,1)} %param.18, s32[16]{0:T(128)} %copy-done.11, f32[3072]{0:T(1024)} %bitcast.147, f32[16]{0:T(128)S(1)} %fusion.49), kind=kOutput, calls=%fused_computation.36 | convolution fusion | flops 1130608 | bytes 368896 | tf_op jit(solution)/shard_map/dot_general | solution.py:88
  83.7 1.0 %fusion.24 = bf16[16,3072]{1,0:T(8,128)(2,1)S(1)} fusion(f32[16,3072]{1,0:T(8,128)S(1)} %get-tuple-element.18, bf16[1,16,3072]{2,1,0:T(8,128)(2,1)S(1)} %copy-done.4, f32[16]{0:T(128)S(1)} %broadcast_multiply_fusion, f32[16]{0:T(128)} %copy-done.10, bf16[1,16,3072]{2,1,0:T(8,128)(2,1)} %param.16), kind=kLoop, calls=%fused_computation.40 | loop fusion | flops 393216 | bytes 491648 | tf_op jit(solution)/shard_map/convert_element_type | solution.py:98
  84.7 2.7 %collective-permute-start.3 = (bf16[16,3072]{1,0:T(8,128)(2,1)S(1)}, bf16[16,3072]{1,0:T(8,128)(2,1)S(1)}, u32[]{:S(2)}, u32[]{:S(2)}) collective-permute-start(bf16[16,3072]{1,0:T(8,128)(2,1)S(1)} %fusion.24), channel_id=1, source_target_pairs={{16,0},{32,16},{48,32},{64,48},{80,64},{96,80},{112,96},{128,112},... | collective-permute-start | bytes 294920 | tf_op jit(solution)/shard_map/ppermute | solution.py:10
  87.4 7.1 %collective-permute-done.3 = bf16[16,3072]{1,0:T(8,128)(2,1)S(1)} collective-permute-done((bf16[16,3072]{1,0:T(8,128)(2,1)S(1)}, bf16[16,3072]{1,0:T(8,128)(2,1)S(1)}, u32[]{:S(2)}, u32[]{:S(2)}) %collective-permute-start.3) | collective-permute-done | bytes 98336 | tf_op jit(solution)/shard_map/ppermute | solution.py:10
  94.5 0.6 copy.62
  95.2 0.6 copy.63
  (48 shorter events, 2.8 us)
Async XLA Ops:
  0.6 13.5 %copy-start = (bf16[1,512,3072]{2,1,0:T(8,128)(2,1)S(1)}, bf16[1,512,3072]{2,1,0:T(8,128)(2,1)}, u32[]{:S(2)}) copy-start(bf16[1,512,3072]{2,1,0:T(8,128)(2,1)} %param.19) | copy-start | bytes 9437188
  0.6 13.5 %copy-start.5 = (bf16[1,256,512]{2,1,0:T(8,128)(2,1)S(1)}, bf16[1,256,512]{2,1,0:T(8,128)(2,1)}, u32[]{:S(2)}) copy-start(bf16[1,256,512]{2,1,0:T(8,128)(2,1)} %param.11) | copy-start | bytes 786436
  1.9 13.3 %copy-start.10 = (f32[16]{0:T(128)}, f32[16]{0:T(128)S(1)}, u32[]{:S(2)}) copy-start(f32[16]{0:T(128)S(1)} %add_rsqrt_fusion) | copy-start | bytes 196
  2.7 11.5 %copy-start.11 = (s32[16]{0:T(128)}, s32[16]{0:T(128)S(1)}, u32[]{:S(2)}) copy-start(s32[16]{0:T(128)S(1)} %broadcast_minimum_fusion.1) | copy-start | bytes 196
  3.4 16.1 %copy-start.7 = (f32[1,3072]{1,0:T(1,128)}, f32[1,3072]{1,0:T(1,128)S(1)}, u32[]{:S(2)}) copy-start(f32[1,3072]{1,0:T(1,128)S(1)} %mul.194) | copy-start | bytes 36868
  7.0 31.0 %all-to-all-start = ((bf16[8,16,3200]{2,1,0:T(8,128)(2,1)}), bf16[8,16,3200]{2,1,0:T(8,128)(2,1)}, u32[]{:S(2)}, u32[]{:S(2)}) async-start(bf16[8,16,3200]{2,1,0:T(8,128)(2,1)} %broadcast_in_dim.8), calls=%async_computation | async-start | bytes 1638400 | tf_op jit(solution)/shard_map/all_to_all | solution.py:50
  15.1 1.2 %copy-start.1 = (bf16[256,3072]{1,0:T(8,128)(2,1)}, bf16[256,3072]{1,0:T(8,128)(2,1)S(1)}, u32[]{:S(2)}) copy-start(bf16[256,3072]{1,0:T(8,128)(2,1)S(1)} %convolution_convert_fusion) | copy-start | bytes 4718596
  15.2 4.0 %copy-start.3 = (bf16[1,16,3072]{2,1,0:T(8,128)(2,1)S(1)}, bf16[1,16,3072]{2,1,0:T(8,128)(2,1)}, u32[]{:S(2)}) copy-start(bf16[1,16,3072]{2,1,0:T(8,128)(2,1)} %param.10) | copy-start | bytes 294916
  15.2 4.2 %copy-start.6 = (s32[1,256,2]{1,2,0:T(2,128)S(1)}, s32[1,256,2]{1,2,0:T(2,128)}, u32[]{:S(2)}) copy-start(s32[1,256,2]{1,2,0:T(2,128)} %param.15) | copy-start | bytes 6148
  15.2 4.2 %copy-start.9 = (s32[1,256,2]{1,2,0:T(2,128)S(1)}, s32[1,256,2]{1,2,0:T(2,128)}, u32[]{:S(2)}) copy-start(s32[1,256,2]{1,2,0:T(2,128)} %param.12) | copy-start | bytes 6148
  15.2 4.3 %copy-start.8 = (bf16[1,3072,8]{1,2,0:T(8,128)(2,1)S(1)}, bf16[1,3072,8]{1,2,0:T(8,128)(2,1)}, u32[]{:S(2)}) copy-start(bf16[1,3072,8]{1,2,0:T(8,128)(2,1)} %param.18) | copy-start | bytes 147460
  17.3 4.5 %collective-permute-start = (bf16[8,16,3072]{2,1,0:T(8,128)(2,1)}, bf16[8,16,3072]{2,1,0:T(8,128)(2,1)}, u32[]{:S(2)}, u32[]{:S(2)}) collective-permute-start(bf16[8,16,3072]{2,1,0:T(8,128)(2,1)} %fusion.8), channel_id=1, source_target_pairs={{0,1},{1,0},{2,3},{3,2},{4,5},{5,4},{6,7},{7,6},{8,9},{9,8},{10,11... | collective-permute-start | bytes 2359304 | tf_op jit(solution)/shard_map/ppermute | solution.py:55
  38.0 7.4 %collective-permute-start.1 = (bf16[8,1,16,3200]{3,2,0,1:T(8,128)(2,1)}, bf16[8,1,16,3200]{3,2,0,1:T(8,128)(2,1)}, u32[]{:S(2)}, u32[]{:S(2)}) collective-permute-start(bf16[8,1,16,3200]{3,2,0,1:T(8,128)(2,1)} %bitcast.19), channel_id=1, source_target_pairs={{0,1},{1,0},{2,3},{3,2},{4,5},{5,4},{6,7},{7,6},{8,9},{9,8},{10,11... | collective-permute-start | bytes 2457608 | tf_op jit(solution)/shard_map/ppermute | solution.py:61
  40.6 28.3 %all-to-all-start.1 = ((bf16[8,16,3072]{2,1,0:T(8,128)(2,1)}), bf16[8,16,3072]{2,1,0:T(8,128)(2,1)}, u32[]{:S(2)}, u32[]{:S(2)}) async-start(bf16[8,16,3072]{2,1,0:T(8,128)(2,1)} %fusion.6), calls=%async_computation.1 | async-start | bytes 1572864 | tf_op jit(solution)/shard_map/all_to_all | solution.py:58
  47.9 1.2 %copy-start.2 = (bf16[8,2,16,3200]{3,2,1,0:T(8,128)(2,1)}, bf16[8,2,16,3200]{3,2,1,0:T(8,128)(2,1)S(1)}, u32[]{:S(2)}) copy-start(bf16[8,2,16,3200]{3,2,1,0:T(8,128)(2,1)S(1)} %copy.54) | copy-start | bytes 4915204
  49.2 33.3 %copy-start.4 = (bf16[1,16,3072]{2,1,0:T(8,128)(2,1)S(1)}, bf16[1,16,3072]{2,1,0:T(8,128)(2,1)}, u32[]{:S(2)}) copy-start(bf16[1,16,3072]{2,1,0:T(8,128)(2,1)} %param.13) | copy-start | bytes 294916
  70.8 11.0 %all-to-all-start.2 = ((f32[16,1,16]{2,1,0:T(1,128)}), f32[16,1,16]{2,1,0:T(1,128)S(1)}, u32[]{:S(2)}, u32[]{:S(2)}) async-start(f32[16,1,16]{2,1,0:T(1,128)} %all_to_all.16), calls=%async_computation.2 | async-start | bytes 16384 | tf_op jit(solution)/shard_map/all_to_all | solution.py:77
  75.0 12.4 %collective-permute-start.2 = (bf16[16,3072]{1,0:T(8,128)(2,1)}, bf16[16,3072]{1,0:T(8,128)(2,1)S(1)}, u32[]{:S(2)}, u32[]{:S(2)}) collective-permute-start(bf16[16,3072]{1,0:T(8,128)(2,1)} %fusion.29), channel_id=1, source_target_pairs={{0,16},{16,32},{32,48},{48,64},{64,80},{80,96},{96,112},{112,128},... | collective-permute-start | bytes 294920 | tf_op jit(solution)/shard_map/ppermute | solution.py:10
  84.7 9.8 %collective-permute-start.3 = (bf16[16,3072]{1,0:T(8,128)(2,1)S(1)}, bf16[16,3072]{1,0:T(8,128)(2,1)S(1)}, u32[]{:S(2)}, u32[]{:S(2)}) collective-permute-start(bf16[16,3072]{1,0:T(8,128)(2,1)S(1)} %fusion.24), channel_id=1, source_target_pairs={{16,0},{32,16},{48,32},{64,48},{80,64},{96,80},{112,96},{128,112},... | collective-permute-start | bytes 294920 | tf_op jit(solution)/shard_map/ppermute | solution.py:10

commit v5 on v4

--- a/solution.py
+++ b/solution.py
@@ -28,7 +28,7 @@
     return (route, onehot, sigma, route * sigma)
 
 
-def shards(x_fwd, act_fwd, ids_fwd, x_bwd, act_bwd, ids_bwd, grad_out, gain, w_router, w_down):
+def layer(x_fwd, act_fwd, ids_fwd, x_bwd, act_bwd, ids_bwd, grad_out, gain, w_router, w_down):
     x_fwd, act_fwd, ids_fwd, x_bwd, act_bwd = (x_fwd[0], act_fwd[0], ids_fwd[0], x_bwd[0], act_bwd[0])
     ids_bwd, grad_out, gain, w_router, w_down = (ids_bwd[0], grad_out[0], gain[0], w_router[0], w_down[0])
     experts = w_router.shape[1]
@@ -38,7 +38,7 @@
     first_row = (lax.axis_index("ety") * lax.axis_size("etc") + lax.axis_index("etc")) * own_rows
     pad = 128
 
-    wide_f, inverse_f, logit_f = norm_logits(x_fwd, gain, w_router)
+    wide_f, _, logit_f = norm_logits(x_fwd, gain, w_router)
     backward_wide_rows, backward_inverse_norm, logit_b = norm_logits(x_bwd, gain, w_router)
 
     packed = jnp.concatenate(
@@ -67,15 +67,26 @@
     full_g = full[:, :width]
     full_b = full[:, width : width + experts]
 
-    route_b, onehot_b, sigma_b, coef_b = routing(full_b, ids_bwd, experts)
+    _, _, _, coef_b = routing(full_b, ids_bwd, experts)
     back_up = lax.dot_general(
         full_g, w_down, (((1,), (1,)), ((), ())), preferred_element_type=jnp.float32
     )
     dact = (coef_b[:, None] * back_up).astype(jnp.bfloat16)
     dprob_part = jnp.sum(act_bwd.astype(jnp.float32) * back_up, axis=1)
-    dprob_part, z_sum = lax.optimization_barrier((dprob_part, z_sum))
-    dprob_got = lax.all_to_all(dprob_part.reshape(groups, own_rows), ("ety", "etc"), 0, 0, tiled=True)
-    dprob_mine = jnp.sum(dprob_got, axis=0)
+    halves = dprob_part.reshape(chips, 2, own_rows)
+    keep = jnp.where(core == 0, halves[:, 0], halves[:, 1])
+    give = jnp.where(core == 0, halves[:, 1], halves[:, 0])
+    dprob_left = keep + lax.ppermute(give, "etc", [(0, 1), (1, 0)])
+    chip = lax.axis_index("ety")
+    span = chips // 2
+    while span >= 1:
+        bit = (chip // span) % 2
+        split = dprob_left.reshape(2, -1, own_rows)
+        keep = jnp.where(bit == 0, split[0], split[1])
+        give = jnp.where(bit == 0, split[1], split[0])
+        dprob_left = keep + lax.ppermute(give, "ety", [(i, i ^ span) for i in range(chips)])
+        span //= 2
+    dprob_mine = dprob_left.reshape(own_rows) + 0.0
 
     ids_f_own = lax.dynamic_slice_in_dim(ids_fwd, first_row, own_rows, 0)
     _, _, _, coef_f = routing(logit_f, ids_f_own, experts)
@@ -83,18 +94,17 @@
 
     ids_b_own = lax.dynamic_slice_in_dim(ids_bwd, first_row, own_rows, 0)
     route_mine, onehot_mine, sigma_mine, _ = routing(logit_b, ids_b_own, experts)
-    slope = route_mine * dprob_mine * sigma_mine * (1.0 - sigma_mine)
     router_wide = w_router.astype(jnp.float32)
     spread = router_wide[:, 0][None, :] - jnp.dot(
         onehot_mine, router_wide.T, precision=lax.Precision.HIGHEST
     )
-    dnormed = slope[:, None] * spread
-    scaled_rows = dnormed * gain.astype(jnp.float32)
+    scaled_rows = spread * gain.astype(jnp.float32)
     normalized_input = backward_wide_rows * backward_inverse_norm
-    norm_input_gradient = backward_inverse_norm * (
+    along = (route_mine * sigma_mine * (1.0 - sigma_mine))[:, None] * backward_inverse_norm * (
         scaled_rows
         - normalized_input * jnp.mean(scaled_rows * normalized_input, axis=-1, keepdims=True)
     )
+    norm_input_gradient = dprob_mine[:, None] * along
     input_grad = (grad_out.astype(jnp.float32) + norm_input_gradient).astype(jnp.bfloat16)
     fwd_in = from_behind(layer_out, "section", 1)
     incoming_gradient = from_behind(input_grad, "section", -1)
@@ -118,7 +128,7 @@
         P("section", et, None),
     )
     return jax.shard_map(
-        shards,
+        layer,
         mesh=mesh,
         in_specs=placed,
         out_specs=(P("section", et, None), P("section", et, None), P("section", None, et)),

time: 96.5 us -> 110 us (1.14)
  the two profiles are of different devices: /device:TPU:198 before, /device:TPU:296 now
where the time goes in v5:
time: 110 us
  waiting for transfers between devices  41.2 us (37%)
  starting transfers between devices  39.6 us (36%)
  other arithmetic  12.2 us (11%)
  local copies, waits for them, and re-layouts  8.13 us (7%)
  matrix products  7.29 us (7%)
    ppermute x3, waiting for transfers between devices, layer(): lax.ppermute(give, 'ety', [(i, i ^ span) for i in range(chips)])  16.8 us
    all_to_all x1, waiting for transfers between devices, layer(): lax.all_to_all(tiled, 'ety', 0, 0, tiled=True)  14.9 us
    ppermute x3, starting transfers between devices, layer(): lax.ppermute(give, 'ety', [(i, i ^ span) for i in range(chips)])  11.8 us
    all_to_all x1, starting transfers between devices, layer(): lax.all_to_all(pair_z.reshape(chips * own_rows, width), 'ety', 0, 0, tile...  8.87 us
    ppermute x2, waiting for transfers between devices, from_behind(): lax.ppermute(value, axis, [(source, source + steps) for source in range(f...  7.74 us
    all_to_all x1, starting transfers between devices, layer(): lax.all_to_all(tiled, 'ety', 0, 0, tiled=True)  7.09 us
    unnamed x30, local copies, waits for them, and re-layouts  6.45 us
    ppermute x2, starting transfers between devices, from_behind(): lax.ppermute(value, axis, [(source, source + steps) for source in range(f...  5.83 us
  transfers between devices with their start and end apart: 10, of which 6 were waited for; matrix products, arithmetic and copies ran while one was open for 12% of the time, Pallas kernels for 0%

profile of v5, /device:TPU:296, one launch (start us, length us, event | category | flops | bytes accessed | tf_op | source)
XLA Modules:
  0.0 109.5 jit_solution(9944072291096097031)
XLA Ops:
  0.7 1.9 %copy-done = bf16[1,512,3072]{2,1,0:T(8,128)(2,1)S(1)} copy-done((bf16[1,512,3072]{2,1,0:T(8,128)(2,1)S(1)}, bf16[1,512,3072]{2,1,0:T(8,128)(2,1)}, u32[]{:S(2)}) %copy-start) | copy-done | bytes 3145752
  2.5 1.9 %convolution_convert_fusion = bf16[256,3072]{1,0:T(8,128)(2,1)S(1)} fusion(bf16[1,512,3072]{2,1,0:T(8,128)(2,1)S(1)} %copy-done, bf16[1,256,512]{2,1,0:T(8,128)(2,1)} %param.11), kind=kOutput, calls=%fused_computation | convolution fusion | flops 806092800 | bytes 4980736 | tf_op jit(solution)/shard_map/dot_general | solution.py:51
  4.5 1.1 copy-done.1
  5.6 1.0 fusion.7
  6.6 2.0 %collective-permute-start = (bf16[8,16,3072]{2,1,0:T(8,128)(2,1)}, bf16[8,16,3072]{2,1,0:T(8,128)(2,1)}, u32[]{:S(2)}, u32[]{:S(2)}) collective-permute-start(bf16[8,16,3072]{2,1,0:T(8,128)(2,1)} %fusion.7), channel_id=1, source_target_pairs={{0,1},{1,0},{2,3},{3,2},{4,5},{5,4},{6,7},{7,6},{8,9},{9,8},{10,11... | collective-permute-start | bytes 2359304 | tf_op jit(solution)/shard_map/ppermute | solution.py:55
  9.3 1.0 broadcast_in_dim.8
  10.3 7.1 %all-to-all-start = ((bf16[8,16,3200]{2,1,0:T(8,128)(2,1)}), bf16[8,16,3200]{2,1,0:T(8,128)(2,1)}, u32[]{:S(2)}, u32[]{:S(2)}) async-start(bf16[8,16,3200]{2,1,0:T(8,128)(2,1)} %broadcast_in_dim.8), calls=%async_computation | async-start | bytes 1638400 | tf_op jit(solution)/shard_map/all_to_all | solution.py:50
  19.8 2.9 %fusion.5 = bf16[8,16,3072]{2,1,0:T(8,128)(2,1)} fusion(bf16[8,16,3072]{2,1,0:T(8,128)(2,1)} %collective-permute-done, pred[]{:T(512)S(6)} %eq.81, bf16[8,2,16,3072]{3,2,1,0:T(8,128)(2,1)} %bitcast.146), kind=kLoop, calls=%fused_computation.9 | loop fusion | flops 1966080 | bytes 3145729 | tf_op jit(solution)/shard_map/convert_element_type | solution.py:56
  22.6 14.9 %all-to-all-done = bf16[8,16,3200]{2,1,0:T(8,128)(2,1)} async-done(((bf16[8,16,3200]{2,1,0:T(8,128)(2,1)}), bf16[8,16,3200]{2,1,0:T(8,128)(2,1)}, u32[]{:S(2)}, u32[]{:S(2)}) %all-to-all-start) | async-done | bytes 819232 | tf_op jit(solution)/shard_map/all_to_all | solution.py:50
  37.5 1.9 %collective-permute-start.2 = (bf16[8,1,16,3200]{3,2,1,0:T(8,128)(2,1)}, bf16[8,1,16,3200]{3,2,1,0:T(8,128)(2,1)S(1)}, u32[]{:S(2)}, u32[]{:S(2)}) collective-permute-start(bf16[8,1,16,3200]{3,2,1,0:T(8,128)(2,1)} %bitcast.18), channel_id=1, source_target_pairs={{0,1},{1,0},{2,3},{3,2},{4,5},{5,4},{6,7},{7,6},{8,9},{9,8},{10,11... | collective-permute-start | bytes 2457608 | tf_op jit(solution)/shard_map/ppermute | solution.py:61
  39.4 1.7 %fusion.19 = (f32[16]{0:T(128)}, f32[16,3072]{1,0:T(8,128)S(1)}) fusion(bf16[1,16,3072]{2,1,0:T(8,128)(2,1)S(1)} %copy-done.3, f32[16]{0:T(128)} %copy-done.11, f32[3072]{0:T(1024)S(1)} %bitcast.155, bf16[1,3072,8]{1,2,0:T(8,128)(2,1)} %param.18, s32[16]{0:T(128)} %copy-done.12, f32[3072]{0:T(1024)S(1)} %bitcast.156), kind=kOutput, calls=%fused_computation.35 | convolution fusion | flops 1081456 | bytes 368832 | tf_op jit(solution)/shard_map/dot_general | solution.py:98
  41.1 0.8 collective-permute-done.2
  41.9 1.7 %maximum_select_fusion = bf16[8,2,16,3200]{3,2,1,0:T(8,128)(2,1)S(1)} fusion(bf16[8,1,16,3200]{3,2,1,0:T(8,128)(2,1)S(1)} %collective-permute-done.2, bf16[8,1,16,3200]{3,2,1,0:T(8,128)(2,1)} %bitcast.18, pred[]{:T(512)S(6)} %eq.81), kind=kLoop, calls=%fused_computation.6 | loop fusion | flops 2457600 | bytes 3276801 | tf_op jit(solution)/shard_map/jit(_where)/select_n | solution.py:62
  43.6 1.2 %copy-done.2 = bf16[8,2,16,3200]{3,2,1,0:T(8,128)(2,1)} copy-done((bf16[8,2,16,3200]{3,2,1,0:T(8,128)(2,1)}, bf16[8,2,16,3200]{3,2,1,0:T(8,128)(2,1)S(1)}, u32[]{:S(2)}) %copy-start.2) | copy-done | bytes 1638424
  45.4 0.9 copy.32
  46.4 3.3 %fusion.10 = (bf16[1,256,512]{2,1,0:T(8,128)(2,1)}, f32[256]{0:T(256)S(1)}) fusion(f32[256]{0:T(256)S(1)} %bitcast.161, bf16[1,256,512]{2,1,0:T(8,128)(2,1)} %param.14, bf16[1,512,3072]{2,1,0:T(8,128)(2,1)S(1)} %copy-done, bf16[256,3200]{1,0:T(8,128)(2,1)} %bitcast.148), kind=kOutput, calls=%fused_computation.21 | convolution fusion | flops 805961472 | bytes 5244928 | tf_op jit(solution)/shard_map/dot_general | solution.py:71
  49.7 2.0 %collective-permute-start.3 = (f32[8,16]{1,0:T(8,128)S(1)}, f32[8,16]{1,0:T(8,128)S(1)}, u32[]{:S(2)}, u32[]{:S(2)}) collective-permute-start(f32[8,16]{1,0:T(8,128)S(1)} %bitcast.159), channel_id=1, source_target_pairs={{0,1},{1,0},{2,3},{3,2},{4,5},{5,4},{6,7},{7,6},{8,9},{9,8},{10,11... | collective-permute-start | bytes 1544 | tf_op jit(solution)/shard_map/ppermute | solution.py:79
  51.8 1.0 collective-permute-done.3
  52.8 6.4 %collective-permute-start.4 = (f32[4,16]{1,0:T(4,128)S(1)}, f32[4,16]{1,0:T(4,128)S(1)}, u32[]{:S(2)}, u32[]{:S(2)}) collective-permute-start(f32[4,16]{1,0:T(4,128)S(1)} %slice_select_fusion), channel_id=1, source_target_pairs={{0,8},{2,10},{4,12},{6,14},{8,0},{10,2},{12,4},{14,6},{1,9},{3,11}... | collective-permute-start | bytes 776 | tf_op jit(solution)/shard_map/ppermute | solution.py:87
  59.2 3.0 %collective-permute-done.4 = f32[4,16]{1,0:T(4,128)S(1)} collective-permute-done((f32[4,16]{1,0:T(4,128)S(1)}, f32[4,16]{1,0:T(4,128)S(1)}, u32[]{:S(2)}, u32[]{:S(2)}) %collective-permute-start.4) | collective-permute-done | bytes 288 | tf_op jit(solution)/shard_map/ppermute | solution.py:87
  62.2 2.1 %collective-permute-start.5 = (f32[2,16]{1,0:T(2,128)S(1)}, f32[2,16]{1,0:T(2,128)S(1)}, u32[]{:S(2)}, u32[]{:S(2)}) collective-permute-start(f32[2,16]{1,0:T(2,128)S(1)} %broadcast_select_fusion.2), channel_id=1, source_target_pairs={{0,4},{2,6},{4,0},{6,2},{8,12},{10,14},{12,8},{14,10},{1,5},{3,7},... | collective-permute-start | bytes 392 | tf_op jit(solution)/shard_map/ppermute | solution.py:87
  64.3 8.9 %all-to-all-start.1 = ((bf16[8,16,3072]{2,1,0:T(8,128)(2,1)}), bf16[8,16,3072]{2,1,0:T(8,128)(2,1)}, u32[]{:S(2)}, u32[]{:S(2)}) async-start(bf16[8,16,3072]{2,1,0:T(8,128)(2,1)} %fusion.5), calls=%async_computation.1 | async-start | bytes 1572864 | tf_op jit(solution)/shard_map/all_to_all | solution.py:58
  73.2 3.4 %collective-permute-start.6 = (f32[1,16]{1,0:T(1,128)S(1)}, f32[1,16]{1,0:T(1,128)S(1)}, u32[]{:S(2)}, u32[]{:S(2)}) collective-permute-start(f32[1,16]{1,0:T(1,128)S(1)} %broadcast_select_fusion.3), channel_id=1, source_target_pairs={{0,2},{2,0},{4,6},{6,4},{8,10},{10,8},{12,14},{14,12},{1,3},{3,1},... | collective-permute-start | bytes 200 | tf_op jit(solution)/shard_map/ppermute | solution.py:87
  77.1 13.8 %collective-permute-done.6 = f32[1,16]{1,0:T(1,128)S(1)} collective-permute-done((f32[1,16]{1,0:T(1,128)S(1)}, f32[1,16]{1,0:T(1,128)S(1)}, u32[]{:S(2)}, u32[]{:S(2)}) %collective-permute-start.6) | collective-permute-done | bytes 96 | tf_op jit(solution)/shard_map/ppermute | solution.py:87
  91.0 1.7 %fusion.24 = bf16[16,3072]{1,0:T(8,128)(2,1)} fusion(f32[16,3072]{1,0:T(8,128)S(1)} %get-tuple-element.14, bf16[1,16,3072]{2,1,0:T(8,128)(2,1)S(1)} %copy-done.3, f32[16]{0:T(128)S(1)} %broadcast_multiply_fusion, f32[16]{0:T(128)} %copy-done.11, f32[16]{0:T(128)} %fusion.48, f32[16]{0:T(128)S(1)} %fusion.47, bf16[1,16,3072]{2,1,0:T(8,128)(2,1)} %param.16), kind=kLoop, calls=%fused_computation.40 | loop fusion | flops 442368 | bytes 491776 | tf_op jit(solution)/shard_map/convert_element_type | solution.py:108
  92.6 3.8 %collective-permute-start.7 = (bf16[16,3072]{1,0:T(8,128)(2,1)}, bf16[16,3072]{1,0:T(8,128)(2,1)S(1)}, u32[]{:S(2)}, u32[]{:S(2)}) collective-permute-start(bf16[16,3072]{1,0:T(8,128)(2,1)} %fusion.24), channel_id=1, source_target_pairs={{16,0},{32,16},{48,32},{64,48},{80,64},{96,80},{112,96},{128,112},... | collective-permute-start | bytes 294920 | tf_op jit(solution)/shard_map/ppermute | solution.py:10
  96.4 1.3 %convert_reduce_fusion = f32[16,3072]{1,0:T(8,128)S(1)} fusion(bf16[8,16,3072]{2,1,0:T(8,128)(2,1)} %all-to-all-done.1), kind=kLoop, calls=%fused_computation.10 | loop fusion | flops 737280 | bytes 983040 | tf_op jit(solution)/shard_map/reduce_sum | solution.py:59
  97.7 0.7 fusion.29
  98.4 2.1 %collective-permute-start.1 = (bf16[16,3072]{1,0:T(8,128)(2,1)S(1)}, bf16[16,3072]{1,0:T(8,128)(2,1)S(1)}, u32[]{:S(2)}, u32[]{:S(2)}) collective-permute-start(bf16[16,3072]{1,0:T(8,128)(2,1)S(1)} %fusion.29), channel_id=1, source_target_pairs={{0,16},{16,32},{32,48},{48,64},{64,80},{80,96},{96,112},{112,128},... | collective-permute-start | bytes 294920 | tf_op jit(solution)/shard_map/ppermute | solution.py:10
  100.5 7.7 %collective-permute-done.1 = bf16[16,3072]{1,0:T(8,128)(2,1)S(1)} collective-permute-done((bf16[16,3072]{1,0:T(8,128)(2,1)S(1)}, bf16[16,3072]{1,0:T(8,128)(2,1)S(1)}, u32[]{:S(2)}, u32[]{:S(2)}) %collective-permute-start.1) | collective-permute-done | bytes 98336 | tf_op jit(solution)/shard_map/ppermute | solution.py:10
  108.2 0.6 copy.36
  108.9 0.6 copy.37
  (62 shorter events, 4.4 us)
Async XLA Ops:
  0.6 1.9 %copy-start = (bf16[1,512,3072]{2,1,0:T(8,128)(2,1)S(1)}, bf16[1,512,3072]{2,1,0:T(8,128)(2,1)}, u32[]{:S(2)}) copy-start(bf16[1,512,3072]{2,1,0:T(8,128)(2,1)} %param.19) | copy-start | bytes 9437188
  4.5 1.2 %copy-start.1 = (bf16[256,3072]{1,0:T(8,128)(2,1)}, bf16[256,3072]{1,0:T(8,128)(2,1)S(1)}, u32[]{:S(2)}) copy-start(bf16[256,3072]{1,0:T(8,128)(2,1)S(1)} %convolution_convert_fusion) | copy-start | bytes 4718596
  4.5 4.2 %copy-start.7 = (s32[1,256,2]{1,2,0:T(2,128)S(1)}, s32[1,256,2]{1,2,0:T(2,128)}, u32[]{:S(2)}) copy-start(s32[1,256,2]{1,2,0:T(2,128)} %param.15) | copy-start | bytes 6148
  4.5 4.2 %copy-start.10 = (s32[1,256,2]{1,2,0:T(2,128)S(1)}, s32[1,256,2]{1,2,0:T(2,128)}, u32[]{:S(2)}) copy-start(s32[1,256,2]{1,2,0:T(2,128)} %param.12) | copy-start | bytes 6148
  4.5 4.3 %copy-start.3 = (bf16[1,16,3072]{2,1,0:T(8,128)(2,1)S(1)}, bf16[1,16,3072]{2,1,0:T(8,128)(2,1)}, u32[]{:S(2)}) copy-start(bf16[1,16,3072]{2,1,0:T(8,128)(2,1)} %param.13) | copy-start | bytes 294916
  4.5 4.4 %copy-start.8 = (bf16[1,3072]{1,0:T(2,128)(2,1)S(1)}, bf16[1,3072]{1,0:T(2,128)(2,1)}, u32[]{:S(2)}) copy-start(bf16[1,3072]{1,0:T(2,128)(2,1)} %param.17) | copy-start | bytes 18436
  4.5 4.4 %copy-start.6 = (bf16[1,3072,8]{1,2,0:T(8,128)(2,1)S(1)}, bf16[1,3072,8]{1,2,0:T(8,128)(2,1)}, u32[]{:S(2)}) copy-start(bf16[1,3072,8]{1,2,0:T(8,128)(2,1)} %param.18) | copy-start | bytes 147460
  4.5 4.8 %copy-start.5 = (bf16[1,16,3072]{2,1,0:T(8,128)(2,1)S(1)}, bf16[1,16,3072]{2,1,0:T(8,128)(2,1)}, u32[]{:S(2)}) copy-start(bf16[1,16,3072]{2,1,0:T(8,128)(2,1)} %param.16) | copy-start | bytes 294916
  6.6 10.8 %copy-start.4 = (bf16[1,16,3072]{2,1,0:T(8,128)(2,1)S(1)}, bf16[1,16,3072]{2,1,0:T(8,128)(2,1)}, u32[]{:S(2)}) copy-start(bf16[1,16,3072]{2,1,0:T(8,128)(2,1)} %param.10) | copy-start | bytes 294916
  6.6 13.2 %collective-permute-start = (bf16[8,16,3072]{2,1,0:T(8,128)(2,1)}, bf16[8,16,3072]{2,1,0:T(8,128)(2,1)}, u32[]{:S(2)}, u32[]{:S(2)}) collective-permute-start(bf16[8,16,3072]{2,1,0:T(8,128)(2,1)} %fusion.7), channel_id=1, source_target_pairs={{0,1},{1,0},{2,3},{3,2},{4,5},{5,4},{6,7},{7,6},{8,9},{9,8},{10,11... | collective-permute-start | bytes 2359304 | tf_op jit(solution)/shard_map/ppermute | solution.py:55
  8.8 9.4 %copy-start.12 = (s32[16]{0:T(128)}, s32[16]{0:T(128)S(1)}, u32[]{:S(2)}) copy-start(s32[16]{0:T(128)S(1)} %broadcast_minimum_fusion.1) | copy-start | bytes 196
  8.9 9.7 %copy-start.11 = (f32[16]{0:T(128)}, f32[16]{0:T(128)S(1)}, u32[]{:S(2)}) copy-start(f32[16]{0:T(128)S(1)} %add_rsqrt_fusion) | copy-start | bytes 196
  10.3 27.2 %all-to-all-start = ((bf16[8,16,3200]{2,1,0:T(8,128)(2,1)}), bf16[8,16,3200]{2,1,0:T(8,128)(2,1)}, u32[]{:S(2)}, u32[]{:S(2)}) async-start(bf16[8,16,3200]{2,1,0:T(8,128)(2,1)} %broadcast_in_dim.8), calls=%async_computation | async-start | bytes 1638400 | tf_op jit(solution)/shard_map/all_to_all | solution.py:50
  37.5 4.4 %collective-permute-start.2 = (bf16[8,1,16,3200]{3,2,1,0:T(8,128)(2,1)}, bf16[8,1,16,3200]{3,2,1,0:T(8,128)(2,1)S(1)}, u32[]{:S(2)}, u32[]{:S(2)}) collective-permute-start(bf16[8,1,16,3200]{3,2,1,0:T(8,128)(2,1)} %bitcast.18), channel_id=1, source_target_pairs={{0,1},{1,0},{2,3},{3,2},{4,5},{5,4},{6,7},{7,6},{8,9},{9,8},{10,11... | collective-permute-start | bytes 2457608 | tf_op jit(solution)/shard_map/ppermute | solution.py:61
  41.1 5.2 %copy-start.9 = (s32[256]{0:T(256)S(1)}, s32[256]{0:T(256)}, u32[]{:S(2)}) copy-start(s32[256]{0:T(256)} %broadcast_minimum_fusion) | copy-start | bytes 3076
  43.6 1.2 %copy-start.2 = (bf16[8,2,16,3200]{3,2,1,0:T(8,128)(2,1)}, bf16[8,2,16,3200]{3,2,1,0:T(8,128)(2,1)S(1)}, u32[]{:S(2)}) copy-start(bf16[8,2,16,3200]{3,2,1,0:T(8,128)(2,1)S(1)} %maximum_select_fusion) | copy-start | bytes 4915204
  49.7 3.1 %collective-permute-start.3 = (f32[8,16]{1,0:T(8,128)S(1)}, f32[8,16]{1,0:T(8,128)S(1)}, u32[]{:S(2)}, u32[]{:S(2)}) collective-permute-start(f32[8,16]{1,0:T(8,128)S(1)} %bitcast.159), channel_id=1, source_target_pairs={{0,1},{1,0},{2,3},{3,2},{4,5},{5,4},{6,7},{7,6},{8,9},{9,8},{10,11... | collective-permute-start | bytes 1544 | tf_op jit(solution)/shard_map/ppermute | solution.py:79
  52.8 9.4 %collective-permute-start.4 = (f32[4,16]{1,0:T(4,128)S(1)}, f32[4,16]{1,0:T(4,128)S(1)}, u32[]{:S(2)}, u32[]{:S(2)}) collective-permute-start(f32[4,16]{1,0:T(4,128)S(1)} %slice_select_fusion), channel_id=1, source_target_pairs={{0,8},{2,10},{4,12},{6,14},{8,0},{10,2},{12,4},{14,6},{1,9},{3,11}... | collective-permute-start | bytes 776 | tf_op jit(solution)/shard_map/ppermute | solution.py:87
  62.2 11.0 %collective-permute-start.5 = (f32[2,16]{1,0:T(2,128)S(1)}, f32[2,16]{1,0:T(2,128)S(1)}, u32[]{:S(2)}, u32[]{:S(2)}) collective-permute-start(f32[2,16]{1,0:T(2,128)S(1)} %broadcast_select_fusion.2), channel_id=1, source_target_pairs={{0,4},{2,6},{4,0},{6,2},{8,12},{10,14},{12,8},{14,10},{1,5},{3,7},... | collective-permute-start | bytes 392 | tf_op jit(solution)/shard_map/ppermute | solution.py:87
  64.3 32.1 %all-to-all-start.1 = ((bf16[8,16,3072]{2,1,0:T(8,128)(2,1)}), bf16[8,16,3072]{2,1,0:T(8,128)(2,1)}, u32[]{:S(2)}, u32[]{:S(2)}) async-start(bf16[8,16,3072]{2,1,0:T(8,128)(2,1)} %fusion.5), calls=%async_computation.1 | async-start | bytes 1572864 | tf_op jit(solution)/shard_map/all_to_all | solution.py:58
  73.2 17.8 %collective-permute-start.6 = (f32[1,16]{1,0:T(1,128)S(1)}, f32[1,16]{1,0:T(1,128)S(1)}, u32[]{:S(2)}, u32[]{:S(2)}) collective-permute-start(f32[1,16]{1,0:T(1,128)S(1)} %broadcast_select_fusion.3), channel_id=1, source_target_pairs={{0,2},{2,0},{4,6},{6,4},{8,10},{10,8},{12,14},{14,12},{1,3},{3,1},... | collective-permute-start | bytes 200 | tf_op jit(solution)/shard_map/ppermute | solution.py:87
  92.6 7.9 %collective-permute-start.7 = (bf16[16,3072]{1,0:T(8,128)(2,1)}, bf16[16,3072]{1,0:T(8,128)(2,1)S(1)}, u32[]{:S(2)}, u32[]{:S(2)}) collective-permute-start(bf16[16,3072]{1,0:T(8,128)(2,1)} %fusion.24), channel_id=1, source_target_pairs={{16,0},{32,16},{48,32},{64,48},{80,64},{96,80},{112,96},{128,112},... | collective-permute-start | bytes 294920 | tf_op jit(solution)/shard_map/ppermute | solution.py:10
  98.4 9.8 %collective-permute-start.1 = (bf16[16,3072]{1,0:T(8,128)(2,1)S(1)}, bf16[16,3072]{1,0:T(8,128)(2,1)S(1)}, u32[]{:S(2)}, u32[]{:S(2)}) collective-permute-start(bf16[16,3072]{1,0:T(8,128)(2,1)S(1)} %fusion.29), channel_id=1, source_target_pairs={{0,16},{16,32},{32,48},{48,64},{64,80},{80,96},{96,112},{112,128},... | collective-permute-start | bytes 294920 | tf_op jit(solution)/shard_map/ppermute | solution.py:10

commit v6 on v5

--- a/solution.py
+++ b/solution.py
@@ -34,63 +34,87 @@
     experts = w_router.shape[1]
     width = x_fwd.shape[1]
     own_rows = x_fwd.shape[0]
-    groups = lax.axis_size("ety") * lax.axis_size("etc")
-    first_row = (lax.axis_index("ety") * lax.axis_size("etc") + lax.axis_index("etc")) * own_rows
+    hidden = w_down.shape[0]
+    chips = lax.axis_size("ety")
+    core = lax.axis_index("etc")
+    swap = [(0, 1), (1, 0)]
+    first_row = (lax.axis_index("ety") * 2 + core) * own_rows
     pad = 128
+
+    def by_core(mine, other):
+        return jnp.where(
+            core == 0, jnp.stack([mine, other], axis=1), jnp.stack([other, mine], axis=1)
+        )
+
+    tiled = jnp.broadcast_to(grad_out[None], (chips,) + grad_out.shape)
+    same_g = lax.all_to_all(tiled.reshape(chips * own_rows, width), "ety", 0, 0, tiled=True)
+    other_g = lax.ppermute(same_g, "etc", swap)
 
     wide_f, _, logit_f = norm_logits(x_fwd, gain, w_router)
     backward_wide_rows, backward_inverse_norm, logit_b = norm_logits(x_bwd, gain, w_router)
+    logit_pad = jnp.pad(logit_b, ((0, 0), (0, pad - experts)))
 
-    packed = jnp.concatenate(
-        [grad_out, jnp.pad(logit_b, ((0, 0), (0, pad - experts)))], axis=1
-    )
-    chips = lax.axis_size("ety")
-    core = lax.axis_index("etc")
-    tiled = jnp.broadcast_to(packed[None], (chips,) + packed.shape).reshape(chips * own_rows, -1)
-    same_core = lax.all_to_all(tiled, "ety", 0, 0, tiled=True).reshape(chips, 1, own_rows, -1)
     z_fwd = jnp.dot(act_fwd, w_down, preferred_element_type=jnp.float32).astype(jnp.bfloat16)
     z_fwd = z_fwd.reshape(chips, 2, own_rows, width)
     mine_z = jnp.where(core == 0, z_fwd[:, 0], z_fwd[:, 1])
     give_z = jnp.where(core == 0, z_fwd[:, 1], z_fwd[:, 0])
-    given = lax.ppermute(give_z, "etc", [(0, 1), (1, 0)])
-    pair_z = (mine_z.astype(jnp.float32) + given.astype(jnp.float32)).astype(jnp.bfloat16)
-    pair_z, same_core = lax.optimization_barrier((pair_z, same_core))
-    got = lax.all_to_all(pair_z.reshape(chips * own_rows, width), "ety", 0, 0, tiled=True)
-    z_sum = jnp.sum(got.reshape(chips, own_rows, width).astype(jnp.float32), axis=0)
+    given = lax.ppermute(
+        jnp.concatenate([give_z, jnp.broadcast_to(logit_pad[None], (chips, own_rows, pad))], axis=-1),
+        "etc",
+        swap,
+    )
+    pair_z = (mine_z.astype(jnp.float32) + given[..., :width].astype(jnp.float32)).astype(jnp.bfloat16)
+    partner_logits = given[0, :, width : width + experts]
 
-    other_core = lax.ppermute(same_core, "etc", [(0, 1), (1, 0)])
-    full = jnp.where(
-        core == 0,
-        jnp.concatenate([same_core, other_core], axis=1),
-        jnp.concatenate([other_core, same_core], axis=1),
-    ).reshape(groups * own_rows, -1)
-    full_g = full[:, :width]
-    full_b = full[:, width : width + experts]
+    act_halves = act_bwd.reshape(chips, 2, own_rows, hidden)
+    act_same = jnp.where(core == 0, act_halves[:, 0], act_halves[:, 1])
+    act_other = jnp.where(core == 0, act_halves[:, 1], act_halves[:, 0])
 
-    _, _, _, coef_b = routing(full_b, ids_bwd, experts)
-    back_up = lax.dot_general(
-        full_g, w_down, (((1,), (1,)), ((), ())), preferred_element_type=jnp.float32
+    def up_of(rows):
+        return lax.dot_general(
+            rows, w_down, (((1,), (1,)), ((), ())), preferred_element_type=jnp.float32
+        ).reshape(chips, own_rows, hidden)
+
+    up_same = up_of(same_g)
+    up_other = up_of(other_g)
+    dp_same = jnp.sum(act_same.astype(jnp.float32) * up_same, axis=-1)
+    dp_other = jnp.sum(act_other.astype(jnp.float32) * up_other, axis=-1)
+    dprob_part = by_core(dp_same, dp_other)
+    dprob_hi = dprob_part.astype(jnp.bfloat16)
+    dprob_lo = (dprob_part - dprob_hi.astype(jnp.float32)).astype(jnp.bfloat16)
+    extra = jnp.concatenate(
+        [
+            dprob_hi[:, 0, :, None],
+            dprob_lo[:, 0, :, None],
+            dprob_hi[:, 1, :, None],
+            dprob_lo[:, 1, :, None],
+            jnp.broadcast_to(logit_b[None], (chips, own_rows, experts)),
+            jnp.broadcast_to(partner_logits[None], (chips, own_rows, experts)),
+            jnp.zeros((chips, own_rows, pad - 4 - 2 * experts), jnp.bfloat16),
+        ],
+        axis=-1,
     )
-    dact = (coef_b[:, None] * back_up).astype(jnp.bfloat16)
-    dprob_part = jnp.sum(act_bwd.astype(jnp.float32) * back_up, axis=1)
-    halves = dprob_part.reshape(chips, 2, own_rows)
-    keep = jnp.where(core == 0, halves[:, 0], halves[:, 1])
-    give = jnp.where(core == 0, halves[:, 1], halves[:, 0])
-    dprob_left = keep + lax.ppermute(give, "etc", [(0, 1), (1, 0)])
-    chip = lax.axis_index("ety")
-    span = chips // 2
-    while span >= 1:
-        bit = (chip // span) % 2
-        split = dprob_left.reshape(2, -1, own_rows)
-        keep = jnp.where(bit == 0, split[0], split[1])
-        give = jnp.where(bit == 0, split[1], split[0])
-        dprob_left = keep + lax.ppermute(give, "ety", [(i, i ^ span) for i in range(chips)])
-        span //= 2
-    dprob_mine = dprob_left.reshape(own_rows) + 0.0
+
+    sent = jnp.concatenate([pair_z, extra], axis=-1).reshape(chips * own_rows, width + pad)
+    got = lax.all_to_all(sent, "ety", 0, 0, tiled=True).reshape(chips, own_rows, width + pad)
+    z_sum = jnp.sum(got[..., :width].astype(jnp.float32), axis=0)
+    tail = got[..., width:].astype(jnp.float32)
+    d_core0 = jnp.sum(tail[..., 0] + tail[..., 1], axis=0)
+    d_core1 = jnp.sum(tail[..., 2] + tail[..., 3], axis=0)
+    d_mine = jnp.where(core == 0, d_core0, d_core1)
+    d_partner = jnp.where(core == 0, d_core1, d_core0)
+    dprob_mine = d_mine + lax.ppermute(d_partner, "etc", swap)
 
     ids_f_own = lax.dynamic_slice_in_dim(ids_fwd, first_row, own_rows, 0)
     _, _, _, coef_f = routing(logit_f, ids_f_own, experts)
     layer_out = (wide_f + coef_f[:, None] * z_sum).astype(jnp.bfloat16)
+
+    full_b = by_core(
+        got[..., width + 4 : width + 4 + experts], got[..., width + 4 + experts : width + 4 + 2 * experts]
+    ).reshape(chips * 2 * own_rows, experts)
+    _, _, _, coef_b = routing(full_b, ids_bwd, experts)
+    back_up = by_core(up_same, up_other).reshape(chips * 2 * own_rows, hidden)
+    dact = (coef_b[:, None] * back_up).astype(jnp.bfloat16)
 
     ids_b_own = lax.dynamic_slice_in_dim(ids_bwd, first_row, own_rows, 0)
     route_mine, onehot_mine, sigma_mine, _ = routing(logit_b, ids_b_own, experts)

time: 110 us -> 123 us (1.12)
  the two profiles are of different devices: /device:TPU:296 before, /device:TPU:198 now
where the time goes in v6:
time: 123 us; the launch traced here: 122 us
  waiting for transfers between devices  37.8 us (31%)
  other arithmetic  26.4 us (21%)
  starting transfers between devices  24.8 us (20%)
  local copies, waits for them, and re-layouts  19.2 us (16%)
  matrix products  12.4 us (10%)
    all_to_all x1, waiting for transfers between devices, layer(): lax.all_to_all(sent, 'ety', 0, 0, tiled=True)  17.4 us
    all_to_all x1, waiting for transfers between devices, layer(): lax.all_to_all(tiled.reshape(chips * own_rows, width), 'ety', 0, 0, tiled...  14.1 us
    concatenate x7, local copies, waits for them, and re-layouts, layer(): jnp.concatenate([pair_z, extra], axis=-1)  9.01 us
    ppermute x2, starting transfers between devices, from_behind(): lax.ppermute(value, axis, [(source, source + steps) for source in range(f...  7.32 us
    all_to_all x1, starting transfers between devices, layer(): lax.all_to_all(tiled.reshape(chips * own_rows, width), 'ety', 0, 0, tiled...  7.1 us
    ppermute x2, waiting for transfers between devices, from_behind(): lax.ppermute(value, axis, [(source, source + steps) for source in range(f...  6.3 us
    dot_general x2, matrix products, up_of(): lax.dot_general(rows, w_down, (((1,), (1,)), ((), ())), preferred_element...  5.44 us
    all_to_all x1, starting transfers between devices, layer(): lax.all_to_all(sent, 'ety', 0, 0, tiled=True)  4.37 us
  transfers between devices with their start and end apart: 7, of which 3 were waited for; matrix products, arithmetic and copies ran while one was open for 25% of the time, Pallas kernels for 0%

profile of v6, /device:TPU:198, one launch (start us, length us, event | category | flops | bytes accessed | tf_op | source)
XLA Modules:
  0.0 121.5 jit_solution(11944139164210829098)
XLA Ops:
  0.7 1.5 %dynamic-slice_reduce_fusion = (s32[16]{0:T(128)S(1)}, s32[16]{0:T(128)}) fusion(s32[1,256,2]{1,2,0:T(2,128)} %param.15, s32[]{:T(128)S(6)} %select_n.86, s32[1,256,2]{1,2,0:T(2,128)} %param.12), kind=kLoop, calls=%fused_computation.94 | loop fusion | flops 32 | bytes 388 | tf_op jit(solution)/shard_map/reduce_sum | solution.py:23
  3.9 1.7 %select_reduce_fusion.1 = (f32[16]{0:T(128)}, bf16[16,8]{0,1:T(8,128)(2,1)S(1)}) fusion(s32[16]{0:T(128)S(1)} %broadcast_minimum_fusion.1, bf16[1,3072,8]{1,2,0:T(8,128)(2,1)} %param.18, bf16[1,16,3072]{2,1,0:T(8,128)(2,1)} %param.13, f32[16]{0:T(128)S(1)} %add_rsqrt_fusion, f32[3072]{0:T(1024)S(1)} %bitcast.185), kind=kOutput, calls=%fused_computation.73 | convolution fusion | flops 983664 | bytes 160192 | tf_op jit(solution)/shard_map/dot_general | solution.py:17
  5.7 1.9 %convolution_convert_fusion = bf16[256,3072]{1,0:T(8,128)(2,1)S(1)} fusion(bf16[1,512,3072]{2,1,0:T(8,128)(2,1)S(1)} %copy-done, bf16[1,256,512]{2,1,0:T(8,128)(2,1)} %param.11), kind=kOutput, calls=%fused_computation | convolution fusion | flops 806092800 | bytes 4980736 | tf_op jit(solution)/shard_map/dot_general | solution.py:57
  9.9 1.9 %collective-permute-start = (bf16[8,16,3200]{2,1,0:T(8,128)(2,1)}, bf16[8,16,3200]{2,1,0:T(8,128)(2,1)}, u32[]{:S(2)}, u32[]{:S(2)}) collective-permute-start(bf16[8,16,3200]{2,1,0:T(8,128)(2,1)} %pad_maximum_fusion), channel_id=1, source_target_pairs={{0,1},{1,0},{2,3},{3,2},{4,5},{5,4},{6,7},{7,6},{8,9},{9,8},{10,11... | collective-permute-start | bytes 2457608 | tf_op jit(solution)/shard_map/ppermute | solution.py:61
  12.8 7.1 %all-to-all-start = ((bf16[8,16,3072]{2,1,0:T(8,128)(2,1)}), bf16[8,16,3072]{2,1,0:T(8,128)(2,1)}, u32[]{:S(2)}, u32[]{:S(2)}) async-start(bf16[8,16,3072]{2,1,0:T(8,128)(2,1)} %broadcast_in_dim.20), calls=%async_computation | async-start | bytes 1572864 | tf_op jit(solution)/shard_map/all_to_all | solution.py:50
  21.2 1.3 %fusion.44 = f32[16]{0:T(128)} fusion(s32[1,256,2]{1,2,0:T(2,128)} %param.15, s32[]{:T(128)S(6)} %select_n.86), kind=kLoop, calls=%fused_computation.88 | loop fusion | flops 80 | bytes 196 | tf_op jit(solution)/shard_map/reduce_sum | solution.py:22
  22.6 1.4 %fusion.43 = f32[16]{0:T(128)} fusion(s32[1,256,2]{1,2,0:T(2,128)} %param.12, s32[]{:T(128)S(6)} %select_n.86), kind=kLoop, calls=%fused_computation.87 | loop fusion | flops 80 | bytes 196 | tf_op jit(solution)/shard_map/reduce_sum | solution.py:22
  23.9 1.2 %fusion.41 = f32[256]{0:T(256)} fusion(s32[1,256,2]{1,2,0:T(2,128)} %param.15), kind=kLoop, calls=%fused_computation.78 | loop fusion | flops 1280 | bytes 3072 | tf_op jit(solution)/shard_map/reduce_sum | solution.py:22
  25.8 2.2 %fusion.17 = (f32[16]{0:T(128)}, f32[16,3072]{1,0:T(8,128)}) fusion(bf16[1,16,3072]{2,1,0:T(8,128)(2,1)S(1)} %copy-done.2, f32[16]{0:T(128)} %copy-done.16, f32[3072]{0:T(1024)S(1)} %bitcast.186, bf16[1,3072,8]{1,2,0:T(8,128)(2,1)S(1)} %copy-done.7, s32[16]{0:T(128)} %copy-done.17, f32[3072]{0:T(1024)S(1)} %bitcast.188), kind=kOutput, calls=%fused_computation.35 | convolution fusion | flops 1081456 | bytes 368832 | tf_op jit(solution)/shard_map/dot_general | solution.py:122
  28.0 1.7 %broadcast_select_fusion = (bf16[8,1,16,512]{3,2,0,1:T(8,128)(2,1)}, bf16[8,1,16,512]{3,2,0,1:T(8,128)(2,1)}) fusion(pred[]{:T(512)S(6)} %eq.70, bf16[8,2,16,512]{3,2,1,0:T(8,128)(2,1)} %bitcast.181), kind=kLoop, calls=%fused_computation.52 | loop fusion | flops 131072 | bytes 524289 | tf_op jit(solution)/shard_map/jit(_where)/select_n | solution.py:71
  29.7 14.1 %all-to-all-done = bf16[8,16,3072]{2,1,0:T(8,128)(2,1)} async-done(((bf16[8,16,3072]{2,1,0:T(8,128)(2,1)}), bf16[8,16,3072]{2,1,0:T(8,128)(2,1)}, u32[]{:S(2)}, u32[]{:S(2)}) %all-to-all-start) | async-done | bytes 786464 | tf_op jit(solution)/shard_map/all_to_all | solution.py:50
  43.8 2.1 %collective-permute-start.1 = (bf16[128,3072]{1,0:T(8,128)(2,1)}, bf16[128,3072]{1,0:T(8,128)(2,1)}, u32[]{:S(2)}, u32[]{:S(2)}) collective-permute-start(bf16[128,3072]{1,0:T(8,128)(2,1)} %bitcast.17), channel_id=1, source_target_pairs={{0,1},{1,0},{2,3},{3,2},{4,5},{5,4},{6,7},{7,6},{8,9},{9,8},{10,11... | collective-permute-start | bytes 2359304 | tf_op jit(solution)/shard_map/ppermute | solution.py:51
  45.9 2.9 %fusion.6 = bf16[8,16,3072]{2,1,0:T(8,128)(2,1)} fusion(bf16[8,16,3200]{2,1,0:T(8,128)(2,1)} %collective-permute-done, pred[]{:T(512)S(6)} %eq.70, bf16[8,2,16,3072]{3,2,1,0:T(8,128)(2,1)} %bitcast.176), kind=kLoop, calls=%fused_computation.9 | loop fusion | flops 1966080 | bytes 3145729 | tf_op jit(solution)/shard_map/convert_element_type | solution.py:66
  48.8 1.3 %slice_bitcast_fusion.6 = bf16[16,8]{1,0:T(8,128)(2,1)} fusion(bf16[8,16,3200]{2,1,0:T(8,128)(2,1)} %collective-permute-done), kind=kLoop, calls=%fused_computation.72 | loop fusion | bytes 512 | tf_op jit(solution)/shard_map/broadcast_in_dim | solution.py:92
  50.1 2.4 %fusion.9 = (f32[128]{0:T(128)S(1)}, f32[128,512]{1,0:T(8,128)S(1)}) fusion(bf16[8,1,16,512]{3,2,0,1:T(8,128)(2,1)S(1)} %copy-done.4, bf16[128,3072]{1,0:T(8,128)(2,1)} %bitcast.17, bf16[1,512,3072]{2,1,0:T(8,128)(2,1)S(1)} %copy-done), kind=kOutput, calls=%fused_computation.23 | convolution fusion | flops 402849664 | bytes 4325888 | tf_op jit(solution)/shard_map/dot_general | solution.py:74
  52.5 3.0 %fusion.8 = (f32[128]{0:T(128)S(1)}, f32[128,512]{1,0:T(8,128)}) fusion(bf16[8,1,16,512]{3,2,0,1:T(8,128)(2,1)} %get-tuple-element.9, bf16[128,3072]{1,0:T(8,128)(2,1)} %collective-permute-done.1, bf16[1,512,3072]{2,1,0:T(8,128)(2,1)S(1)} %copy-done), kind=kOutput, calls=%fused_computation.21 | convolution fusion | flops 402849664 | bytes 4325888 | tf_op jit(solution)/shard_map/dot_general | solution.py:74
  57.7 1.3 %slice_bitcast_fusion.7 = (bf16[8,16,1]{1,0,2:T(8,128)(2,1)}, bf16[8,16,1]{1,0,2:T(8,128)(2,1)}) fusion(bf16[8,2,16]{2,0,1:T(8,128)(2,1)} %subtract_convert_fusion), kind=kLoop, calls=%fused_computation.79 | loop fusion | bytes 1024 | tf_op jit(solution)/shard_map/concatenate | solution.py:98
  59.0 1.4 %copy.42 = bf16[8,16,1]{2,1,0:T(8,128)(2,1)} copy(bf16[8,16,1]{1,0,2:T(8,128)(2,1)} %get-tuple-element.12) | data formatting | bytes 512 | tf_op jit(solution)/shard_map/concatenate | solution.py:98
  60.4 1.4 %copy.43 = bf16[8,16,1]{2,1,0:T(8,128)(2,1)} copy(bf16[8,16,1]{1,0,2:T(8,128)(2,1)} %get-tuple-element.13) | data formatting | bytes 512 | tf_op jit(solution)/shard_map/concatenate | solution.py:98
  61.8 1.4 %copy.44 = bf16[8,16,1]{2,1,0:T(8,128)(2,1)} copy(bf16[8,16,1]{1,0,2:T(8,128)(2,1)} %get-tuple-element.11) | data formatting | bytes 512 | tf_op jit(solution)/shard_map/concatenate | solution.py:98
  63.2 1.3 %broadcast_in_dim.23 = bf16[8,16,8]{2,1,0:T(8,128)(2,1)} broadcast(bf16[16,8]{1,0:T(8,128)(2,1)} %slice_bitcast_fusion.6), dimensions={1,2} | broadcast | bytes 2304 | tf_op jit(solution)/shard_map/broadcast_in_dim | solution.py:92
  65.7 2.1 %concatenate.21 = bf16[8,16,3200]{2,1,0:T(8,128)(2,1)} concatenate(bf16[8,16,3072]{2,1,0:T(8,128)(2,1)} %fusion.6, bf16[8,16,1]{2,1,0:T(8,128)(2,1)S(1)} %copy.41, bf16[8,16,1]{2,1,0:T(8,128)(2,1)} %copy.42, bf16[8,16,1]{2,1,0:T(8,128)(2,1)} %copy.43, bf16[8,16,1]{2,1,0:T(8,128)(2,1)} %copy.44, bf16[8,16,8]{2,1,0:T(8,128)(2,1)} %broadcast_in_dim.21, ...), dimensions={2} | concatenate | bytes 1638400 | tf_op jit(solution)/shard_map/concatenate | solution.py:98
  67.8 4.4 %all-to-all-start.1 = ((bf16[8,16,3200]{2,1,0:T(8,128)(2,1)}), bf16[8,16,3200]{2,1,0:T(8,128)(2,1)}, u32[]{:S(2)}, u32[]{:S(2)}) async-start(bf16[8,16,3200]{2,1,0:T(8,128)(2,1)} %concatenate.21), calls=%async_computation.1 | async-start | bytes 1638400 | tf_op jit(solution)/shard_map/all_to_all | solution.py:99
  72.2 1.1 broadcast_multiply_fusion
  76.4 1.2 %fusion.48 = f32[16]{0:T(128)} fusion(f32[16]{0:T(128)} %fusion.44, f32[16]{0:T(128)} %get-tuple-element.23, f32[16,8]{0,1:T(8,128)} %convert_element_type.165, f32[16]{0:T(128)} %copy-done.15), kind=kLoop, calls=%fused_computation.99 | loop fusion | flops 160 | bytes 320 | tf_op jit(solution)/shard_map/mul | solution.py:127
  79.5 17.4 %all-to-all-done.1 = bf16[8,16,3200]{2,1,0:T(8,128)(2,1)} async-done(((bf16[8,16,3200]{2,1,0:T(8,128)(2,1)}), bf16[8,16,3200]{2,1,0:T(8,128)(2,1)}, u32[]{:S(2)}, u32[]{:S(2)}) %all-to-all-start.1) | async-done | bytes 819232 | tf_op jit(solution)/shard_map/all_to_all | solution.py:99
  99.4 2.0 %collective-permute-start.3 = (f32[16]{0:T(128)S(1)}, f32[16]{0:T(128)S(1)}, u32[]{:S(2)}, u32[]{:S(2)}) collective-permute-start(f32[16]{0:T(128)S(1)} %broadcast_select_fusion.2), channel_id=1, source_target_pairs={{0,1},{1,0},{2,3},{3,2},{4,5},{5,4},{6,7},{7,6},{8,9},{9,8},{10,11... | collective-permute-start | bytes 200 | tf_op jit(solution)/shard_map/ppermute | solution.py:106
  101.4 1.3 %convert_reduce_fusion = f32[16,3072]{1,0:T(8,128)S(1)} fusion(bf16[8,16,3200]{2,1,0:T(8,128)(2,1)} %all-to-all-done.1), kind=kLoop, calls=%fused_computation.10 | loop fusion | flops 737280 | bytes 983040 | tf_op jit(solution)/shard_map/reduce_sum | solution.py:100
  103.6 5.4 %collective-permute-start.2 = (bf16[16,3072]{1,0:T(8,128)(2,1)S(1)}, bf16[16,3072]{1,0:T(8,128)(2,1)S(1)}, u32[]{:S(2)}, u32[]{:S(2)}) collective-permute-start(bf16[16,3072]{1,0:T(8,128)(2,1)S(1)} %fusion.27), channel_id=1, source_target_pairs={{0,16},{16,32},{32,48},{48,64},{64,80},{80,96},{96,112},{112,128},... | collective-permute-start | bytes 294920 | tf_op jit(solution)/shard_map/ppermute | solution.py:10
  110.2 1.9 %collective-permute-start.4 = (bf16[16,3072]{1,0:T(8,128)(2,1)S(1)}, bf16[16,3072]{1,0:T(8,128)(2,1)S(1)}, u32[]{:S(2)}, u32[]{:S(2)}) collective-permute-start(bf16[16,3072]{1,0:T(8,128)(2,1)S(1)} %fusion.22), channel_id=1, source_target_pairs={{16,0},{32,16},{48,32},{64,48},{80,64},{96,80},{112,96},{128,112},... | collective-permute-start | bytes 294920 | tf_op jit(solution)/shard_map/ppermute | solution.py:10
  112.1 1.8 %multiply_convert_fusion = bf16[1,256,512]{2,1,0:T(8,128)(2,1)} fusion(f32[1,256,512]{2,1,0:T(8,128)} %bitcast.177, f32[256]{0:T(256)S(1)} %bitcast.189), kind=kLoop, calls=%fused_computation.19 | loop fusion | flops 262144 | bytes 787456 | tf_op jit(solution)/shard_map/convert_element_type | solution.py:117
  113.9 6.3 %collective-permute-done.4 = bf16[16,3072]{1,0:T(8,128)(2,1)S(1)} collective-permute-done((bf16[16,3072]{1,0:T(8,128)(2,1)S(1)}, bf16[16,3072]{1,0:T(8,128)(2,1)S(1)}, u32[]{:S(2)}, u32[]{:S(2)}) %collective-permute-start.4) | collective-permute-done | bytes 98336 | tf_op jit(solution)/shard_map/ppermute | solution.py:10
  (86 shorter events, 21.1 us)
Async XLA Ops:
  0.6 5.1 %copy-start = (bf16[1,512,3072]{2,1,0:T(8,128)(2,1)S(1)}, bf16[1,512,3072]{2,1,0:T(8,128)(2,1)}, u32[]{:S(2)}) copy-start(bf16[1,512,3072]{2,1,0:T(8,128)(2,1)} %param.19) | copy-start | bytes 9437188
  2.1 3.5 %copy-start.17 = (s32[16]{0:T(128)}, s32[16]{0:T(128)S(1)}, u32[]{:S(2)}) copy-start(s32[16]{0:T(128)S(1)} %broadcast_minimum_fusion.1) | copy-start | bytes 196
  3.2 2.4 %copy-start.15 = (f32[16]{0:T(128)}, f32[16]{0:T(128)S(1)}, u32[]{:S(2)}) copy-start(f32[16]{0:T(128)S(1)} %fusion.23) | copy-start | bytes 196
  3.2 4.5 %copy-start.16 = (f32[16]{0:T(128)}, f32[16]{0:T(128)S(1)}, u32[]{:S(2)}) copy-start(f32[16]{0:T(128)S(1)} %add_rsqrt_fusion) | copy-start | bytes 196
  3.9 21.9 %copy-start.8 = (f32[1,3072]{1,0:T(1,128)}, f32[1,3072]{1,0:T(1,128)S(1)}, u32[]{:S(2)}) copy-start(f32[1,3072]{1,0:T(1,128)S(1)} %mul.201) | copy-start | bytes 36868
  5.7 2.0 %copy-start.10 = (bf16[16,8]{1,0:T(8,128)(2,1)}, bf16[16,8]{1,0:T(8,128)(2,1)S(1)}, u32[]{:S(2)}) copy-start(bf16[16,8]{1,0:T(8,128)(2,1)S(1)} %copy.59) | copy-start | bytes 772
  7.7 1.2 copy-start.1
  7.7 4.1 %copy-start.6 = (bf16[1,16,3072]{2,1,0:T(8,128)(2,1)S(1)}, bf16[1,16,3072]{2,1,0:T(8,128)(2,1)}, u32[]{:S(2)}) copy-start(bf16[1,16,3072]{2,1,0:T(8,128)(2,1)} %param.16) | copy-start | bytes 294916
  8.8 11.1 %copy-start.13 = (s32[1,256,2]{1,2,0:T(2,128)S(1)}, s32[1,256,2]{1,2,0:T(2,128)}, u32[]{:S(2)}) copy-start(s32[1,256,2]{1,2,0:T(2,128)} %param.15) | copy-start | bytes 6148
  8.8 11.7 %copy-start.7 = (bf16[1,3072,8]{1,2,0:T(8,128)(2,1)S(1)}, bf16[1,3072,8]{1,2,0:T(8,128)(2,1)}, u32[]{:S(2)}) copy-start(bf16[1,3072,8]{1,2,0:T(8,128)(2,1)} %param.18) | copy-start | bytes 147460
  8.8 16.3 %copy-start.5 = (bf16[1,16,3072]{2,1,0:T(8,128)(2,1)S(1)}, bf16[1,16,3072]{2,1,0:T(8,128)(2,1)}, u32[]{:S(2)}) copy-start(bf16[1,16,3072]{2,1,0:T(8,128)(2,1)} %param.10) | copy-start | bytes 294916
  8.8 17.0 %copy-start.2 = (bf16[1,16,3072]{2,1,0:T(8,128)(2,1)S(1)}, bf16[1,16,3072]{2,1,0:T(8,128)(2,1)}, u32[]{:S(2)}) copy-start(bf16[1,16,3072]{2,1,0:T(8,128)(2,1)} %param.13) | copy-start | bytes 294916
  9.9 36.0 %collective-permute-start = (bf16[8,16,3200]{2,1,0:T(8,128)(2,1)}, bf16[8,16,3200]{2,1,0:T(8,128)(2,1)}, u32[]{:S(2)}, u32[]{:S(2)}) collective-permute-start(bf16[8,16,3200]{2,1,0:T(8,128)(2,1)} %pad_maximum_fusion), channel_id=1, source_target_pairs={{0,1},{1,0},{2,3},{3,2},{4,5},{5,4},{6,7},{7,6},{8,9},{9,8},{10,11... | collective-permute-start | bytes 2457608 | tf_op jit(solution)/shard_map/ppermute | solution.py:61
  12.8 31.0 %all-to-all-start = ((bf16[8,16,3072]{2,1,0:T(8,128)(2,1)}), bf16[8,16,3072]{2,1,0:T(8,128)(2,1)}, u32[]{:S(2)}, u32[]{:S(2)}) async-start(bf16[8,16,3072]{2,1,0:T(8,128)(2,1)} %broadcast_in_dim.20), calls=%async_computation | async-start | bytes 1572864 | tf_op jit(solution)/shard_map/all_to_all | solution.py:50
  43.8 6.2 %copy-start.4 = (bf16[8,1,16,512]{3,2,0,1:T(8,128)(2,1)S(1)}, bf16[8,1,16,512]{3,2,0,1:T(8,128)(2,1)}, u32[]{:S(2)}) copy-start(bf16[8,1,16,512]{3,2,0,1:T(8,128)(2,1)} %get-tuple-element.10) | copy-start | bytes 393220
  43.8 8.7 %collective-permute-start.1 = (bf16[128,3072]{1,0:T(8,128)(2,1)}, bf16[128,3072]{1,0:T(8,128)(2,1)}, u32[]{:S(2)}, u32[]{:S(2)}) collective-permute-start(bf16[128,3072]{1,0:T(8,128)(2,1)} %bitcast.17), channel_id=1, source_target_pairs={{0,1},{1,0},{2,3},{3,2},{4,5},{5,4},{6,7},{7,6},{8,9},{9,8},{10,11... | collective-permute-start | bytes 2359304 | tf_op jit(solution)/shard_map/ppermute | solution.py:51
  52.5 12.0 %copy-start.11 = (bf16[16,8]{1,0:T(8,128)(2,1)S(1)}, bf16[16,8]{1,0:T(8,128)(2,1)}, u32[]{:S(2)}) copy-start(bf16[16,8]{1,0:T(8,128)(2,1)} %copy-done.10) | copy-start | bytes 772
  52.5 22.0 %copy-start.9 = (f32[1,3072]{1,0:T(1,128)S(1)}, f32[1,3072]{1,0:T(1,128)}, u32[]{:S(2)}) copy-start(f32[1,3072]{1,0:T(1,128)} %copy-done.8) | copy-start | bytes 36868
  67.8 30.1 %copy-start.12 = (s32[8,2,16]{2,0,1:T(8,128)S(1)}, s32[8,2,16]{2,0,1:T(8,128)}, u32[]{:S(2)}) copy-start(s32[8,2,16]{2,0,1:T(8,128)} %copy.48) | copy-start | bytes 3076
  67.8 41.2 %copy-start.14 = (f32[256]{0:T(256)S(1)}, f32[256]{0:T(256)}, u32[]{:S(2)}) copy-start(f32[256]{0:T(256)} %fusion.41) | copy-start | bytes 3076
  67.8 29.1 %all-to-all-start.1 = ((bf16[8,16,3200]{2,1,0:T(8,128)(2,1)}), bf16[8,16,3200]{2,1,0:T(8,128)(2,1)}, u32[]{:S(2)}, u32[]{:S(2)}) async-start(bf16[8,16,3200]{2,1,0:T(8,128)(2,1)} %concatenate.21), calls=%async_computation.1 | async-start | bytes 1638400 | tf_op jit(solution)/shard_map/all_to_all | solution.py:99
  78.7 30.4 %copy-start.3 = (f32[16,3072]{1,0:T(8,128)S(1)}, f32[16,3072]{1,0:T(8,128)}, u32[]{:S(2)}) copy-start(f32[16,3072]{1,0:T(8,128)} %get-tuple-element.22) | copy-start | bytes 589828
  99.4 9.7 %collective-permute-start.3 = (f32[16]{0:T(128)S(1)}, f32[16]{0:T(128)S(1)}, u32[]{:S(2)}, u32[]{:S(2)}) collective-permute-start(f32[16]{0:T(128)S(1)} %broadcast_select_fusion.2), channel_id=1, source_target_pairs={{0,1},{1,0},{2,3},{3,2},{4,5},{5,4},{6,7},{7,6},{8,9},{9,8},{10,11... | collective-permute-start | bytes 200 | tf_op jit(solution)/shard_map/ppermute | solution.py:106
  103.6 10.3 %collective-permute-start.2 = (bf16[16,3072]{1,0:T(8,128)(2,1)S(1)}, bf16[16,3072]{1,0:T(8,128)(2,1)S(1)}, u32[]{:S(2)}, u32[]{:S(2)}) collective-permute-start(bf16[16,3072]{1,0:T(8,128)(2,1)S(1)} %fusion.27), channel_id=1, source_target_pairs={{0,16},{16,32},{32,48},{48,64},{64,80},{80,96},{96,112},{112,128},... | collective-permute-start | bytes 294920 | tf_op jit(solution)/shard_map/ppermute | solution.py:10
  110.2 10.1 %collective-permute-start.4 = (bf16[16,3072]{1,0:T(8,128)(2,1)S(1)}, bf16[16,3072]{1,0:T(8,128)(2,1)S(1)}, u32[]{:S(2)}, u32[]{:S(2)}) collective-permute-start(bf16[16,3072]{1,0:T(8,128)(2,1)S(1)} %fusion.22), channel_id=1, source_target_pairs={{16,0},{32,16},{48,32},{64,48},{80,64},{96,80},{112,96},{128,112},... | collective-permute-start | bytes 294920 | tf_op jit(solution)/shard_map/ppermute | solution.py:10

commit v7 on v4

--- a/solution.py
+++ b/solution.py
@@ -55,8 +55,8 @@
     given = lax.ppermute(give_z, "etc", [(0, 1), (1, 0)])
     pair_z = (mine_z.astype(jnp.float32) + given.astype(jnp.float32)).astype(jnp.bfloat16)
     pair_z, same_core = lax.optimization_barrier((pair_z, same_core))
-    got = lax.all_to_all(pair_z.reshape(chips * own_rows, width), "ety", 0, 0, tiled=True)
-    z_sum = jnp.sum(got.reshape(chips, own_rows, width).astype(jnp.float32), axis=0)
+    cut = width // 2
+    got_a = lax.all_to_all(pair_z[..., :cut].reshape(chips * own_rows, cut), "ety", 0, 0, tiled=True)
 
     other_core = lax.ppermute(same_core, "etc", [(0, 1), (1, 0)])
     full = jnp.where(
@@ -73,9 +73,30 @@
     )
     dact = (coef_b[:, None] * back_up).astype(jnp.bfloat16)
     dprob_part = jnp.sum(act_bwd.astype(jnp.float32) * back_up, axis=1)
-    dprob_part, z_sum = lax.optimization_barrier((dprob_part, z_sum))
-    dprob_got = lax.all_to_all(dprob_part.reshape(groups, own_rows), ("ety", "etc"), 0, 0, tiled=True)
-    dprob_mine = jnp.sum(dprob_got, axis=0)
+    halves = dprob_part.reshape(chips, 2, own_rows)
+    keep = jnp.where(core == 0, halves[:, 0], halves[:, 1])
+    give = jnp.where(core == 0, halves[:, 1], halves[:, 0])
+    pair_d = keep + lax.ppermute(give, "etc", [(0, 1), (1, 0)])
+    pair_hi = pair_d.astype(jnp.bfloat16)
+    pair_lo = (pair_d - pair_hi.astype(jnp.float32)).astype(jnp.bfloat16)
+    extra = jnp.concatenate(
+        [pair_hi[..., None], pair_lo[..., None], jnp.zeros((chips, own_rows, pad - 2), jnp.bfloat16)],
+        axis=-1,
+    )
+    sent_b = jnp.concatenate([pair_z[..., cut:], extra], axis=-1)
+    got_b = lax.all_to_all(
+        sent_b.reshape(chips * own_rows, width - cut + pad), "ety", 0, 0, tiled=True
+    ).reshape(chips, own_rows, -1)
+    got_a = got_a.reshape(chips, own_rows, cut)
+    z_sum = jnp.concatenate(
+        [
+            jnp.sum(got_a.astype(jnp.float32), axis=0),
+            jnp.sum(got_b[..., : width - cut].astype(jnp.float32), axis=0),
+        ],
+        axis=-1,
+    )
+    tail = got_b[..., width - cut :].astype(jnp.float32)
+    dprob_mine = jnp.sum(tail[..., 0] + tail[..., 1], axis=0)
 
     ids_f_own = lax.dynamic_slice_in_dim(ids_fwd, first_row, own_rows, 0)
     _, _, _, coef_f = routing(logit_f, ids_f_own, experts)

time: 96.5 us -> 112 us (1.16)
  local copies, waits for them, and re-layouts: 5.53 us -> 12.7 us
  other arithmetic: 14.9 us -> 20.4 us
  starting transfers between devices: 26.8 us -> 31.8 us
  waiting for transfers between devices: 40.3 us -> 35.8 us
  matrix products: 7.3 us -> 9.05 us
    all_to_all x2, waiting for transfers between devices: 17.8 us -> 13.5 us  [the longest x1 13.5 us: shards(): lax.all_to_all(sent_b.reshape(chips * own_rows, width - cut + pad), 'ety'...]
    all_to_all x2, starting transfers between devices: 7.7 us -> 11 us  [the longest x1 6.94 us: shards(): lax.all_to_all(sent_b.reshape(chips * own_rows, width - cut + pad), 'ety'...]
    concatenate x0 -> x3, local copies, waits for them, and re-layouts: none -> 3.15 us  [shards(): sent_b = jnp.concatenate([pair_z[..., cut:], extra], axis=-1)]
    ppermute x0 -> x1, starting transfers between devices: none -> 2.4 us  [shards(): pair_d = keep + lax.ppermute(give, 'etc', [(0, 1), (1, 0)])]
    slice x0 -> x1, local copies, waits for them, and re-layouts: none -> 1.93 us  [shards(): pair_z[..., :cut].reshape(chips * own_rows, cut)]
    mul x1, other arithmetic: 0.01 us -> 1.3 us  [shards(): layer_out = (wide_f + coef_f[:, None] * z_sum).astype(jnp.bfloat16)]
    dot_general x2, matrix products: 1.89 us -> 3.1 us  [norm_logits(): jnp.dot(normed, w_router, preferred_element_type=jnp.float32)]
    reduce_sum x2 -> x3, other arithmetic: 1.28 us -> 2.31 us  [the longest x1 1.07 us: shards(): jnp.sum(got_b[..., :width - cut].astype(jnp.float32), axis=0)]
  transfers between devices with their start and end apart: 7 -> 8, of which waited for: 5 -> 4; matrix products, arithmetic and copies ran while one was open for 17% -> 27% of each run, Pallas kernels for 0% -> 0%
where the time goes in v7:
time: 112 us; the launch traced here: 111 us
  waiting for transfers between devices  35.8 us (32%)
  starting transfers between devices  31.8 us (28%)
  other arithmetic  20.4 us (18%)
  local copies, waits for them, and re-layouts  12.7 us (11%)
  matrix products  9.05 us (8%)
    all_to_all x1, waiting for transfers between devices, shards(): lax.all_to_all(sent_b.reshape(chips * own_rows, width - cut + pad), 'ety'...  13.5 us
    all_to_all x1, waiting for transfers between devices, shards(): lax.all_to_all(tiled, 'ety', 0, 0, tiled=True)  13.3 us
    ppermute x2, waiting for transfers between devices, from_behind(): lax.ppermute(value, axis, [(source, source + steps) for source in range(f...  7.89 us
    ppermute x2, starting transfers between devices, from_behind(): lax.ppermute(value, axis, [(source, source + steps) for source in range(f...  7.33 us
    all_to_all x1, starting transfers between devices, shards(): lax.all_to_all(tiled, 'ety', 0, 0, tiled=True)  7.1 us
    all_to_all x1, starting transfers between devices, shards(): lax.all_to_all(sent_b.reshape(chips * own_rows, width - cut + pad), 'ety'...  6.94 us
    unnamed x36, local copies, waits for them, and re-layouts  4.61 us
    all_to_all x1, starting transfers between devices, shards(): lax.all_to_all(pair_z[..., :cut].reshape(chips * own_rows, cut), 'ety', 0...  4.09 us
  transfers between devices with their start and end apart: 8, of which 4 were waited for; matrix products, arithmetic and copies ran while one was open for 27% of the time, Pallas kernels for 0%

profile of v7, /device:TPU:198, one launch (start us, length us, event | category | flops | bytes accessed | tf_op | source)
XLA Modules:
  0.0 110.7 jit_solution(4609861456581743432)
XLA Ops:
  0.7 1.2 %fusion.25 = f32[16]{0:T(128)S(1)} fusion(bf16[1,16,3072]{2,1,0:T(8,128)(2,1)} %param.13), kind=kLoop, calls=%fused_computation.42 | loop fusion | flops 147440 | bytes 98368 | tf_op jit(solution)/shard_map/reduce_sum | solution.py:15
  3.4 1.7 %select_reduce_fusion.1 = (f32[16]{0:T(128)}, bf16[16,8]{0,1:T(8,128)(2,1)S(1)}) fusion(s32[16]{0:T(128)S(1)} %broadcast_minimum_fusion.1, bf16[1,3072,8]{1,2,0:T(8,128)(2,1)} %param.18, bf16[1,16,3072]{2,1,0:T(8,128)(2,1)} %param.13, f32[16]{0:T(128)S(1)} %add_rsqrt_fusion, f32[3072]{0:T(1024)S(1)} %bitcast.149), kind=kOutput, calls=%fused_computation.65 | convolution fusion | flops 983664 | bytes 160192 | tf_op jit(solution)/shard_map/dot_general | solution.py:17
  5.2 0.9 fusion.32
  6.1 1.0 broadcast_in_dim.10
  7.1 7.1 %all-to-all-start = ((bf16[8,16,3200]{2,1,0:T(8,128)(2,1)}), bf16[8,16,3200]{2,1,0:T(8,128)(2,1)}, u32[]{:S(2)}, u32[]{:S(2)}) async-start(bf16[8,16,3200]{2,1,0:T(8,128)(2,1)} %broadcast_in_dim.10), calls=%async_computation | async-start | bytes 1638400 | tf_op jit(solution)/shard_map/all_to_all | solution.py:50
  14.2 1.0 convolution_convert_fusion
  15.2 1.1 %copy-done.1 = bf16[256,3072]{1,0:T(8,128)(2,1)} copy-done((bf16[256,3072]{1,0:T(8,128)(2,1)}, bf16[256,3072]{1,0:T(8,128)(2,1)S(1)}, u32[]{:S(2)}) %copy-start.1) | copy-done | bytes 1572888
  16.3 1.0 fusion.8
  17.3 2.0 %collective-permute-start = (bf16[8,16,3072]{2,1,0:T(8,128)(2,1)}, bf16[8,16,3072]{2,1,0:T(8,128)(2,1)}, u32[]{:S(2)}, u32[]{:S(2)}) collective-permute-start(bf16[8,16,3072]{2,1,0:T(8,128)(2,1)} %fusion.8), channel_id=1, source_target_pairs={{0,1},{1,0},{2,3},{3,2},{4,5},{5,4},{6,7},{7,6},{8,9},{9,8},{10,11... | collective-permute-start | bytes 2359304 | tf_op jit(solution)/shard_map/ppermute | solution.py:55
  20.8 1.2 %collective-permute-done = bf16[8,16,3072]{2,1,0:T(8,128)(2,1)} collective-permute-done((bf16[8,16,3072]{2,1,0:T(8,128)(2,1)}, bf16[8,16,3072]{2,1,0:T(8,128)(2,1)}, u32[]{:S(2)}, u32[]{:S(2)}) %collective-permute-start) | collective-permute-done | bytes 786464 | tf_op jit(solution)/shard_map/ppermute | solution.py:55
  21.9 2.9 %fusion.6 = bf16[8,16,3072]{2,1,0:T(8,128)(2,1)} fusion(bf16[8,16,3072]{2,1,0:T(8,128)(2,1)} %collective-permute-done, pred[]{:T(512)S(6)} %eq.65, bf16[8,2,16,3072]{3,2,1,0:T(8,128)(2,1)} %bitcast.142), kind=kLoop, calls=%fused_computation.10 | loop fusion | flops 1966080 | bytes 3145729 | tf_op jit(solution)/shard_map/convert_element_type | solution.py:56
  24.8 13.3 %all-to-all-done = bf16[8,16,3200]{2,1,0:T(8,128)(2,1)} async-done(((bf16[8,16,3200]{2,1,0:T(8,128)(2,1)}), bf16[8,16,3200]{2,1,0:T(8,128)(2,1)}, u32[]{:S(2)}, u32[]{:S(2)}) %all-to-all-start) | async-done | bytes 819232 | tf_op jit(solution)/shard_map/all_to_all | solution.py:50
  38.1 1.9 %collective-permute-start.1 = (bf16[8,1,16,3200]{3,2,1,0:T(8,128)(2,1)}, bf16[8,1,16,3200]{3,2,1,0:T(8,128)(2,1)}, u32[]{:S(2)}, u32[]{:S(2)}) collective-permute-start(bf16[8,1,16,3200]{3,2,1,0:T(8,128)(2,1)} %bitcast.18), channel_id=1, source_target_pairs={{0,1},{1,0},{2,3},{3,2},{4,5},{5,4},{6,7},{7,6},{8,9},{9,8},{10,11... | collective-permute-start | bytes 2457608 | tf_op jit(solution)/shard_map/ppermute | solution.py:61
  40.0 1.4 %select_reduce_fusion.2 = (f32[16]{0:T(128)}, f32[16,8]{0,1:T(8,128)}) fusion(s32[16]{0:T(128)S(1)} %broadcast_minimum_fusion.2, bf16[1,3072,8]{1,2,0:T(8,128)(2,1)S(1)} %copy-done.11, bf16[1,16,3072]{2,1,0:T(8,128)(2,1)S(1)} %copy-done.3, f32[3072]{0:T(1024)S(1)} %bitcast.150, f32[16]{0:T(128)S(1)} %add_rsqrt_fusion.1), kind=kOutput, calls=%fused_computation.68 | convolution fusion | flops 983664 | bytes 160448 | tf_op jit(solution)/shard_map/dot_general | solution.py:17
  41.4 1.9 %fusion.59 = (bf16[8,16,1536]{2,1,0:T(8,128)(2,1)}, bf16[8,16,1536]{2,1,0:T(8,128)(2,1)S(1)}) fusion(bf16[8,16,3072]{2,1,0:T(8,128)(2,1)} %fusion.6), kind=kLoop, calls=%fused_computation.105 | loop fusion | bytes 1572864 | tf_op jit(solution)/shard_map/slice | solution.py:59
  43.4 4.1 %all-to-all-start.1 = ((bf16[8,16,1536]{2,1,0:T(8,128)(2,1)}), bf16[8,16,1536]{2,1,0:T(8,128)(2,1)}, u32[]{:S(2)}, u32[]{:S(2)}) async-start(bf16[8,16,1536]{2,1,0:T(8,128)(2,1)} %get-tuple-element.7), calls=%async_computation.1 | async-start | bytes 786432 | tf_op jit(solution)/shard_map/all_to_all | solution.py:59
  47.5 2.3 %maximum_select_fusion = bf16[8,2,16,3200]{3,2,1,0:T(8,128)(2,1)S(1)} fusion(bf16[8,1,16,3200]{3,2,1,0:T(8,128)(2,1)} %collective-permute-done.1, bf16[8,1,16,3200]{3,2,1,0:T(8,128)(2,1)} %bitcast.18, pred[]{:T(512)S(6)} %eq.65), kind=kLoop, calls=%fused_computation.7 | loop fusion | flops 2457600 | bytes 3276801 | tf_op jit(solution)/shard_map/jit(_where)/select_n | solution.py:62
  49.8 1.2 %copy-done.2 = bf16[8,2,16,3200]{3,2,1,0:T(8,128)(2,1)} copy-done((bf16[8,2,16,3200]{3,2,1,0:T(8,128)(2,1)}, bf16[8,2,16,3200]{3,2,1,0:T(8,128)(2,1)S(1)}, u32[]{:S(2)}) %copy-start.2) | copy-done | bytes 1638424
  51.6 0.9 copy.38
  53.2 3.8 %fusion.11 = (bf16[1,256,512]{2,1,0:T(8,128)(2,1)}, f32[256]{0:T(256)}) fusion(f32[256]{0:T(256)S(1)} %bitcast.157, bf16[1,256,512]{2,1,0:T(8,128)(2,1)} %param.14, bf16[1,512,3072]{2,1,0:T(8,128)(2,1)S(1)} %copy-done, bf16[256,3200]{1,0:T(8,128)(2,1)} %bitcast.144), kind=kOutput, calls=%fused_computation.23 | convolution fusion | flops 805961472 | bytes 5244928 | tf_op jit(solution)/shard_map/dot_general | solution.py:71
  57.8 2.4 %collective-permute-start.2 = (f32[8,16]{1,0:T(8,128)S(1)}, f32[8,16]{1,0:T(8,128)S(1)}, u32[]{:S(2)}, u32[]{:S(2)}) collective-permute-start(f32[8,16]{1,0:T(8,128)S(1)} %bitcast.154), channel_id=1, source_target_pairs={{0,1},{1,0},{2,3},{3,2},{4,5},{5,4},{6,7},{7,6},{8,9},{9,8},{10,11... | collective-permute-start | bytes 1544 | tf_op jit(solution)/shard_map/ppermute | solution.py:79
  60.2 1.3 %fusion.55 = f32[16]{0:T(128)} fusion(f32[16]{0:T(128)} %get-tuple-element.15, f32[16,8]{0,1:T(8,128)} %get-tuple-element.16, f32[16]{0:T(128)} %fusion.46), kind=kLoop, calls=%fused_computation.98 | loop fusion | flops 80 | bytes 256 | tf_op jit(solution)/shard_map/mul | solution.py:103
  64.9 1.7 %concatenate.26 = bf16[8,16,1664]{2,1,0:T(8,128)(2,1)} concatenate(bf16[8,16,1536]{2,1,0:T(8,128)(2,1)S(1)} %get-tuple-element.8, bf16[8,16,1]{2,1,0:T(8,128)(2,1)} %copy.34, bf16[8,16,1]{2,1,0:T(8,128)(2,1)} %copy.35, bf16[8,16,126]{2,1,0:T(8,128)(2,1)} %broadcast_in_dim.11), dimensions={2} | concatenate | bytes 851968 | tf_op jit(solution)/shard_map/concatenate | solution.py:86
  66.5 6.9 %all-to-all-start.2 = ((bf16[8,16,1664]{2,1,0:T(8,128)(2,1)}), bf16[8,16,1664]{2,1,0:T(8,128)(2,1)}, u32[]{:S(2)}, u32[]{:S(2)}) async-start(bf16[8,16,1664]{2,1,0:T(8,128)(2,1)} %concatenate.26), calls=%async_computation.2 | async-start | bytes 851968 | tf_op jit(solution)/shard_map/all_to_all | solution.py:87
  73.5 1.4 %slice_convert_fusion.1 = f32[3072,1]{0,1:T(1,128)} fusion(bf16[3072,8]{0,1:T(8,128)(2,1)} %bitcast.156), kind=kLoop, calls=%fused_computation.60 | loop fusion | flops 3072 | bytes 18432 | tf_op jit(solution)/shard_map/sub | solution.py:109
  74.9 1.1 convert_reduce_fusion.1
  76.0 13.5 %all-to-all-done.2 = bf16[8,16,1664]{2,1,0:T(8,128)(2,1)} async-done(((bf16[8,16,1664]{2,1,0:T(8,128)(2,1)}), bf16[8,16,1664]{2,1,0:T(8,128)(2,1)}, u32[]{:S(2)}, u32[]{:S(2)}) %all-to-all-start.2) | async-done | bytes 426016 | tf_op jit(solution)/shard_map/all_to_all | solution.py:87
  90.4 1.1 convert_reduce_fusion
  91.6 5.4 %collective-permute-start.3 = (bf16[16,3072]{1,0:T(8,128)(2,1)S(1)}, bf16[16,3072]{1,0:T(8,128)(2,1)S(1)}, u32[]{:S(2)}, u32[]{:S(2)}) collective-permute-start(bf16[16,3072]{1,0:T(8,128)(2,1)S(1)} %fusion.29), channel_id=1, source_target_pairs={{0,16},{16,32},{32,48},{48,64},{64,80},{80,96},{96,112},{112,128},... | collective-permute-start | bytes 294920 | tf_op jit(solution)/shard_map/ppermute | solution.py:10
  97.7 1.1 %fusion.20 = (f32[16]{0:T(128)S(1)}, f32[16,3072]{1,0:T(8,128)S(1)}) fusion(bf16[1,16,3072]{2,1,0:T(8,128)(2,1)S(1)} %copy-done.5, f32[16]{0:T(128)} %copy-done.14, f32[3072]{0:T(1024)S(1)} %bitcast.151, bf16[1,3072,8]{1,2,0:T(8,128)(2,1)} %param.18, s32[16]{0:T(128)} %copy-done.15, f32[3072]{0:T(1024)} %bitcast.152, f32[16]{0:T(128)S(1)} %fusion.52), kind=kOutput, calls=%fused_computation.37 | convolution fusion | flops 1130608 | bytes 368896 | tf_op jit(solution)/shard_map/dot_general | solution.py:109
  99.6 1.9 %collective-permute-start.4 = (bf16[16,3072]{1,0:T(8,128)(2,1)S(1)}, bf16[16,3072]{1,0:T(8,128)(2,1)S(1)}, u32[]{:S(2)}, u32[]{:S(2)}) collective-permute-start(bf16[16,3072]{1,0:T(8,128)(2,1)S(1)} %fusion.24), channel_id=1, source_target_pairs={{16,0},{32,16},{48,32},{64,48},{80,64},{96,80},{112,96},{128,112},... | collective-permute-start | bytes 294920 | tf_op jit(solution)/shard_map/ppermute | solution.py:10
  101.5 7.9 %collective-permute-done.4 = bf16[16,3072]{1,0:T(8,128)(2,1)S(1)} collective-permute-done((bf16[16,3072]{1,0:T(8,128)(2,1)S(1)}, bf16[16,3072]{1,0:T(8,128)(2,1)S(1)}, u32[]{:S(2)}, u32[]{:S(2)}) %collective-permute-start.4) | collective-permute-done | bytes 98336 | tf_op jit(solution)/shard_map/ppermute | solution.py:10
  (66 shorter events, 12.3 us)
Async XLA Ops:
  0.6 13.5 %copy-start = (bf16[1,512,3072]{2,1,0:T(8,128)(2,1)S(1)}, bf16[1,512,3072]{2,1,0:T(8,128)(2,1)}, u32[]{:S(2)}) copy-start(bf16[1,512,3072]{2,1,0:T(8,128)(2,1)} %param.19) | copy-start | bytes 9437188
  0.6 13.5 %copy-start.7 = (bf16[1,256,512]{2,1,0:T(8,128)(2,1)S(1)}, bf16[1,256,512]{2,1,0:T(8,128)(2,1)}, u32[]{:S(2)}) copy-start(bf16[1,256,512]{2,1,0:T(8,128)(2,1)} %param.11) | copy-start | bytes 786436
  1.9 13.3 %copy-start.14 = (f32[16]{0:T(128)}, f32[16]{0:T(128)S(1)}, u32[]{:S(2)}) copy-start(f32[16]{0:T(128)S(1)} %add_rsqrt_fusion) | copy-start | bytes 196
  2.7 12.5 %copy-start.15 = (s32[16]{0:T(128)}, s32[16]{0:T(128)S(1)}, u32[]{:S(2)}) copy-start(s32[16]{0:T(128)S(1)} %broadcast_minimum_fusion.1) | copy-start | bytes 196
  3.4 36.6 %copy-start.9 = (f32[1,3072]{1,0:T(1,128)}, f32[1,3072]{1,0:T(1,128)S(1)}, u32[]{:S(2)}) copy-start(f32[1,3072]{1,0:T(1,128)S(1)} %mul.194) | copy-start | bytes 36868
  7.1 31.0 %all-to-all-start = ((bf16[8,16,3200]{2,1,0:T(8,128)(2,1)}), bf16[8,16,3200]{2,1,0:T(8,128)(2,1)}, u32[]{:S(2)}, u32[]{:S(2)}) async-start(bf16[8,16,3200]{2,1,0:T(8,128)(2,1)} %broadcast_in_dim.10), calls=%async_computation | async-start | bytes 1638400 | tf_op jit(solution)/shard_map/all_to_all | solution.py:50
  15.2 1.2 %copy-start.1 = (bf16[256,3072]{1,0:T(8,128)(2,1)}, bf16[256,3072]{1,0:T(8,128)(2,1)S(1)}, u32[]{:S(2)}) copy-start(bf16[256,3072]{1,0:T(8,128)(2,1)S(1)} %convolution_convert_fusion) | copy-start | bytes 4718596
  15.2 4.2 %copy-start.3 = (bf16[1,16,3072]{2,1,0:T(8,128)(2,1)S(1)}, bf16[1,16,3072]{2,1,0:T(8,128)(2,1)}, u32[]{:S(2)}) copy-start(bf16[1,16,3072]{2,1,0:T(8,128)(2,1)} %param.10) | copy-start | bytes 294916
  15.2 4.3 %copy-start.8 = (s32[1,256,2]{1,2,0:T(2,128)S(1)}, s32[1,256,2]{1,2,0:T(2,128)}, u32[]{:S(2)}) copy-start(s32[1,256,2]{1,2,0:T(2,128)} %param.15) | copy-start | bytes 6148
  15.2 4.3 %copy-start.13 = (s32[1,256,2]{1,2,0:T(2,128)S(1)}, s32[1,256,2]{1,2,0:T(2,128)}, u32[]{:S(2)}) copy-start(s32[1,256,2]{1,2,0:T(2,128)} %param.12) | copy-start | bytes 6148
  17.3 22.7 %copy-start.11 = (bf16[1,3072,8]{1,2,0:T(8,128)(2,1)S(1)}, bf16[1,3072,8]{1,2,0:T(8,128)(2,1)}, u32[]{:S(2)}) copy-start(bf16[1,3072,8]{1,2,0:T(8,128)(2,1)} %param.18) | copy-start | bytes 147460
  17.3 4.6 %collective-permute-start = (bf16[8,16,3072]{2,1,0:T(8,128)(2,1)}, bf16[8,16,3072]{2,1,0:T(8,128)(2,1)}, u32[]{:S(2)}, u32[]{:S(2)}) collective-permute-start(bf16[8,16,3072]{2,1,0:T(8,128)(2,1)} %fusion.8), channel_id=1, source_target_pairs={{0,1},{1,0},{2,3},{3,2},{4,5},{5,4},{6,7},{7,6},{8,9},{9,8},{10,11... | collective-permute-start | bytes 2359304 | tf_op jit(solution)/shard_map/ppermute | solution.py:55
  38.1 9.4 %collective-permute-start.1 = (bf16[8,1,16,3200]{3,2,1,0:T(8,128)(2,1)}, bf16[8,1,16,3200]{3,2,1,0:T(8,128)(2,1)}, u32[]{:S(2)}, u32[]{:S(2)}) collective-permute-start(bf16[8,1,16,3200]{3,2,1,0:T(8,128)(2,1)} %bitcast.18), channel_id=1, source_target_pairs={{0,1},{1,0},{2,3},{3,2},{4,5},{5,4},{6,7},{7,6},{8,9},{9,8},{10,11... | collective-permute-start | bytes 2457608 | tf_op jit(solution)/shard_map/ppermute | solution.py:61
  43.4 23.2 %all-to-all-start.1 = ((bf16[8,16,1536]{2,1,0:T(8,128)(2,1)}), bf16[8,16,1536]{2,1,0:T(8,128)(2,1)}, u32[]{:S(2)}, u32[]{:S(2)}) async-start(bf16[8,16,1536]{2,1,0:T(8,128)(2,1)} %get-tuple-element.7), calls=%async_computation.1 | async-start | bytes 786432 | tf_op jit(solution)/shard_map/all_to_all | solution.py:59
  49.8 1.2 %copy-start.2 = (bf16[8,2,16,3200]{3,2,1,0:T(8,128)(2,1)}, bf16[8,2,16,3200]{3,2,1,0:T(8,128)(2,1)S(1)}, u32[]{:S(2)}) copy-start(bf16[8,2,16,3200]{3,2,1,0:T(8,128)(2,1)S(1)} %maximum_select_fusion) | copy-start | bytes 4915204
  57.8 4.9 %collective-permute-start.2 = (f32[8,16]{1,0:T(8,128)S(1)}, f32[8,16]{1,0:T(8,128)S(1)}, u32[]{:S(2)}, u32[]{:S(2)}) collective-permute-start(f32[8,16]{1,0:T(8,128)S(1)} %bitcast.154), channel_id=1, source_target_pairs={{0,1},{1,0},{2,3},{3,2},{4,5},{5,4},{6,7},{7,6},{8,9},{9,8},{10,11... | collective-permute-start | bytes 1544 | tf_op jit(solution)/shard_map/ppermute | solution.py:79
  62.1 29.4 %copy-start.12 = (f32[16]{0:T(128)S(1)}, f32[16]{0:T(128)}, u32[]{:S(2)}) copy-start(f32[16]{0:T(128)} %fusion.55) | copy-start | bytes 196
  64.9 32.8 %copy-start.10 = (f32[1,3072]{1,0:T(1,128)S(1)}, f32[1,3072]{1,0:T(1,128)}, u32[]{:S(2)}) copy-start(f32[1,3072]{1,0:T(1,128)} %copy-done.9) | copy-start | bytes 36868
  66.5 25.0 %copy-start.4 = (bf16[1,16,3072]{2,1,0:T(8,128)(2,1)S(1)}, bf16[1,16,3072]{2,1,0:T(8,128)(2,1)}, u32[]{:S(2)}) copy-start(bf16[1,16,3072]{2,1,0:T(8,128)(2,1)} %param.10) | copy-start | bytes 294916
  66.5 31.2 %copy-start.5 = (bf16[1,16,3072]{2,1,0:T(8,128)(2,1)S(1)}, bf16[1,16,3072]{2,1,0:T(8,128)(2,1)}, u32[]{:S(2)}) copy-start(bf16[1,16,3072]{2,1,0:T(8,128)(2,1)} %param.13) | copy-start | bytes 294916
  66.5 32.3 %copy-start.6 = (bf16[1,16,3072]{2,1,0:T(8,128)(2,1)S(1)}, bf16[1,16,3072]{2,1,0:T(8,128)(2,1)}, u32[]{:S(2)}) copy-start(bf16[1,16,3072]{2,1,0:T(8,128)(2,1)} %param.16) | copy-start | bytes 294916
  66.5 22.9 %all-to-all-start.2 = ((bf16[8,16,1664]{2,1,0:T(8,128)(2,1)}), bf16[8,16,1664]{2,1,0:T(8,128)(2,1)}, u32[]{:S(2)}, u32[]{:S(2)}) async-start(bf16[8,16,1664]{2,1,0:T(8,128)(2,1)} %concatenate.26), calls=%async_computation.2 | async-start | bytes 851968 | tf_op jit(solution)/shard_map/all_to_all | solution.py:87
  91.6 9.9 %collective-permute-start.3 = (bf16[16,3072]{1,0:T(8,128)(2,1)S(1)}, bf16[16,3072]{1,0:T(8,128)(2,1)S(1)}, u32[]{:S(2)}, u32[]{:S(2)}) collective-permute-start(bf16[16,3072]{1,0:T(8,128)(2,1)S(1)} %fusion.29), channel_id=1, source_target_pairs={{0,16},{16,32},{32,48},{48,64},{64,80},{80,96},{96,112},{112,128},... | collective-permute-start | bytes 294920 | tf_op jit(solution)/shard_map/ppermute | solution.py:10
  99.6 9.8 %collective-permute-start.4 = (bf16[16,3072]{1,0:T(8,128)(2,1)S(1)}, bf16[16,3072]{1,0:T(8,128)(2,1)S(1)}, u32[]{:S(2)}, u32[]{:S(2)}) collective-permute-start(bf16[16,3072]{1,0:T(8,128)(2,1)S(1)} %fusion.24), channel_id=1, source_target_pairs={{16,0},{32,16},{48,32},{64,48},{80,64},{96,80},{112,96},{128,112},... | collective-permute-start | bytes 294920 | tf_op jit(solution)/shard_map/ppermute | solution.py:10

commit v8 on v4

--- a/solution.py
+++ b/solution.py
@@ -56,7 +56,6 @@
     pair_z = (mine_z.astype(jnp.float32) + given.astype(jnp.float32)).astype(jnp.bfloat16)
     pair_z, same_core = lax.optimization_barrier((pair_z, same_core))
     got = lax.all_to_all(pair_z.reshape(chips * own_rows, width), "ety", 0, 0, tiled=True)
-    z_sum = jnp.sum(got.reshape(chips, own_rows, width).astype(jnp.float32), axis=0)
 
     other_core = lax.ppermute(same_core, "etc", [(0, 1), (1, 0)])
     full = jnp.where(
@@ -73,9 +72,10 @@
     )
     dact = (coef_b[:, None] * back_up).astype(jnp.bfloat16)
     dprob_part = jnp.sum(act_bwd.astype(jnp.float32) * back_up, axis=1)
-    dprob_part, z_sum = lax.optimization_barrier((dprob_part, z_sum))
+    dprob_part, got = lax.optimization_barrier((dprob_part, got))
     dprob_got = lax.all_to_all(dprob_part.reshape(groups, own_rows), ("ety", "etc"), 0, 0, tiled=True)
     dprob_mine = jnp.sum(dprob_got, axis=0)
+    z_sum = jnp.sum(got.reshape(chips, own_rows, width).astype(jnp.float32), axis=0)
 
     ids_f_own = lax.dynamic_slice_in_dim(ids_fwd, first_row, own_rows, 0)
     _, _, _, coef_f = routing(logit_f, ids_f_own, experts)
@@ -83,18 +83,17 @@
 
     ids_b_own = lax.dynamic_slice_in_dim(ids_bwd, first_row, own_rows, 0)
     route_mine, onehot_mine, sigma_mine, _ = routing(logit_b, ids_b_own, experts)
-    slope = route_mine * dprob_mine * sigma_mine * (1.0 - sigma_mine)
     router_wide = w_router.astype(jnp.float32)
     spread = router_wide[:, 0][None, :] - jnp.dot(
         onehot_mine, router_wide.T, precision=lax.Precision.HIGHEST
     )
-    dnormed = slope[:, None] * spread
-    scaled_rows = dnormed * gain.astype(jnp.float32)
+    scaled_rows = spread * gain.astype(jnp.float32)
     normalized_input = backward_wide_rows * backward_inverse_norm
-    norm_input_gradient = backward_inverse_norm * (
+    along = (route_mine * sigma_mine * (1.0 - sigma_mine))[:, None] * backward_inverse_norm * (
         scaled_rows
         - normalized_input * jnp.mean(scaled_rows * normalized_input, axis=-1, keepdims=True)
     )
+    norm_input_gradient = dprob_mine[:, None] * along
     input_grad = (grad_out.astype(jnp.float32) + norm_input_gradient).astype(jnp.bfloat16)
     fwd_in = from_behind(layer_out, "section", 1)
     incoming_gradient = from_behind(input_grad, "section", -1)

time: 96.5 us -> 95.5 us (0.990)
  the two profiles are of different devices: /device:TPU:198 before, /device:TPU:206 now
where the time goes in v8:
time: 95.5 us; the launch traced here: 94.7 us
  waiting for transfers between devices  33.9 us (35%)
  starting transfers between devices  29 us (30%)
  other arithmetic  16.7 us (17%)
  matrix products  7.25 us (8%)
  local copies, waits for them, and re-layouts  7 us (7%)
    all_to_all x1, waiting for transfers between devices, shards(): lax.all_to_all(pair_z.reshape(chips * own_rows, width), 'ety', 0, 0, tile...  13.1 us
    all_to_all x1, waiting for transfers between devices, shards(): lax.all_to_all(tiled, 'ety', 0, 0, tiled=True)  12 us
    ppermute x2, waiting for transfers between devices, from_behind(): lax.ppermute(value, axis, [(source, source + steps) for source in range(f...  7.89 us
    all_to_all x1, starting transfers between devices, shards(): lax.all_to_all(tiled, 'ety', 0, 0, tiled=True)  7.55 us
    ppermute x2, starting transfers between devices, from_behind(): lax.ppermute(value, axis, [(source, source + steps) for source in range(f...  7.31 us
    all_to_all x1, starting transfers between devices, shards(): lax.all_to_all(pair_z.reshape(chips * own_rows, width), 'ety', 0, 0, tile...  5.55 us
    all_to_all x1, starting transfers between devices, shards(): lax.all_to_all(dprob_part.reshape(groups, own_rows), ('ety', 'etc'), 0, 0...  4.76 us
    unnamed x32, local copies, waits for them, and re-layouts  4.6 us
  transfers between devices with their start and end apart: 7, of which 4 were waited for; matrix products, arithmetic and copies ran while one was open for 22% of the time, Pallas kernels for 0%

profile of v8, /device:TPU:206, one launch (start us, length us, event | category | flops | bytes accessed | tf_op | source)
XLA Modules:
  0.0 94.7 jit_solution(6884291662478334150)
XLA Ops:
  0.7 0.9 dynamic-slice_reduce_fusion
  1.6 1.1 %fusion.25 = f32[16]{0:T(128)S(1)} fusion(bf16[1,16,3072]{2,1,0:T(8,128)(2,1)} %param.13), kind=kLoop, calls=%fused_computation.41 | loop fusion | flops 147440 | bytes 98368 | tf_op jit(solution)/shard_map/reduce_sum | solution.py:15
  2.7 0.7 mul.188
  3.5 1.1 %select_reduce_fusion.1 = (f32[16]{0:T(128)S(1)}, bf16[16,8]{0,1:T(8,128)(2,1)S(1)}) fusion(s32[16]{0:T(128)S(1)} %broadcast_minimum_fusion.1, bf16[1,3072,8]{1,2,0:T(8,128)(2,1)} %param.18, bf16[1,16,3072]{2,1,0:T(8,128)(2,1)} %param.13, f32[16]{0:T(128)S(1)} %add_rsqrt_fusion, f32[3072]{0:T(1024)S(1)} %bitcast.153), kind=kOutput, calls=%fused_computation.58 | convolution fusion | flops 983664 | bytes 160192 | tf_op jit(solution)/shard_map/dot_general | solution.py:17
  4.7 0.9 fusion.32
  5.6 1.0 %broadcast_in_dim.8 = bf16[8,16,3200]{2,1,0:T(8,128)(2,1)} broadcast(bf16[16,3200]{1,0:T(8,128)(2,1)S(1)} %fusion.32), dimensions={1,2} | broadcast | bytes 921600 | tf_op jit(solution)/shard_map/broadcast_in_dim | solution.py:49
  6.5 7.5 %all-to-all-start = ((bf16[8,16,3200]{2,1,0:T(8,128)(2,1)}), bf16[8,16,3200]{2,1,0:T(8,128)(2,1)}, u32[]{:S(2)}, u32[]{:S(2)}) async-start(bf16[8,16,3200]{2,1,0:T(8,128)(2,1)} %broadcast_in_dim.8), calls=%async_computation | async-start | bytes 1638400 | tf_op jit(solution)/shard_map/all_to_all | solution.py:50
  14.1 1.0 %convolution_convert_fusion = bf16[256,3072]{1,0:T(8,128)(2,1)S(1)} fusion(bf16[1,512,3072]{2,1,0:T(8,128)(2,1)S(1)} %copy-done, bf16[1,256,512]{2,1,0:T(8,128)(2,1)S(1)} %copy-done.5), kind=kOutput, calls=%fused_computation | convolution fusion | flops 806092800 | bytes 4980736 | tf_op jit(solution)/shard_map/dot_general | solution.py:51
  15.2 1.1 %copy-done.1 = bf16[256,3072]{1,0:T(8,128)(2,1)} copy-done((bf16[256,3072]{1,0:T(8,128)(2,1)}, bf16[256,3072]{1,0:T(8,128)(2,1)S(1)}, u32[]{:S(2)}) %copy-start.1) | copy-done | bytes 1572888
  16.3 1.0 %fusion.7 = bf16[8,16,3072]{2,1,0:T(8,128)(2,1)} fusion(pred[]{:T(512)S(6)} %eq.63, bf16[8,2,16,3072]{3,2,1,0:T(8,128)(2,1)S(1)} %bitcast.145), kind=kLoop, calls=%fused_computation.15 | loop fusion | flops 393216 | bytes 2359297 | tf_op jit(solution)/shard_map/jit(_where)/select_n | solution.py:54
  17.2 1.9 %collective-permute-start = (bf16[8,16,3072]{2,1,0:T(8,128)(2,1)}, bf16[8,16,3072]{2,1,0:T(8,128)(2,1)}, u32[]{:S(2)}, u32[]{:S(2)}) collective-permute-start(bf16[8,16,3072]{2,1,0:T(8,128)(2,1)} %fusion.7), channel_id=1, source_target_pairs={{0,1},{1,0},{2,3},{3,2},{4,5},{5,4},{6,7},{7,6},{8,9},{9,8},{10,11... | collective-permute-start | bytes 2359304 | tf_op jit(solution)/shard_map/ppermute | solution.py:55
  20.8 0.9 collective-permute-done
  21.7 2.9 %fusion.5 = bf16[8,16,3072]{2,1,0:T(8,128)(2,1)} fusion(bf16[8,16,3072]{2,1,0:T(8,128)(2,1)} %collective-permute-done, pred[]{:T(512)S(6)} %eq.63, bf16[8,2,16,3072]{3,2,1,0:T(8,128)(2,1)} %bitcast.146), kind=kLoop, calls=%fused_computation.10 | loop fusion | flops 1966080 | bytes 3145729 | tf_op jit(solution)/shard_map/convert_element_type | solution.py:56
  24.6 12.0 %all-to-all-done = bf16[8,16,3200]{2,1,0:T(8,128)(2,1)} async-done(((bf16[8,16,3200]{2,1,0:T(8,128)(2,1)}), bf16[8,16,3200]{2,1,0:T(8,128)(2,1)}, u32[]{:S(2)}, u32[]{:S(2)}) %all-to-all-start) | async-done | bytes 819232 | tf_op jit(solution)/shard_map/all_to_all | solution.py:50
  36.6 1.9 %collective-permute-start.1 = (bf16[8,1,16,3200]{3,2,0,1:T(8,128)(2,1)}, bf16[8,1,16,3200]{3,2,0,1:T(8,128)(2,1)}, u32[]{:S(2)}, u32[]{:S(2)}) collective-permute-start(bf16[8,1,16,3200]{3,2,0,1:T(8,128)(2,1)} %bitcast.19), channel_id=1, source_target_pairs={{0,1},{1,0},{2,3},{3,2},{4,5},{5,4},{6,7},{7,6},{8,9},{9,8},{10,11... | collective-permute-start | bytes 2457608 | tf_op jit(solution)/shard_map/ppermute | solution.py:60
  39.7 1.7 %fusion.19 = (f32[16]{0:T(128)}, f32[16,3072]{1,0:T(8,128)S(1)}) fusion(bf16[1,16,3072]{2,1,0:T(8,128)(2,1)S(1)} %copy-done.3, f32[16]{0:T(128)} %copy-done.11, f32[3072]{0:T(1024)S(1)} %bitcast.155, bf16[1,3072,8]{1,2,0:T(8,128)(2,1)} %param.18, s32[16]{0:T(128)} %copy-done.13, f32[3072]{0:T(1024)} %bitcast.156), kind=kOutput, calls=%fused_computation.35 | convolution fusion | flops 1081456 | bytes 368832 | tf_op jit(solution)/shard_map/dot_general | solution.py:87
  41.4 5.5 %all-to-all-start.1 = ((bf16[8,16,3072]{2,1,0:T(8,128)(2,1)}), bf16[8,16,3072]{2,1,0:T(8,128)(2,1)}, u32[]{:S(2)}, u32[]{:S(2)}) async-start(bf16[8,16,3072]{2,1,0:T(8,128)(2,1)} %fusion.5), calls=%async_computation.1 | async-start | bytes 1572864 | tf_op jit(solution)/shard_map/all_to_all | solution.py:58
  47.0 1.1 %broadcast_multiply_fusion = f32[16]{0:T(128)} fusion(f32[16]{0:T(128)} %get-tuple-element.15), kind=kLoop, calls=%fused_computation.91 | loop fusion | flops 16 | bytes 128 | tf_op jit(solution)/shard_map/div | solution.py:94
  48.1 2.3 %maximum_select_fusion = bf16[8,2,16,3200]{3,2,0,1:T(8,128)(2,1)S(1)} fusion(bf16[8,1,16,3200]{3,2,0,1:T(8,128)(2,1)} %collective-permute-done.1, bf16[8,1,16,3200]{3,2,0,1:T(8,128)(2,1)} %bitcast.19, pred[]{:T(512)S(6)} %eq.63), kind=kLoop, calls=%fused_computation.6 | loop fusion | flops 2457600 | bytes 3276801 | tf_op jit(solution)/shard_map/jit(_where)/select_n | solution.py:61
  50.6 1.2 %copy-done.2 = bf16[8,2,16,3200]{3,2,1,0:T(8,128)(2,1)} copy-done((bf16[8,2,16,3200]{3,2,1,0:T(8,128)(2,1)}, bf16[8,2,16,3200]{3,2,1,0:T(8,128)(2,1)S(1)}, u32[]{:S(2)}) %copy-start.2) | copy-done | bytes 1638424
  52.4 0.9 copy.58
  53.4 3.2 %fusion.10 = (bf16[1,256,512]{2,1,0:T(8,128)(2,1)}, f32[256]{0:T(256)S(1)}) fusion(f32[256]{0:T(256)S(1)} %bitcast.160, bf16[1,256,512]{2,1,0:T(8,128)(2,1)} %param.14, bf16[1,512,3072]{2,1,0:T(8,128)(2,1)S(1)} %copy-done, bf16[256,3200]{1,0:T(8,128)(2,1)} %bitcast.148), kind=kOutput, calls=%fused_computation.21 | convolution fusion | flops 805961472 | bytes 5244928 | tf_op jit(solution)/shard_map/dot_general | solution.py:70
  56.6 13.1 %all-to-all-done.1 = bf16[8,16,3072]{2,1,0:T(8,128)(2,1)} async-done(((bf16[8,16,3072]{2,1,0:T(8,128)(2,1)}), bf16[8,16,3072]{2,1,0:T(8,128)(2,1)}, u32[]{:S(2)}, u32[]{:S(2)}) %all-to-all-start.1) | async-done | bytes 786464 | tf_op jit(solution)/shard_map/all_to_all | solution.py:58
  69.7 0.7 all_to_all.19
  70.4 4.8 %all-to-all-start.2 = ((f32[16,1,16]{2,1,0:T(1,128)}), f32[16,1,16]{2,1,0:T(1,128)S(1)}, u32[]{:S(2)}, u32[]{:S(2)}) async-start(f32[16,1,16]{2,1,0:T(1,128)} %all_to_all.19), calls=%async_computation.2 | async-start | bytes 16384 | tf_op jit(solution)/shard_map/all_to_all | solution.py:76
  75.1 1.3 %convert_reduce_fusion = f32[16,3072]{1,0:T(8,128)S(1)} fusion(bf16[8,16,3072]{2,1,0:T(8,128)(2,1)} %bitcast.37), kind=kLoop, calls=%fused_computation.8 | loop fusion | flops 737280 | bytes 983040 | tf_op jit(solution)/shard_map/reduce_sum | solution.py:78
  76.4 0.7 fusion.29
  77.1 5.4 %collective-permute-start.2 = (bf16[16,3072]{1,0:T(8,128)(2,1)}, bf16[16,3072]{1,0:T(8,128)(2,1)S(1)}, u32[]{:S(2)}, u32[]{:S(2)}) collective-permute-start(bf16[16,3072]{1,0:T(8,128)(2,1)} %fusion.29), channel_id=1, source_target_pairs={{0,16},{16,32},{32,48},{48,64},{64,80},{80,96},{96,112},{112,128},... | collective-permute-start | bytes 294920 | tf_op jit(solution)/shard_map/ppermute | solution.py:10
  82.6 1.0 %fusion.24 = bf16[16,3072]{1,0:T(8,128)(2,1)S(1)} fusion(f32[16,3072]{1,0:T(8,128)S(1)} %get-tuple-element.16, bf16[1,16,3072]{2,1,0:T(8,128)(2,1)S(1)} %copy-done.3, f32[16]{0:T(128)} %broadcast_multiply_fusion, f32[16]{0:T(128)S(1)} %copy-done.12, f32[16]{0:T(128)} %fusion.46, f32[16]{0:T(128)S(1)} %reduce_sum.156, bf16[1,16,3072]{2,1,0:T(8,128)(2,1)} %param.16), kind=kLoop, calls=%fused_computation.40 | loop fusion | flops 442368 | bytes 491776 | tf_op jit(solution)/shard_map/convert_element_type | solution.py:97
  83.6 1.9 %collective-permute-start.3 = (bf16[16,3072]{1,0:T(8,128)(2,1)S(1)}, bf16[16,3072]{1,0:T(8,128)(2,1)S(1)}, u32[]{:S(2)}, u32[]{:S(2)}) collective-permute-start(bf16[16,3072]{1,0:T(8,128)(2,1)S(1)} %fusion.24), channel_id=1, source_target_pairs={{16,0},{32,16},{48,32},{64,48},{80,64},{96,80},{112,96},{128,112},... | collective-permute-start | bytes 294920 | tf_op jit(solution)/shard_map/ppermute | solution.py:10
  85.6 7.9 %collective-permute-done.3 = bf16[16,3072]{1,0:T(8,128)(2,1)S(1)} collective-permute-done((bf16[16,3072]{1,0:T(8,128)(2,1)S(1)}, bf16[16,3072]{1,0:T(8,128)(2,1)S(1)}, u32[]{:S(2)}, u32[]{:S(2)}) %collective-permute-start.3) | collective-permute-done | bytes 98336 | tf_op jit(solution)/shard_map/ppermute | solution.py:10
  93.4 0.6 copy.62
  (52 shorter events, 4.6 us)
Async XLA Ops:
  0.6 13.5 %copy-start = (bf16[1,512,3072]{2,1,0:T(8,128)(2,1)S(1)}, bf16[1,512,3072]{2,1,0:T(8,128)(2,1)}, u32[]{:S(2)}) copy-start(bf16[1,512,3072]{2,1,0:T(8,128)(2,1)} %param.19) | copy-start | bytes 9437188
  0.6 13.5 %copy-start.5 = (bf16[1,256,512]{2,1,0:T(8,128)(2,1)S(1)}, bf16[1,256,512]{2,1,0:T(8,128)(2,1)}, u32[]{:S(2)}) copy-start(bf16[1,256,512]{2,1,0:T(8,128)(2,1)} %param.11) | copy-start | bytes 786436
  1.6 12.5 %copy-start.13 = (s32[16]{0:T(128)}, s32[16]{0:T(128)S(1)}, u32[]{:S(2)}) copy-start(s32[16]{0:T(128)S(1)} %broadcast_minimum_fusion.1) | copy-start | bytes 196
  2.7 1.9 %copy-start.11 = (f32[16]{0:T(128)}, f32[16]{0:T(128)S(1)}, u32[]{:S(2)}) copy-start(f32[16]{0:T(128)S(1)} %add_rsqrt_fusion) | copy-start | bytes 196
  6.5 30.0 %all-to-all-start = ((bf16[8,16,3200]{2,1,0:T(8,128)(2,1)}), bf16[8,16,3200]{2,1,0:T(8,128)(2,1)}, u32[]{:S(2)}, u32[]{:S(2)}) async-start(bf16[8,16,3200]{2,1,0:T(8,128)(2,1)} %broadcast_in_dim.8), calls=%async_computation | async-start | bytes 1638400 | tf_op jit(solution)/shard_map/all_to_all | solution.py:50
  15.1 1.2 %copy-start.1 = (bf16[256,3072]{1,0:T(8,128)(2,1)}, bf16[256,3072]{1,0:T(8,128)(2,1)S(1)}, u32[]{:S(2)}) copy-start(bf16[256,3072]{1,0:T(8,128)(2,1)S(1)} %convolution_convert_fusion) | copy-start | bytes 4718596
  15.1 4.0 %copy-start.10 = (s32[1,256,2]{1,2,0:T(2,128)S(1)}, s32[1,256,2]{1,2,0:T(2,128)}, u32[]{:S(2)}) copy-start(s32[1,256,2]{1,2,0:T(2,128)} %param.12) | copy-start | bytes 6148
  15.1 4.1 %copy-start.4 = (bf16[1,16,3072]{2,1,0:T(8,128)(2,1)S(1)}, bf16[1,16,3072]{2,1,0:T(8,128)(2,1)}, u32[]{:S(2)}) copy-start(bf16[1,16,3072]{2,1,0:T(8,128)(2,1)} %param.10) | copy-start | bytes 294916
  15.1 4.3 %copy-start.6 = (bf16[1,3072,8]{1,2,0:T(8,128)(2,1)S(1)}, bf16[1,3072,8]{1,2,0:T(8,128)(2,1)}, u32[]{:S(2)}) copy-start(bf16[1,3072,8]{1,2,0:T(8,128)(2,1)} %param.18) | copy-start | bytes 147460
  15.1 5.0 %copy-start.7 = (s32[1,256,2]{1,2,0:T(2,128)S(1)}, s32[1,256,2]{1,2,0:T(2,128)}, u32[]{:S(2)}) copy-start(s32[1,256,2]{1,2,0:T(2,128)} %param.15) | copy-start | bytes 6148
  17.2 4.5 %collective-permute-start = (bf16[8,16,3072]{2,1,0:T(8,128)(2,1)}, bf16[8,16,3072]{2,1,0:T(8,128)(2,1)}, u32[]{:S(2)}, u32[]{:S(2)}) collective-permute-start(bf16[8,16,3072]{2,1,0:T(8,128)(2,1)} %fusion.7), channel_id=1, source_target_pairs={{0,1},{1,0},{2,3},{3,2},{4,5},{5,4},{6,7},{7,6},{8,9},{9,8},{10,11... | collective-permute-start | bytes 2359304 | tf_op jit(solution)/shard_map/ppermute | solution.py:55
  19.6 20.1 %copy-start.3 = (bf16[1,16,3072]{2,1,0:T(8,128)(2,1)S(1)}, bf16[1,16,3072]{2,1,0:T(8,128)(2,1)}, u32[]{:S(2)}) copy-start(bf16[1,16,3072]{2,1,0:T(8,128)(2,1)} %param.13) | copy-start | bytes 294916
  36.6 11.6 %collective-permute-start.1 = (bf16[8,1,16,3200]{3,2,0,1:T(8,128)(2,1)}, bf16[8,1,16,3200]{3,2,0,1:T(8,128)(2,1)}, u32[]{:S(2)}, u32[]{:S(2)}) collective-permute-start(bf16[8,1,16,3200]{3,2,0,1:T(8,128)(2,1)} %bitcast.19), channel_id=1, source_target_pairs={{0,1},{1,0},{2,3},{3,2},{4,5},{5,4},{6,7},{7,6},{8,9},{9,8},{10,11... | collective-permute-start | bytes 2457608 | tf_op jit(solution)/shard_map/ppermute | solution.py:60
  41.4 28.3 %all-to-all-start.1 = ((bf16[8,16,3072]{2,1,0:T(8,128)(2,1)}), bf16[8,16,3072]{2,1,0:T(8,128)(2,1)}, u32[]{:S(2)}, u32[]{:S(2)}) async-start(bf16[8,16,3072]{2,1,0:T(8,128)(2,1)} %fusion.5), calls=%async_computation.1 | async-start | bytes 1572864 | tf_op jit(solution)/shard_map/all_to_all | solution.py:58
  50.4 2.9 %copy-start.8 = (s32[256]{0:T(256)S(1)}, s32[256]{0:T(256)}, u32[]{:S(2)}) copy-start(s32[256]{0:T(256)} %broadcast_minimum_fusion) | copy-start | bytes 3076
  50.6 1.2 %copy-start.2 = (bf16[8,2,16,3200]{3,2,1,0:T(8,128)(2,1)}, bf16[8,2,16,3200]{3,2,1,0:T(8,128)(2,1)S(1)}, u32[]{:S(2)}) copy-start(bf16[8,2,16,3200]{3,2,1,0:T(8,128)(2,1)S(1)} %copy.54) | copy-start | bytes 4915204
  53.3 23.1 %copy-start.9 = (f32[16]{0:T(128)S(1)}, f32[16]{0:T(128)}, u32[]{:S(2)}) copy-start(f32[16]{0:T(128)} %fusion.52) | copy-start | bytes 196
  53.3 29.2 %copy-start.12 = (f32[16]{0:T(128)S(1)}, f32[16]{0:T(128)}, u32[]{:S(2)}) copy-start(f32[16]{0:T(128)} %copy-done.11) | copy-start | bytes 196
  70.4 12.2 %all-to-all-start.2 = ((f32[16,1,16]{2,1,0:T(1,128)}), f32[16,1,16]{2,1,0:T(1,128)S(1)}, u32[]{:S(2)}, u32[]{:S(2)}) async-start(f32[16,1,16]{2,1,0:T(1,128)} %all_to_all.19), calls=%async_computation.2 | async-start | bytes 16384 | tf_op jit(solution)/shard_map/all_to_all | solution.py:76
  77.1 8.4 %collective-permute-start.2 = (bf16[16,3072]{1,0:T(8,128)(2,1)}, bf16[16,3072]{1,0:T(8,128)(2,1)S(1)}, u32[]{:S(2)}, u32[]{:S(2)}) collective-permute-start(bf16[16,3072]{1,0:T(8,128)(2,1)} %fusion.29), channel_id=1, source_target_pairs={{0,16},{16,32},{32,48},{48,64},{64,80},{80,96},{96,112},{112,128},... | collective-permute-start | bytes 294920 | tf_op jit(solution)/shard_map/ppermute | solution.py:10
  83.6 9.8 %collective-permute-start.3 = (bf16[16,3072]{1,0:T(8,128)(2,1)S(1)}, bf16[16,3072]{1,0:T(8,128)(2,1)S(1)}, u32[]{:S(2)}, u32[]{:S(2)}) collective-permute-start(bf16[16,3072]{1,0:T(8,128)(2,1)S(1)} %fusion.24), channel_id=1, source_target_pairs={{16,0},{32,16},{48,32},{64,48},{80,64},{96,80},{112,96},{128,112},... | collective-permute-start | bytes 294920 | tf_op jit(solution)/shard_map/ppermute | solution.py:10

commit v9 on v8

--- a/solution.py
+++ b/solution.py
@@ -28,7 +28,7 @@
     return (route, onehot, sigma, route * sigma)
 
 
-def shards(x_fwd, act_fwd, ids_fwd, x_bwd, act_bwd, ids_bwd, grad_out, gain, w_router, w_down):
+def layer(x_fwd, act_fwd, ids_fwd, x_bwd, act_bwd, ids_bwd, grad_out, gain, w_router, w_down):
     x_fwd, act_fwd, ids_fwd, x_bwd, act_bwd = (x_fwd[0], act_fwd[0], ids_fwd[0], x_bwd[0], act_bwd[0])
     ids_bwd, grad_out, gain, w_router, w_down = (ids_bwd[0], grad_out[0], gain[0], w_router[0], w_down[0])
     experts = w_router.shape[1]
@@ -38,7 +38,7 @@
     first_row = (lax.axis_index("ety") * lax.axis_size("etc") + lax.axis_index("etc")) * own_rows
     pad = 128
 
-    wide_f, inverse_f, logit_f = norm_logits(x_fwd, gain, w_router)
+    wide_f, _, logit_f = norm_logits(x_fwd, gain, w_router)
     backward_wide_rows, backward_inverse_norm, logit_b = norm_logits(x_bwd, gain, w_router)
 
     packed = jnp.concatenate(
@@ -66,7 +66,7 @@
     full_g = full[:, :width]
     full_b = full[:, width : width + experts]
 
-    route_b, onehot_b, sigma_b, coef_b = routing(full_b, ids_bwd, experts)
+    _, _, _, coef_b = routing(full_b, ids_bwd, experts)
     back_up = lax.dot_general(
         full_g, w_down, (((1,), (1,)), ((), ())), preferred_element_type=jnp.float32
     )
@@ -95,9 +95,9 @@
     )
     norm_input_gradient = dprob_mine[:, None] * along
     input_grad = (grad_out.astype(jnp.float32) + norm_input_gradient).astype(jnp.bfloat16)
-    fwd_in = from_behind(layer_out, "section", 1)
-    incoming_gradient = from_behind(input_grad, "section", -1)
-    return (fwd_in[None], incoming_gradient[None], dact[None])
+    fwd_in = from_behind(layer_out[None], "section", 1)
+    incoming_gradient = from_behind(input_grad[None], "section", -1)
+    return (fwd_in, incoming_gradient, dact[None])
 
 
 def solution(mesh):
@@ -117,7 +117,7 @@
         P("section", et, None),
     )
     return jax.shard_map(
-        shards,
+        layer,
         mesh=mesh,
         in_specs=placed,
         out_specs=(P("section", et, None), P("section", et, None), P("section", None, et)),

time: 95.5 us -> 95.5 us (level)
    broadcast_in_dim x0 -> x1, other arithmetic: none -> 1.03 us  [layer(): incoming_gradient = from_behind(input_grad[None], 'section', -1)]
    convert_element_type x3 -> x2, other arithmetic: 4.62 us -> 3.59 us  [the longest x1 2.86 us: layer(): (mine_z.astype(jnp.float32) + given.astype(jnp.float32)).astype(jnp.bfloa...]
where the time goes in v9:
time: 95.5 us; the launch traced here: 94.7 us
  waiting for transfers between devices  33.9 us (35%)
  starting transfers between devices  29 us (30%)
  other arithmetic  16.7 us (17%)
  matrix products  7.25 us (8%)
  local copies, waits for them, and re-layouts  7 us (7%)
    all_to_all x1, waiting for transfers between devices, layer(): lax.all_to_all(pair_z.reshape(chips * own_rows, width), 'ety', 0, 0, tile...  13.1 us
    all_to_all x1, waiting for transfers between devices, layer(): lax.all_to_all(tiled, 'ety', 0, 0, tiled=True)  12 us
    ppermute x2, waiting for transfers between devices, from_behind(): lax.ppermute(value, axis, [(source, source + steps) for source in range(f...  7.89 us
    all_to_all x1, starting transfers between devices, layer(): lax.all_to_all(tiled, 'ety', 0, 0, tiled=True)  7.55 us
    ppermute x2, starting transfers between devices, from_behind(): lax.ppermute(value, axis, [(source, source + steps) for source in range(f...  7.31 us
    all_to_all x1, starting transfers between devices, layer(): lax.all_to_all(pair_z.reshape(chips * own_rows, width), 'ety', 0, 0, tile...  5.55 us
    all_to_all x1, starting transfers between devices, layer(): lax.all_to_all(dprob_part.reshape(groups, own_rows), ('ety', 'etc'), 0, 0...  4.76 us
    unnamed x32, local copies, waits for them, and re-layouts  4.6 us
  transfers between devices with their start and end apart: 7, of which 4 were waited for; matrix products, arithmetic and copies ran while one was open for 22% of the time, Pallas kernels for 0%

profile of v9, /device:TPU:206, one launch (start us, length us, event | category | flops | bytes accessed | tf_op | source)
XLA Modules:
  0.0 94.7 jit_solution(6884291662478334150)
XLA Ops:
  0.7 0.9 dynamic-slice_reduce_fusion
  1.6 1.1 %fusion.23 = f32[16]{0:T(128)S(1)} fusion(bf16[1,16,3072]{2,1,0:T(8,128)(2,1)} %param.13), kind=kLoop, calls=%fused_computation.40 | loop fusion | flops 147440 | bytes 98368 | tf_op jit(solution)/shard_map/reduce_sum | solution.py:15
  2.7 0.7 mul.196
  3.5 1.1 %select_reduce_fusion.1 = (f32[16]{0:T(128)S(1)}, bf16[16,8]{0,1:T(8,128)(2,1)S(1)}) fusion(s32[16]{0:T(128)S(1)} %broadcast_minimum_fusion.1, bf16[1,3072,8]{1,2,0:T(8,128)(2,1)} %param.18, bf16[1,16,3072]{2,1,0:T(8,128)(2,1)} %param.13, f32[16]{0:T(128)S(1)} %add_rsqrt_fusion, f32[3072]{0:T(1024)S(1)} %bitcast.147), kind=kOutput, calls=%fused_computation.59 | convolution fusion | flops 983664 | bytes 160192 | tf_op jit(solution)/shard_map/dot_general | solution.py:17
  4.7 0.9 fusion.30
  5.6 1.0 %broadcast_in_dim.6 = bf16[8,16,3200]{2,1,0:T(8,128)(2,1)} broadcast(bf16[16,3200]{1,0:T(8,128)(2,1)S(1)} %fusion.30), dimensions={1,2} | broadcast | bytes 921600 | tf_op jit(solution)/shard_map/broadcast_in_dim | solution.py:49
  6.5 7.5 %all-to-all-start = ((bf16[8,16,3200]{2,1,0:T(8,128)(2,1)}), bf16[8,16,3200]{2,1,0:T(8,128)(2,1)}, u32[]{:S(2)}, u32[]{:S(2)}) async-start(bf16[8,16,3200]{2,1,0:T(8,128)(2,1)} %broadcast_in_dim.6), calls=%async_computation | async-start | bytes 1638400 | tf_op jit(solution)/shard_map/all_to_all | solution.py:50
  14.1 1.0 %convolution_convert_fusion = bf16[256,3072]{1,0:T(8,128)(2,1)S(1)} fusion(bf16[1,512,3072]{2,1,0:T(8,128)(2,1)S(1)} %copy-done, bf16[1,256,512]{2,1,0:T(8,128)(2,1)S(1)} %copy-done.5), kind=kOutput, calls=%fused_computation | convolution fusion | flops 806092800 | bytes 4980736 | tf_op jit(solution)/shard_map/dot_general | solution.py:51
  15.2 1.1 %copy-done.1 = bf16[256,3072]{1,0:T(8,128)(2,1)} copy-done((bf16[256,3072]{1,0:T(8,128)(2,1)}, bf16[256,3072]{1,0:T(8,128)(2,1)S(1)}, u32[]{:S(2)}) %copy-start.1) | copy-done | bytes 1572888
  16.3 1.0 %fusion.7 = bf16[8,16,3072]{2,1,0:T(8,128)(2,1)} fusion(pred[]{:T(512)S(6)} %eq.63, bf16[8,2,16,3072]{3,2,1,0:T(8,128)(2,1)S(1)} %bitcast.141), kind=kLoop, calls=%fused_computation.15 | loop fusion | flops 393216 | bytes 2359297 | tf_op jit(solution)/shard_map/jit(_where)/select_n | solution.py:54
  17.2 1.9 %collective-permute-start = (bf16[8,16,3072]{2,1,0:T(8,128)(2,1)}, bf16[8,16,3072]{2,1,0:T(8,128)(2,1)}, u32[]{:S(2)}, u32[]{:S(2)}) collective-permute-start(bf16[8,16,3072]{2,1,0:T(8,128)(2,1)} %fusion.7), channel_id=1, source_target_pairs={{0,1},{1,0},{2,3},{3,2},{4,5},{5,4},{6,7},{7,6},{8,9},{9,8},{10,11... | collective-permute-start | bytes 2359304 | tf_op jit(solution)/shard_map/ppermute | solution.py:55
  20.8 0.9 collective-permute-done
  21.7 2.9 %fusion.5 = bf16[8,16,3072]{2,1,0:T(8,128)(2,1)} fusion(bf16[8,16,3072]{2,1,0:T(8,128)(2,1)} %collective-permute-done, pred[]{:T(512)S(6)} %eq.63, bf16[8,2,16,3072]{3,2,1,0:T(8,128)(2,1)} %bitcast.142), kind=kLoop, calls=%fused_computation.10 | loop fusion | flops 1966080 | bytes 3145729 | tf_op jit(solution)/shard_map/convert_element_type | solution.py:56
  24.6 12.0 %all-to-all-done = bf16[8,16,3200]{2,1,0:T(8,128)(2,1)} async-done(((bf16[8,16,3200]{2,1,0:T(8,128)(2,1)}), bf16[8,16,3200]{2,1,0:T(8,128)(2,1)}, u32[]{:S(2)}, u32[]{:S(2)}) %all-to-all-start) | async-done | bytes 819232 | tf_op jit(solution)/shard_map/all_to_all | solution.py:50
  36.6 1.9 %collective-permute-start.1 = (bf16[8,1,16,3200]{3,2,0,1:T(8,128)(2,1)}, bf16[8,1,16,3200]{3,2,0,1:T(8,128)(2,1)}, u32[]{:S(2)}, u32[]{:S(2)}) collective-permute-start(bf16[8,1,16,3200]{3,2,0,1:T(8,128)(2,1)} %bitcast.18), channel_id=1, source_target_pairs={{0,1},{1,0},{2,3},{3,2},{4,5},{5,4},{6,7},{7,6},{8,9},{9,8},{10,11... | collective-permute-start | bytes 2457608 | tf_op jit(solution)/shard_map/ppermute | solution.py:60
  39.7 1.7 %fusion.17 = (f32[16]{0:T(128)}, f32[16,3072]{1,0:T(8,128)S(1)}) fusion(bf16[1,16,3072]{2,1,0:T(8,128)(2,1)S(1)} %copy-done.3, f32[16]{0:T(128)} %copy-done.11, f32[3072]{0:T(1024)S(1)} %bitcast.149, bf16[1,3072,8]{1,2,0:T(8,128)(2,1)} %param.18, s32[16]{0:T(128)} %copy-done.13, f32[3072]{0:T(1024)} %bitcast.150), kind=kOutput, calls=%fused_computation.34 | convolution fusion | flops 1081456 | bytes 368832 | tf_op jit(solution)/shard_map/dot_general | solution.py:87
  41.4 5.5 %all-to-all-start.1 = ((bf16[8,16,3072]{2,1,0:T(8,128)(2,1)}), bf16[8,16,3072]{2,1,0:T(8,128)(2,1)}, u32[]{:S(2)}, u32[]{:S(2)}) async-start(bf16[8,16,3072]{2,1,0:T(8,128)(2,1)} %fusion.5), calls=%async_computation.1 | async-start | bytes 1572864 | tf_op jit(solution)/shard_map/all_to_all | solution.py:58
  47.0 1.1 %broadcast_multiply_fusion = f32[16]{0:T(128)} fusion(f32[16]{0:T(128)} %get-tuple-element.15), kind=kLoop, calls=%fused_computation.92 | loop fusion | flops 16 | bytes 128 | tf_op jit(solution)/shard_map/div | solution.py:94
  48.1 2.3 %maximum_select_fusion = bf16[8,2,16,3200]{3,2,0,1:T(8,128)(2,1)S(1)} fusion(bf16[8,1,16,3200]{3,2,0,1:T(8,128)(2,1)} %collective-permute-done.1, bf16[8,1,16,3200]{3,2,0,1:T(8,128)(2,1)} %bitcast.18, pred[]{:T(512)S(6)} %eq.63), kind=kLoop, calls=%fused_computation.6 | loop fusion | flops 2457600 | bytes 3276801 | tf_op jit(solution)/shard_map/jit(_where)/select_n | solution.py:61
  50.6 1.2 %copy-done.2 = bf16[8,2,16,3200]{3,2,1,0:T(8,128)(2,1)} copy-done((bf16[8,2,16,3200]{3,2,1,0:T(8,128)(2,1)}, bf16[8,2,16,3200]{3,2,1,0:T(8,128)(2,1)S(1)}, u32[]{:S(2)}) %copy-start.2) | copy-done | bytes 1638424
  52.4 0.9 copy.58
  53.4 3.2 %fusion.10 = (bf16[1,256,512]{2,1,0:T(8,128)(2,1)}, f32[256]{0:T(256)S(1)}) fusion(f32[256]{0:T(256)S(1)} %bitcast.154, bf16[1,256,512]{2,1,0:T(8,128)(2,1)} %param.14, bf16[1,512,3072]{2,1,0:T(8,128)(2,1)S(1)} %copy-done, bf16[256,3200]{1,0:T(8,128)(2,1)} %bitcast.144), kind=kOutput, calls=%fused_computation.24 | convolution fusion | flops 805961472 | bytes 5244928 | tf_op jit(solution)/shard_map/dot_general | solution.py:70
  56.6 13.1 %all-to-all-done.1 = bf16[8,16,3072]{2,1,0:T(8,128)(2,1)} async-done(((bf16[8,16,3072]{2,1,0:T(8,128)(2,1)}), bf16[8,16,3072]{2,1,0:T(8,128)(2,1)}, u32[]{:S(2)}, u32[]{:S(2)}) %all-to-all-start.1) | async-done | bytes 786464 | tf_op jit(solution)/shard_map/all_to_all | solution.py:58
  69.7 0.7 all_to_all.19
  70.4 4.8 %all-to-all-start.2 = ((f32[16,1,16]{2,1,0:T(1,128)}), f32[16,1,16]{2,1,0:T(1,128)S(1)}, u32[]{:S(2)}, u32[]{:S(2)}) async-start(f32[16,1,16]{2,1,0:T(1,128)} %all_to_all.19), calls=%async_computation.2 | async-start | bytes 16384 | tf_op jit(solution)/shard_map/all_to_all | solution.py:76
  75.1 1.3 %convert_reduce_fusion = f32[16,3072]{1,0:T(8,128)S(1)} fusion(bf16[8,16,3072]{2,1,0:T(8,128)(2,1)} %bitcast.36), kind=kLoop, calls=%fused_computation.8 | loop fusion | flops 737280 | bytes 983040 | tf_op jit(solution)/shard_map/reduce_sum | solution.py:78
  76.4 0.7 fusion.29
  77.1 5.4 %collective-permute-start.2 = (bf16[1,16,3072]{2,1,0:T(8,128)(2,1)}, bf16[1,16,3072]{2,1,0:T(8,128)(2,1)S(1)}, u32[]{:S(2)}, u32[]{:S(2)}) collective-permute-start(bf16[1,16,3072]{2,1,0:T(8,128)(2,1)} %fusion.29), channel_id=1, source_target_pairs={{0,16},{16,32},{32,48},{48,64},{64,80},{80,96},{96,112},{112,128},... | collective-permute-start | bytes 294920 | tf_op jit(solution)/shard_map/ppermute | solution.py:10
  82.6 1.0 %fusion.35 = bf16[1,16,3072]{2,1,0:T(8,128)(2,1)S(1)} fusion(f32[16,3072]{1,0:T(8,128)S(1)} %get-tuple-element.16, bf16[1,16,3072]{2,1,0:T(8,128)(2,1)S(1)} %copy-done.3, f32[16]{0:T(128)} %broadcast_multiply_fusion, f32[16]{0:T(128)S(1)} %copy-done.12, f32[16]{0:T(128)} %fusion.45, f32[16]{0:T(128)S(1)} %reduce_sum.159, bf16[1,16,3072]{2,1,0:T(8,128)(2,1)} %param.16), kind=kLoop, calls=%fused_computation.51 | loop fusion | flops 442368 | bytes 491776 | tf_op jit(solution)/shard_map/broadcast_in_dim | solution.py:99
  83.6 1.9 %collective-permute-start.3 = (bf16[1,16,3072]{2,1,0:T(8,128)(2,1)S(1)}, bf16[1,16,3072]{2,1,0:T(8,128)(2,1)S(1)}, u32[]{:S(2)}, u32[]{:S(2)}) collective-permute-start(bf16[1,16,3072]{2,1,0:T(8,128)(2,1)S(1)} %fusion.35), channel_id=1, source_target_pairs={{16,0},{32,16},{48,32},{64,48},{80,64},{96,80},{112,96},{128,112},... | collective-permute-start | bytes 294920 | tf_op jit(solution)/shard_map/ppermute | solution.py:10
  85.6 7.9 %collective-permute-done.3 = bf16[1,16,3072]{2,1,0:T(8,128)(2,1)S(1)} collective-permute-done((bf16[1,16,3072]{2,1,0:T(8,128)(2,1)S(1)}, bf16[1,16,3072]{2,1,0:T(8,128)(2,1)S(1)}, u32[]{:S(2)}, u32[]{:S(2)}) %collective-permute-start.3) | collective-permute-done | bytes 98336 | tf_op jit(solution)/shard_map/ppermute | solution.py:10
  93.4 0.6 copy.62
  (52 shorter events, 4.6 us)
Async XLA Ops:
  0.6 13.5 %copy-start = (bf16[1,512,3072]{2,1,0:T(8,128)(2,1)S(1)}, bf16[1,512,3072]{2,1,0:T(8,128)(2,1)}, u32[]{:S(2)}) copy-start(bf16[1,512,3072]{2,1,0:T(8,128)(2,1)} %param.19) | copy-start | bytes 9437188
  0.6 13.5 %copy-start.5 = (bf16[1,256,512]{2,1,0:T(8,128)(2,1)S(1)}, bf16[1,256,512]{2,1,0:T(8,128)(2,1)}, u32[]{:S(2)}) copy-start(bf16[1,256,512]{2,1,0:T(8,128)(2,1)} %param.11) | copy-start | bytes 786436
  1.6 12.5 %copy-start.13 = (s32[16]{0:T(128)}, s32[16]{0:T(128)S(1)}, u32[]{:S(2)}) copy-start(s32[16]{0:T(128)S(1)} %broadcast_minimum_fusion.1) | copy-start | bytes 196
  2.7 1.9 %copy-start.11 = (f32[16]{0:T(128)}, f32[16]{0:T(128)S(1)}, u32[]{:S(2)}) copy-start(f32[16]{0:T(128)S(1)} %add_rsqrt_fusion) | copy-start | bytes 196
  6.5 30.0 %all-to-all-start = ((bf16[8,16,3200]{2,1,0:T(8,128)(2,1)}), bf16[8,16,3200]{2,1,0:T(8,128)(2,1)}, u32[]{:S(2)}, u32[]{:S(2)}) async-start(bf16[8,16,3200]{2,1,0:T(8,128)(2,1)} %broadcast_in_dim.6), calls=%async_computation | async-start | bytes 1638400 | tf_op jit(solution)/shard_map/all_to_all | solution.py:50
  15.1 1.2 %copy-start.1 = (bf16[256,3072]{1,0:T(8,128)(2,1)}, bf16[256,3072]{1,0:T(8,128)(2,1)S(1)}, u32[]{:S(2)}) copy-start(bf16[256,3072]{1,0:T(8,128)(2,1)S(1)} %convolution_convert_fusion) | copy-start | bytes 4718596
  15.1 4.0 %copy-start.10 = (s32[1,256,2]{1,2,0:T(2,128)S(1)}, s32[1,256,2]{1,2,0:T(2,128)}, u32[]{:S(2)}) copy-start(s32[1,256,2]{1,2,0:T(2,128)} %param.12) | copy-start | bytes 6148
  15.1 4.1 %copy-start.4 = (bf16[1,16,3072]{2,1,0:T(8,128)(2,1)S(1)}, bf16[1,16,3072]{2,1,0:T(8,128)(2,1)}, u32[]{:S(2)}) copy-start(bf16[1,16,3072]{2,1,0:T(8,128)(2,1)} %param.10) | copy-start | bytes 294916
  15.1 4.3 %copy-start.6 = (bf16[1,3072,8]{1,2,0:T(8,128)(2,1)S(1)}, bf16[1,3072,8]{1,2,0:T(8,128)(2,1)}, u32[]{:S(2)}) copy-start(bf16[1,3072,8]{1,2,0:T(8,128)(2,1)} %param.18) | copy-start | bytes 147460
  15.1 5.0 %copy-start.7 = (s32[1,256,2]{1,2,0:T(2,128)S(1)}, s32[1,256,2]{1,2,0:T(2,128)}, u32[]{:S(2)}) copy-start(s32[1,256,2]{1,2,0:T(2,128)} %param.15) | copy-start | bytes 6148
  17.2 4.5 %collective-permute-start = (bf16[8,16,3072]{2,1,0:T(8,128)(2,1)}, bf16[8,16,3072]{2,1,0:T(8,128)(2,1)}, u32[]{:S(2)}, u32[]{:S(2)}) collective-permute-start(bf16[8,16,3072]{2,1,0:T(8,128)(2,1)} %fusion.7), channel_id=1, source_target_pairs={{0,1},{1,0},{2,3},{3,2},{4,5},{5,4},{6,7},{7,6},{8,9},{9,8},{10,11... | collective-permute-start | bytes 2359304 | tf_op jit(solution)/shard_map/ppermute | solution.py:55
  19.6 20.1 %copy-start.3 = (bf16[1,16,3072]{2,1,0:T(8,128)(2,1)S(1)}, bf16[1,16,3072]{2,1,0:T(8,128)(2,1)}, u32[]{:S(2)}) copy-start(bf16[1,16,3072]{2,1,0:T(8,128)(2,1)} %param.13) | copy-start | bytes 294916
  36.6 11.6 %collective-permute-start.1 = (bf16[8,1,16,3200]{3,2,0,1:T(8,128)(2,1)}, bf16[8,1,16,3200]{3,2,0,1:T(8,128)(2,1)}, u32[]{:S(2)}, u32[]{:S(2)}) collective-permute-start(bf16[8,1,16,3200]{3,2,0,1:T(8,128)(2,1)} %bitcast.18), channel_id=1, source_target_pairs={{0,1},{1,0},{2,3},{3,2},{4,5},{5,4},{6,7},{7,6},{8,9},{9,8},{10,11... | collective-permute-start | bytes 2457608 | tf_op jit(solution)/shard_map/ppermute | solution.py:60
  41.4 28.3 %all-to-all-start.1 = ((bf16[8,16,3072]{2,1,0:T(8,128)(2,1)}), bf16[8,16,3072]{2,1,0:T(8,128)(2,1)}, u32[]{:S(2)}, u32[]{:S(2)}) async-start(bf16[8,16,3072]{2,1,0:T(8,128)(2,1)} %fusion.5), calls=%async_computation.1 | async-start | bytes 1572864 | tf_op jit(solution)/shard_map/all_to_all | solution.py:58
  50.4 2.9 %copy-start.8 = (s32[256]{0:T(256)S(1)}, s32[256]{0:T(256)}, u32[]{:S(2)}) copy-start(s32[256]{0:T(256)} %broadcast_minimum_fusion) | copy-start | bytes 3076
  50.6 1.2 %copy-start.2 = (bf16[8,2,16,3200]{3,2,1,0:T(8,128)(2,1)}, bf16[8,2,16,3200]{3,2,1,0:T(8,128)(2,1)S(1)}, u32[]{:S(2)}) copy-start(bf16[8,2,16,3200]{3,2,1,0:T(8,128)(2,1)S(1)} %copy.54) | copy-start | bytes 4915204
  53.3 23.1 %copy-start.9 = (f32[16]{0:T(128)S(1)}, f32[16]{0:T(128)}, u32[]{:S(2)}) copy-start(f32[16]{0:T(128)} %fusion.51) | copy-start | bytes 196
  53.3 29.2 %copy-start.12 = (f32[16]{0:T(128)S(1)}, f32[16]{0:T(128)}, u32[]{:S(2)}) copy-start(f32[16]{0:T(128)} %copy-done.11) | copy-start | bytes 196
  70.4 12.2 %all-to-all-start.2 = ((f32[16,1,16]{2,1,0:T(1,128)}), f32[16,1,16]{2,1,0:T(1,128)S(1)}, u32[]{:S(2)}, u32[]{:S(2)}) async-start(f32[16,1,16]{2,1,0:T(1,128)} %all_to_all.19), calls=%async_computation.2 | async-start | bytes 16384 | tf_op jit(solution)/shard_map/all_to_all | solution.py:76
  77.1 8.4 %collective-permute-start.2 = (bf16[1,16,3072]{2,1,0:T(8,128)(2,1)}, bf16[1,16,3072]{2,1,0:T(8,128)(2,1)S(1)}, u32[]{:S(2)}, u32[]{:S(2)}) collective-permute-start(bf16[1,16,3072]{2,1,0:T(8,128)(2,1)} %fusion.29), channel_id=1, source_target_pairs={{0,16},{16,32},{32,48},{48,64},{64,80},{80,96},{96,112},{112,128},... | collective-permute-start | bytes 294920 | tf_op jit(solution)/shard_map/ppermute | solution.py:10
  83.6 9.8 %collective-permute-start.3 = (bf16[1,16,3072]{2,1,0:T(8,128)(2,1)S(1)}, bf16[1,16,3072]{2,1,0:T(8,128)(2,1)S(1)}, u32[]{:S(2)}, u32[]{:S(2)}) collective-permute-start(bf16[1,16,3072]{2,1,0:T(8,128)(2,1)S(1)} %fusion.35), channel_id=1, source_target_pairs={{16,0},{32,16},{48,32},{64,48},{80,64},{96,80},{112,96},{128,112},... | collective-permute-start | bytes 294920 | tf_op jit(solution)/shard_map/ppermute | solution.py:10

commit v10 on v9

--- a/solution.py
+++ b/solution.py
@@ -72,8 +72,12 @@
     )
     dact = (coef_b[:, None] * back_up).astype(jnp.bfloat16)
     dprob_part = jnp.sum(act_bwd.astype(jnp.float32) * back_up, axis=1)
-    dprob_part, got = lax.optimization_barrier((dprob_part, got))
-    dprob_got = lax.all_to_all(dprob_part.reshape(groups, own_rows), ("ety", "etc"), 0, 0, tiled=True)
+    halves = dprob_part.reshape(chips, 2, own_rows)
+    keep = jnp.where(core == 0, halves[:, 0], halves[:, 1])
+    give = jnp.where(core == 0, halves[:, 1], halves[:, 0])
+    pair_d = keep + lax.ppermute(give, "etc", [(0, 1), (1, 0)])
+    pair_d, got = lax.optimization_barrier((pair_d, got))
+    dprob_got = lax.all_to_all(pair_d, "ety", 0, 0, tiled=True)
     dprob_mine = jnp.sum(dprob_got, axis=0)
     z_sum = jnp.sum(got.reshape(chips, own_rows, width).astype(jnp.float32), axis=0)
 

time: 95.5 us -> 93.6 us (0.980)
  waiting for transfers between devices: 33.9 us -> 29.1 us
  starting transfers between devices: 29 us -> 31.1 us
    all_to_all x1, waiting for transfers between devices: 13.1 us -> 8.99 us  [layer(): lax.all_to_all(pair_z.reshape(chips * own_rows, width), 'ety', 0, 0, tile...]
    ppermute x0 -> x1, starting transfers between devices: none -> 2.12 us  [layer(): pair_d = keep + lax.ppermute(give, 'etc', [(0, 1), (1, 0)])]
  transfers between devices with their start and end apart: 7 -> 8, of which waited for: 4 -> 4; matrix products, arithmetic and copies ran while one was open for 22% -> 24% of each run, Pallas kernels for 0% -> 0%
where the time goes in v10:
time: 93.6 us; the launch traced here: 92.8 us
  starting transfers between devices  31.1 us (33%)
  waiting for transfers between devices  29.1 us (31%)
  other arithmetic  16.7 us (18%)
  matrix products  7.87 us (8%)
  local copies, waits for them, and re-layouts  7.07 us (8%)
    all_to_all x1, waiting for transfers between devices, layer(): lax.all_to_all(tiled, 'ety', 0, 0, tiled=True)  12 us
    all_to_all x1, waiting for transfers between devices, layer(): lax.all_to_all(pair_z.reshape(chips * own_rows, width), 'ety', 0, 0, tile...  8.99 us
    ppermute x2, waiting for transfers between devices, from_behind(): lax.ppermute(value, axis, [(source, source + steps) for source in range(f...  7.89 us
    all_to_all x1, starting transfers between devices, layer(): lax.all_to_all(tiled, 'ety', 0, 0, tiled=True)  7.55 us
    ppermute x2, starting transfers between devices, from_behind(): lax.ppermute(value, axis, [(source, source + steps) for source in range(f...  7.31 us
    all_to_all x1, starting transfers between devices, layer(): lax.all_to_all(pair_z.reshape(chips * own_rows, width), 'ety', 0, 0, tile...  5.55 us
    all_to_all x1, starting transfers between devices, layer(): dprob_got = lax.all_to_all(pair_d, 'ety', 0, 0, tiled=True)  4.71 us
    unnamed x32, local copies, waits for them, and re-layouts  4.6 us
  transfers between devices with their start and end apart: 8, of which 4 were waited for; matrix products, arithmetic and copies ran while one was open for 24% of the time, Pallas kernels for 0%

profile of v10, /device:TPU:206, one launch (start us, length us, event | category | flops | bytes accessed | tf_op | source)
XLA Modules:
  0.0 92.8 jit_solution(1081502652006244243)
XLA Ops:
  0.7 0.9 %dynamic-slice_reduce_fusion = (s32[16]{0:T(128)S(1)}, s32[16]{0:T(128)S(1)}) fusion(s32[1,256,2]{1,2,0:T(2,128)} %param.15, s32[]{:T(128)S(6)} %select_n.50, s32[1,256,2]{1,2,0:T(2,128)} %param.12), kind=kLoop, calls=%fused_computation.75 | loop fusion | flops 32 | bytes 388 | tf_op jit(solution)/shard_map/reduce_sum | solution.py:23
  1.6 1.1 %fusion.23 = f32[16]{0:T(128)S(1)} fusion(bf16[1,16,3072]{2,1,0:T(8,128)(2,1)} %param.13), kind=kLoop, calls=%fused_computation.40 | loop fusion | flops 147440 | bytes 98368 | tf_op jit(solution)/shard_map/reduce_sum | solution.py:15
  2.7 0.7 mul.196
  3.5 1.1 %select_reduce_fusion.1 = (f32[16]{0:T(128)S(1)}, bf16[16,8]{0,1:T(8,128)(2,1)S(1)}) fusion(s32[16]{0:T(128)S(1)} %broadcast_minimum_fusion.1, bf16[1,3072,8]{1,2,0:T(8,128)(2,1)} %param.18, bf16[1,16,3072]{2,1,0:T(8,128)(2,1)} %param.13, f32[16]{0:T(128)S(1)} %add_rsqrt_fusion, f32[3072]{0:T(1024)S(1)} %bitcast.151), kind=kOutput, calls=%fused_computation.61 | convolution fusion | flops 983664 | bytes 160192 | tf_op jit(solution)/shard_map/dot_general | solution.py:17
  4.7 0.9 fusion.30
  5.6 1.0 %broadcast_in_dim.6 = bf16[8,16,3200]{2,1,0:T(8,128)(2,1)} broadcast(bf16[16,3200]{1,0:T(8,128)(2,1)S(1)} %fusion.30), dimensions={1,2} | broadcast | bytes 921600 | tf_op jit(solution)/shard_map/broadcast_in_dim | solution.py:49
  6.5 7.5 %all-to-all-start = ((bf16[8,16,3200]{2,1,0:T(8,128)(2,1)}), bf16[8,16,3200]{2,1,0:T(8,128)(2,1)}, u32[]{:S(2)}, u32[]{:S(2)}) async-start(bf16[8,16,3200]{2,1,0:T(8,128)(2,1)} %broadcast_in_dim.6), calls=%async_computation | async-start | bytes 1638400 | tf_op jit(solution)/shard_map/all_to_all | solution.py:50
  14.1 1.0 %convolution_convert_fusion = bf16[256,3072]{1,0:T(8,128)(2,1)S(1)} fusion(bf16[1,512,3072]{2,1,0:T(8,128)(2,1)S(1)} %copy-done, bf16[1,256,512]{2,1,0:T(8,128)(2,1)S(1)} %copy-done.5), kind=kOutput, calls=%fused_computation | convolution fusion | flops 806092800 | bytes 4980736 | tf_op jit(solution)/shard_map/dot_general | solution.py:51
  15.2 1.1 %copy-done.1 = bf16[256,3072]{1,0:T(8,128)(2,1)} copy-done((bf16[256,3072]{1,0:T(8,128)(2,1)}, bf16[256,3072]{1,0:T(8,128)(2,1)S(1)}, u32[]{:S(2)}) %copy-start.1) | copy-done | bytes 1572888
  16.3 1.0 %fusion.7 = bf16[8,16,3072]{2,1,0:T(8,128)(2,1)} fusion(pred[]{:T(512)S(6)} %eq.65, bf16[8,2,16,3072]{3,2,1,0:T(8,128)(2,1)S(1)} %bitcast.145), kind=kLoop, calls=%fused_computation.15 | loop fusion | flops 393216 | bytes 2359297 | tf_op jit(solution)/shard_map/jit(_where)/select_n | solution.py:54
  17.2 1.9 %collective-permute-start = (bf16[8,16,3072]{2,1,0:T(8,128)(2,1)}, bf16[8,16,3072]{2,1,0:T(8,128)(2,1)}, u32[]{:S(2)}, u32[]{:S(2)}) collective-permute-start(bf16[8,16,3072]{2,1,0:T(8,128)(2,1)} %fusion.7), channel_id=1, source_target_pairs={{0,1},{1,0},{2,3},{3,2},{4,5},{5,4},{6,7},{7,6},{8,9},{9,8},{10,11... | collective-permute-start | bytes 2359304 | tf_op jit(solution)/shard_map/ppermute | solution.py:55
  21.7 2.9 %fusion.5 = bf16[8,16,3072]{2,1,0:T(8,128)(2,1)} fusion(bf16[8,16,3072]{2,1,0:T(8,128)(2,1)} %collective-permute-done, pred[]{:T(512)S(6)} %eq.65, bf16[8,2,16,3072]{3,2,1,0:T(8,128)(2,1)} %bitcast.146), kind=kLoop, calls=%fused_computation.10 | loop fusion | flops 1966080 | bytes 3145729 | tf_op jit(solution)/shard_map/convert_element_type | solution.py:56
  24.6 12.0 %all-to-all-done = bf16[8,16,3200]{2,1,0:T(8,128)(2,1)} async-done(((bf16[8,16,3200]{2,1,0:T(8,128)(2,1)}), bf16[8,16,3200]{2,1,0:T(8,128)(2,1)}, u32[]{:S(2)}, u32[]{:S(2)}) %all-to-all-start) | async-done | bytes 819232 | tf_op jit(solution)/shard_map/all_to_all | solution.py:50
  36.6 1.9 %collective-permute-start.1 = (bf16[8,1,16,3200]{3,2,0,1:T(8,128)(2,1)}, bf16[8,1,16,3200]{3,2,0,1:T(8,128)(2,1)}, u32[]{:S(2)}, u32[]{:S(2)}) collective-permute-start(bf16[8,1,16,3200]{3,2,0,1:T(8,128)(2,1)} %bitcast.18), channel_id=1, source_target_pairs={{0,1},{1,0},{2,3},{3,2},{4,5},{5,4},{6,7},{7,6},{8,9},{9,8},{10,11... | collective-permute-start | bytes 2457608 | tf_op jit(solution)/shard_map/ppermute | solution.py:60
  38.5 1.7 %fusion.17 = (f32[16]{0:T(128)}, f32[16,3072]{1,0:T(8,128)S(1)}) fusion(bf16[1,16,3072]{2,1,0:T(8,128)(2,1)S(1)} %copy-done.3, f32[16]{0:T(128)} %copy-done.11, f32[3072]{0:T(1024)S(1)} %bitcast.153, bf16[1,3072,8]{1,2,0:T(8,128)(2,1)} %param.18, s32[16]{0:T(128)} %copy-done.13, f32[3072]{0:T(1024)S(1)} %bitcast.154), kind=kOutput, calls=%fused_computation.34 | convolution fusion | flops 1081456 | bytes 368832 | tf_op jit(solution)/shard_map/dot_general | solution.py:91
  40.2 5.5 %all-to-all-start.1 = ((bf16[8,16,3072]{2,1,0:T(8,128)(2,1)}), bf16[8,16,3072]{2,1,0:T(8,128)(2,1)}, u32[]{:S(2)}, u32[]{:S(2)}) async-start(bf16[8,16,3072]{2,1,0:T(8,128)(2,1)} %fusion.5), calls=%async_computation.1 | async-start | bytes 1572864 | tf_op jit(solution)/shard_map/all_to_all | solution.py:58
  45.8 2.3 %maximum_select_fusion = bf16[8,2,16,3200]{3,2,0,1:T(8,128)(2,1)S(1)} fusion(bf16[8,1,16,3200]{3,2,0,1:T(8,128)(2,1)} %collective-permute-done.1, bf16[8,1,16,3200]{3,2,0,1:T(8,128)(2,1)} %bitcast.18, pred[]{:T(512)S(6)} %eq.65), kind=kLoop, calls=%fused_computation.6 | loop fusion | flops 2457600 | bytes 3276801 | tf_op jit(solution)/shard_map/jit(_where)/select_n | solution.py:61
  48.2 1.2 %copy-done.2 = bf16[8,2,16,3200]{3,2,1,0:T(8,128)(2,1)} copy-done((bf16[8,2,16,3200]{3,2,1,0:T(8,128)(2,1)}, bf16[8,2,16,3200]{3,2,1,0:T(8,128)(2,1)S(1)}, u32[]{:S(2)}) %copy-start.2) | copy-done | bytes 1638424
  50.0 0.9 copy.50
  51.0 3.8 %fusion.10 = (bf16[1,256,512]{2,1,0:T(8,128)(2,1)}, f32[256]{0:T(256)}) fusion(f32[256]{0:T(256)S(1)} %bitcast.159, bf16[1,256,512]{2,1,0:T(8,128)(2,1)} %param.14, bf16[1,512,3072]{2,1,0:T(8,128)(2,1)S(1)} %copy-done, bf16[256,3200]{1,0:T(8,128)(2,1)} %bitcast.148), kind=kOutput, calls=%fused_computation.24 | convolution fusion | flops 805961472 | bytes 5244928 | tf_op jit(solution)/shard_map/dot_general | solution.py:70
  54.8 0.8 reshape.180
  55.6 2.1 %collective-permute-start.2 = (f32[8,16]{1,0:T(8,128)S(1)}, f32[8,16]{1,0:T(8,128)S(1)}, u32[]{:S(2)}, u32[]{:S(2)}) collective-permute-start(f32[8,16]{1,0:T(8,128)S(1)} %bitcast.157), channel_id=1, source_target_pairs={{0,1},{1,0},{2,3},{3,2},{4,5},{5,4},{6,7},{7,6},{8,9},{9,8},{10,11... | collective-permute-start | bytes 1544 | tf_op jit(solution)/shard_map/ppermute | solution.py:78
  57.7 1.2 %broadcast_multiply_fusion = f32[16]{0:T(128)} fusion(f32[16]{0:T(128)} %get-tuple-element.17), kind=kLoop, calls=%fused_computation.94 | loop fusion | flops 16 | bytes 128 | tf_op jit(solution)/shard_map/div | solution.py:98
  59.5 9.0 %all-to-all-done.1 = bf16[8,16,3072]{2,1,0:T(8,128)(2,1)} async-done(((bf16[8,16,3072]{2,1,0:T(8,128)(2,1)}), bf16[8,16,3072]{2,1,0:T(8,128)(2,1)}, u32[]{:S(2)}, u32[]{:S(2)}) %all-to-all-start.1) | async-done | bytes 786464 | tf_op jit(solution)/shard_map/all_to_all | solution.py:58
  68.5 4.7 %all-to-all-start.2 = ((f32[8,1,16]{2,1,0:T(1,128)}), f32[8,1,16]{2,1,0:T(1,128)S(1)}, u32[]{:S(2)}, u32[]{:S(2)}) async-start(f32[8,1,16]{2,1,0:T(1,128)} %bitcast.26), calls=%async_computation.2 | async-start | bytes 8192 | tf_op jit(solution)/shard_map/all_to_all | solution.py:80
  73.2 1.3 %convert_reduce_fusion = f32[16,3072]{1,0:T(8,128)S(1)} fusion(bf16[8,16,3072]{2,1,0:T(8,128)(2,1)} %bitcast.39), kind=kLoop, calls=%fused_computation.8 | loop fusion | flops 737280 | bytes 983040 | tf_op jit(solution)/shard_map/reduce_sum | solution.py:82
  74.5 0.7 fusion.29
  75.2 5.4 %collective-permute-start.3 = (bf16[1,16,3072]{2,1,0:T(8,128)(2,1)}, bf16[1,16,3072]{2,1,0:T(8,128)(2,1)S(1)}, u32[]{:S(2)}, u32[]{:S(2)}) collective-permute-start(bf16[1,16,3072]{2,1,0:T(8,128)(2,1)} %fusion.29), channel_id=1, source_target_pairs={{0,16},{16,32},{32,48},{48,64},{64,80},{80,96},{96,112},{112,128},... | collective-permute-start | bytes 294920 | tf_op jit(solution)/shard_map/ppermute | solution.py:10
  80.7 1.0 %fusion.35 = bf16[1,16,3072]{2,1,0:T(8,128)(2,1)S(1)} fusion(f32[16,3072]{1,0:T(8,128)S(1)} %get-tuple-element.18, bf16[1,16,3072]{2,1,0:T(8,128)(2,1)S(1)} %copy-done.3, f32[16]{0:T(128)} %broadcast_multiply_fusion, f32[16]{0:T(128)S(1)} %copy-done.12, f32[16]{0:T(128)} %fusion.45, f32[16]{0:T(128)S(1)} %reduce_sum.159, bf16[1,16,3072]{2,1,0:T(8,128)(2,1)} %param.16), kind=kLoop, calls=%fused_computation.51 | loop fusion | flops 442368 | bytes 491776 | tf_op jit(solution)/shard_map/broadcast_in_dim | solution.py:103
  81.7 1.9 %collective-permute-start.4 = (bf16[1,16,3072]{2,1,0:T(8,128)(2,1)S(1)}, bf16[1,16,3072]{2,1,0:T(8,128)(2,1)S(1)}, u32[]{:S(2)}, u32[]{:S(2)}) collective-permute-start(bf16[1,16,3072]{2,1,0:T(8,128)(2,1)S(1)} %fusion.35), channel_id=1, source_target_pairs={{16,0},{32,16},{48,32},{64,48},{80,64},{96,80},{112,96},{128,112},... | collective-permute-start | bytes 294920 | tf_op jit(solution)/shard_map/ppermute | solution.py:10
  83.6 7.9 %collective-permute-done.4 = bf16[1,16,3072]{2,1,0:T(8,128)(2,1)S(1)} collective-permute-done((bf16[1,16,3072]{2,1,0:T(8,128)(2,1)S(1)}, bf16[1,16,3072]{2,1,0:T(8,128)(2,1)S(1)}, u32[]{:S(2)}, u32[]{:S(2)}) %collective-permute-start.4) | collective-permute-done | bytes 98336 | tf_op jit(solution)/shard_map/ppermute | solution.py:10
  91.5 0.6 copy.54
  (56 shorter events, 4.8 us)
Async XLA Ops:
  0.6 13.5 %copy-start = (bf16[1,512,3072]{2,1,0:T(8,128)(2,1)S(1)}, bf16[1,512,3072]{2,1,0:T(8,128)(2,1)}, u32[]{:S(2)}) copy-start(bf16[1,512,3072]{2,1,0:T(8,128)(2,1)} %param.19) | copy-start | bytes 9437188
  0.6 13.4 %copy-start.5 = (bf16[1,256,512]{2,1,0:T(8,128)(2,1)S(1)}, bf16[1,256,512]{2,1,0:T(8,128)(2,1)}, u32[]{:S(2)}) copy-start(bf16[1,256,512]{2,1,0:T(8,128)(2,1)} %param.11) | copy-start | bytes 786436
  1.6 13.5 %copy-start.13 = (s32[16]{0:T(128)}, s32[16]{0:T(128)S(1)}, u32[]{:S(2)}) copy-start(s32[16]{0:T(128)S(1)} %broadcast_minimum_fusion.1) | copy-start | bytes 196
  2.7 1.9 %copy-start.11 = (f32[16]{0:T(128)}, f32[16]{0:T(128)S(1)}, u32[]{:S(2)}) copy-start(f32[16]{0:T(128)S(1)} %add_rsqrt_fusion) | copy-start | bytes 196
  6.5 30.0 %all-to-all-start = ((bf16[8,16,3200]{2,1,0:T(8,128)(2,1)}), bf16[8,16,3200]{2,1,0:T(8,128)(2,1)}, u32[]{:S(2)}, u32[]{:S(2)}) async-start(bf16[8,16,3200]{2,1,0:T(8,128)(2,1)} %broadcast_in_dim.6), calls=%async_computation | async-start | bytes 1638400 | tf_op jit(solution)/shard_map/all_to_all | solution.py:50
  15.1 1.2 %copy-start.1 = (bf16[256,3072]{1,0:T(8,128)(2,1)}, bf16[256,3072]{1,0:T(8,128)(2,1)S(1)}, u32[]{:S(2)}) copy-start(bf16[256,3072]{1,0:T(8,128)(2,1)S(1)} %convolution_convert_fusion) | copy-start | bytes 4718596
  15.1 4.0 %copy-start.7 = (s32[1,256,2]{1,2,0:T(2,128)S(1)}, s32[1,256,2]{1,2,0:T(2,128)}, u32[]{:S(2)}) copy-start(s32[1,256,2]{1,2,0:T(2,128)} %param.15) | copy-start | bytes 6148
  15.1 4.6 %copy-start.4 = (bf16[1,16,3072]{2,1,0:T(8,128)(2,1)S(1)}, bf16[1,16,3072]{2,1,0:T(8,128)(2,1)}, u32[]{:S(2)}) copy-start(bf16[1,16,3072]{2,1,0:T(8,128)(2,1)} %param.10) | copy-start | bytes 294916
  15.1 4.9 %copy-start.10 = (s32[1,256,2]{1,2,0:T(2,128)S(1)}, s32[1,256,2]{1,2,0:T(2,128)}, u32[]{:S(2)}) copy-start(s32[1,256,2]{1,2,0:T(2,128)} %param.12) | copy-start | bytes 6148
  15.1 5.0 %copy-start.6 = (bf16[1,3072,8]{1,2,0:T(8,128)(2,1)S(1)}, bf16[1,3072,8]{1,2,0:T(8,128)(2,1)}, u32[]{:S(2)}) copy-start(bf16[1,3072,8]{1,2,0:T(8,128)(2,1)} %param.18) | copy-start | bytes 147460
  17.2 4.5 %collective-permute-start = (bf16[8,16,3072]{2,1,0:T(8,128)(2,1)}, bf16[8,16,3072]{2,1,0:T(8,128)(2,1)}, u32[]{:S(2)}, u32[]{:S(2)}) collective-permute-start(bf16[8,16,3072]{2,1,0:T(8,128)(2,1)} %fusion.7), channel_id=1, source_target_pairs={{0,1},{1,0},{2,3},{3,2},{4,5},{5,4},{6,7},{7,6},{8,9},{9,8},{10,11... | collective-permute-start | bytes 2359304 | tf_op jit(solution)/shard_map/ppermute | solution.py:55
  20.3 18.2 %copy-start.3 = (bf16[1,16,3072]{2,1,0:T(8,128)(2,1)S(1)}, bf16[1,16,3072]{2,1,0:T(8,128)(2,1)}, u32[]{:S(2)}) copy-start(bf16[1,16,3072]{2,1,0:T(8,128)(2,1)} %param.13) | copy-start | bytes 294916
  36.6 9.2 %collective-permute-start.1 = (bf16[8,1,16,3200]{3,2,0,1:T(8,128)(2,1)}, bf16[8,1,16,3200]{3,2,0,1:T(8,128)(2,1)}, u32[]{:S(2)}, u32[]{:S(2)}) collective-permute-start(bf16[8,1,16,3200]{3,2,0,1:T(8,128)(2,1)} %bitcast.18), channel_id=1, source_target_pairs={{0,1},{1,0},{2,3},{3,2},{4,5},{5,4},{6,7},{7,6},{8,9},{9,8},{10,11... | collective-permute-start | bytes 2457608 | tf_op jit(solution)/shard_map/ppermute | solution.py:60
  40.2 28.3 %all-to-all-start.1 = ((bf16[8,16,3072]{2,1,0:T(8,128)(2,1)}), bf16[8,16,3072]{2,1,0:T(8,128)(2,1)}, u32[]{:S(2)}, u32[]{:S(2)}) async-start(bf16[8,16,3072]{2,1,0:T(8,128)(2,1)} %fusion.5), calls=%async_computation.1 | async-start | bytes 1572864 | tf_op jit(solution)/shard_map/all_to_all | solution.py:58
  48.1 2.9 %copy-start.8 = (s32[256]{0:T(256)S(1)}, s32[256]{0:T(256)}, u32[]{:S(2)}) copy-start(s32[256]{0:T(256)} %broadcast_minimum_fusion) | copy-start | bytes 3076
  48.2 1.2 %copy-start.2 = (bf16[8,2,16,3200]{3,2,1,0:T(8,128)(2,1)}, bf16[8,2,16,3200]{3,2,1,0:T(8,128)(2,1)S(1)}, u32[]{:S(2)}) copy-start(bf16[8,2,16,3200]{3,2,1,0:T(8,128)(2,1)S(1)} %copy.46) | copy-start | bytes 4915204
  51.0 23.5 %copy-start.9 = (f32[16]{0:T(128)S(1)}, f32[16]{0:T(128)}, u32[]{:S(2)}) copy-start(f32[16]{0:T(128)} %fusion.51) | copy-start | bytes 196
  51.0 29.7 %copy-start.12 = (f32[16]{0:T(128)S(1)}, f32[16]{0:T(128)}, u32[]{:S(2)}) copy-start(f32[16]{0:T(128)} %copy-done.11) | copy-start | bytes 196
  55.6 3.3 %collective-permute-start.2 = (f32[8,16]{1,0:T(8,128)S(1)}, f32[8,16]{1,0:T(8,128)S(1)}, u32[]{:S(2)}, u32[]{:S(2)}) collective-permute-start(f32[8,16]{1,0:T(8,128)S(1)} %bitcast.157), channel_id=1, source_target_pairs={{0,1},{1,0},{2,3},{3,2},{4,5},{5,4},{6,7},{7,6},{8,9},{9,8},{10,11... | collective-permute-start | bytes 1544 | tf_op jit(solution)/shard_map/ppermute | solution.py:78
  68.5 12.1 %all-to-all-start.2 = ((f32[8,1,16]{2,1,0:T(1,128)}), f32[8,1,16]{2,1,0:T(1,128)S(1)}, u32[]{:S(2)}, u32[]{:S(2)}) async-start(f32[8,1,16]{2,1,0:T(1,128)} %bitcast.26), calls=%async_computation.2 | async-start | bytes 8192 | tf_op jit(solution)/shard_map/all_to_all | solution.py:80
  75.2 8.4 %collective-permute-start.3 = (bf16[1,16,3072]{2,1,0:T(8,128)(2,1)}, bf16[1,16,3072]{2,1,0:T(8,128)(2,1)S(1)}, u32[]{:S(2)}, u32[]{:S(2)}) collective-permute-start(bf16[1,16,3072]{2,1,0:T(8,128)(2,1)} %fusion.29), channel_id=1, source_target_pairs={{0,16},{16,32},{32,48},{48,64},{64,80},{80,96},{96,112},{112,128},... | collective-permute-start | bytes 294920 | tf_op jit(solution)/shard_map/ppermute | solution.py:10
  81.7 9.8 %collective-permute-start.4 = (bf16[1,16,3072]{2,1,0:T(8,128)(2,1)S(1)}, bf16[1,16,3072]{2,1,0:T(8,128)(2,1)S(1)}, u32[]{:S(2)}, u32[]{:S(2)}) collective-permute-start(bf16[1,16,3072]{2,1,0:T(8,128)(2,1)S(1)} %fusion.35), channel_id=1, source_target_pairs={{16,0},{32,16},{48,32},{64,48},{80,64},{96,80},{112,96},{128,112},... | collective-permute-start | bytes 294920 | tf_op jit(solution)/shard_map/ppermute | solution.py:10

commit v11 on v10

--- a/solution.py
+++ b/solution.py
@@ -77,8 +77,16 @@
     give = jnp.where(core == 0, halves[:, 1], halves[:, 0])
     pair_d = keep + lax.ppermute(give, "etc", [(0, 1), (1, 0)])
     pair_d, got = lax.optimization_barrier((pair_d, got))
-    dprob_got = lax.all_to_all(pair_d, "ety", 0, 0, tiled=True)
-    dprob_mine = jnp.sum(dprob_got, axis=0)
+    chip = lax.axis_index("ety")
+    span = chips // 2
+    while span >= 1:
+        bit = (chip // span) % 2
+        split = pair_d.reshape(2, -1, own_rows)
+        keep = jnp.where(bit == 0, split[0], split[1])
+        give = jnp.where(bit == 0, split[1], split[0])
+        pair_d = keep + lax.ppermute(give, "ety", [(i, i ^ span) for i in range(chips)])
+        span //= 2
+    dprob_mine = pair_d.reshape(own_rows)
     z_sum = jnp.sum(got.reshape(chips, own_rows, width).astype(jnp.float32), axis=0)
 
     ids_f_own = lax.dynamic_slice_in_dim(ids_fwd, first_row, own_rows, 0)

time: 93.6 us -> 112 us (1.20)
  the two profiles are of different devices: /device:TPU:206 before, /device:TPU:198 now
where the time goes in v11:
time: 112 us; the launch traced here: 111 us
  waiting for transfers between devices  39.9 us (36%)
  starting transfers between devices  32.1 us (29%)
  other arithmetic  23.5 us (21%)
  matrix products  7.88 us (7%)
  local copies, waits for them, and re-layouts  6.4 us (6%)
    all_to_all x1, waiting for transfers between devices, layer(): lax.all_to_all(pair_z.reshape(chips * own_rows, width), 'ety', 0, 0, tile...  12.3 us
    all_to_all x1, waiting for transfers between devices, layer(): lax.all_to_all(tiled, 'ety', 0, 0, tiled=True)  10 us
    ppermute x3, waiting for transfers between devices, layer(): lax.ppermute(give, 'ety', [(i, i ^ span) for i in range(chips)])  8.96 us
    ppermute x2, waiting for transfers between devices, from_behind(): lax.ppermute(value, axis, [(source, source + steps) for source in range(f...  7.89 us
    ppermute x2, starting transfers between devices, from_behind(): lax.ppermute(value, axis, [(source, source + steps) for source in range(f...  7.33 us
    ppermute x3, starting transfers between devices, layer(): lax.ppermute(give, 'ety', [(i, i ^ span) for i in range(chips)])  7.24 us
    all_to_all x1, starting transfers between devices, layer(): lax.all_to_all(tiled, 'ety', 0, 0, tiled=True)  7.1 us
    unnamed x36, local copies, waits for them, and re-layouts  4.6 us
  transfers between devices with their start and end apart: 10, of which 6 were waited for; matrix products, arithmetic and copies ran while one was open for 25% of the time, Pallas kernels for 0%

profile of v11, /device:TPU:198, one launch (start us, length us, event | category | flops | bytes accessed | tf_op | source)
XLA Modules:
  0.0 110.8 jit_solution(14471271282378660367)
XLA Ops:
  0.7 1.4 %dynamic-slice_reduce_fusion = (s32[16]{0:T(128)S(1)}, s32[16]{0:T(128)}) fusion(s32[1,256,2]{1,2,0:T(2,128)} %param.15, s32[]{:T(128)S(6)} %select_n.109, s32[1,256,2]{1,2,0:T(2,128)} %param.12), kind=kLoop, calls=%fused_computation.81 | loop fusion | flops 32 | bytes 388 | tf_op jit(solution)/shard_map/reduce_sum | solution.py:23
  2.1 1.0 fusion.23
  3.9 1.7 %select_reduce_fusion.1 = (f32[16]{0:T(128)}, bf16[16,8]{0,1:T(8,128)(2,1)S(1)}) fusion(s32[16]{0:T(128)S(1)} %broadcast_minimum_fusion.1, bf16[1,3072,8]{1,2,0:T(8,128)(2,1)} %param.18, bf16[1,16,3072]{2,1,0:T(8,128)(2,1)} %param.13, f32[16]{0:T(128)S(1)} %add_rsqrt_fusion, f32[3072]{0:T(1024)S(1)} %bitcast.150), kind=kOutput, calls=%fused_computation.61 | convolution fusion | flops 983664 | bytes 160192 | tf_op jit(solution)/shard_map/dot_general | solution.py:17
  7.6 7.1 %all-to-all-start = ((bf16[8,16,3200]{2,1,0:T(8,128)(2,1)}), bf16[8,16,3200]{2,1,0:T(8,128)(2,1)}, u32[]{:S(2)}, u32[]{:S(2)}) async-start(bf16[8,16,3200]{2,1,0:T(8,128)(2,1)} %broadcast_in_dim.6), calls=%async_computation | async-start | bytes 1638400 | tf_op jit(solution)/shard_map/all_to_all | solution.py:50
  14.7 1.0 convolution_convert_fusion
  15.8 1.1 copy-done.1
  17.8 1.9 %collective-permute-start = (bf16[8,16,3072]{2,1,0:T(8,128)(2,1)}, bf16[8,16,3072]{2,1,0:T(8,128)(2,1)}, u32[]{:S(2)}, u32[]{:S(2)}) collective-permute-start(bf16[8,16,3072]{2,1,0:T(8,128)(2,1)} %fusion.7), channel_id=1, source_target_pairs={{0,1},{1,0},{2,3},{3,2},{4,5},{5,4},{6,7},{7,6},{8,9},{9,8},{10,11... | collective-permute-start | bytes 2359304 | tf_op jit(solution)/shard_map/ppermute | solution.py:55
  22.0 1.2 %broadcast_multiply_fusion = f32[16]{0:T(128)} fusion(f32[16]{0:T(128)} %get-tuple-element.17), kind=kLoop, calls=%fused_computation.102 | loop fusion | flops 16 | bytes 128 | tf_op jit(solution)/shard_map/div | solution.py:106
  23.2 1.2 %broadcast_minimum_fusion.2 = s32[16]{0:T(128)} fusion(s32[16]{0:T(128)} %get-tuple-element.22), kind=kLoop, calls=%fused_computation.101 | loop fusion | flops 16 | bytes 128 | tf_op jit(solution)/shard_map/min | solution.py:23
  24.5 1.2 %broadcast_minimum_fusion = s32[256]{0:T(256)} fusion(s32[256]{0:T(256)} %reduce_sum.158), kind=kLoop, calls=%fused_computation.96 | loop fusion | flops 256 | bytes 2048 | tf_op jit(solution)/shard_map/min | solution.py:23
  25.7 2.9 %fusion.5 = bf16[8,16,3072]{2,1,0:T(8,128)(2,1)} fusion(bf16[8,16,3072]{2,1,0:T(8,128)(2,1)} %collective-permute-done, pred[]{:T(512)S(6)} %eq.81, bf16[8,2,16,3072]{3,2,1,0:T(8,128)(2,1)} %bitcast.145), kind=kLoop, calls=%fused_computation.10 | loop fusion | flops 1966080 | bytes 3145729 | tf_op jit(solution)/shard_map/convert_element_type | solution.py:56
  28.6 10.0 %all-to-all-done = bf16[8,16,3200]{2,1,0:T(8,128)(2,1)} async-done(((bf16[8,16,3200]{2,1,0:T(8,128)(2,1)}), bf16[8,16,3200]{2,1,0:T(8,128)(2,1)}, u32[]{:S(2)}, u32[]{:S(2)}) %all-to-all-start) | async-done | bytes 819232 | tf_op jit(solution)/shard_map/all_to_all | solution.py:50
  38.6 1.9 %collective-permute-start.1 = (bf16[8,1,16,3200]{3,2,0,1:T(8,128)(2,1)}, bf16[8,1,16,3200]{3,2,0,1:T(8,128)(2,1)}, u32[]{:S(2)}, u32[]{:S(2)}) collective-permute-start(bf16[8,1,16,3200]{3,2,0,1:T(8,128)(2,1)} %bitcast.18), channel_id=1, source_target_pairs={{0,1},{1,0},{2,3},{3,2},{4,5},{5,4},{6,7},{7,6},{8,9},{9,8},{10,11... | collective-permute-start | bytes 2457608 | tf_op jit(solution)/shard_map/ppermute | solution.py:60
  40.5 1.3 %add_rsqrt_fusion.1 = f32[16]{0:T(128)} fusion(f32[16]{0:T(128)} %fusion.26), kind=kLoop, calls=%fused_computation.98 | loop fusion | flops 32 | bytes 128 | tf_op jit(solution)/shard_map/rsqrt | solution.py:15
  43.9 1.0 select_reduce_fusion.2
  45.4 1.3 %fusion.47 = f32[16]{0:T(128)} fusion(f32[16]{0:T(128)S(1)} %fusion.43, f32[16]{0:T(128)} %get-tuple-element.19, f32[16,8]{0,1:T(8,128)S(1)} %convert_element_type.128, f32[16]{0:T(128)} %copy-done.11), kind=kLoop, calls=%fused_computation.87 | loop fusion | flops 160 | bytes 320 | tf_op jit(solution)/shard_map/mul | solution.py:104
  46.7 4.2 %all-to-all-start.1 = ((bf16[8,16,3072]{2,1,0:T(8,128)(2,1)}), bf16[8,16,3072]{2,1,0:T(8,128)(2,1)}, u32[]{:S(2)}, u32[]{:S(2)}) async-start(bf16[8,16,3072]{2,1,0:T(8,128)(2,1)} %fusion.5), calls=%async_computation.1 | async-start | bytes 1572864 | tf_op jit(solution)/shard_map/all_to_all | solution.py:58
  50.9 2.3 %maximum_select_fusion = bf16[8,2,16,3200]{3,2,0,1:T(8,128)(2,1)S(1)} fusion(bf16[8,1,16,3200]{3,2,0,1:T(8,128)(2,1)} %collective-permute-done.1, bf16[8,1,16,3200]{3,2,0,1:T(8,128)(2,1)} %bitcast.18, pred[]{:T(512)S(6)} %eq.81), kind=kLoop, calls=%fused_computation.6 | loop fusion | flops 2457600 | bytes 3276801 | tf_op jit(solution)/shard_map/jit(_where)/select_n | solution.py:61
  53.4 1.2 %copy-done.2 = bf16[8,2,16,3200]{3,2,1,0:T(8,128)(2,1)} copy-done((bf16[8,2,16,3200]{3,2,1,0:T(8,128)(2,1)}, bf16[8,2,16,3200]{3,2,1,0:T(8,128)(2,1)S(1)}, u32[]{:S(2)}) %copy-start.2) | copy-done | bytes 1638424
  56.2 3.2 %fusion.10 = (bf16[1,256,512]{2,1,0:T(8,128)(2,1)}, f32[256]{0:T(256)S(1)}) fusion(f32[256]{0:T(256)S(1)} %bitcast.158, bf16[1,256,512]{2,1,0:T(8,128)(2,1)} %param.14, bf16[1,512,3072]{2,1,0:T(8,128)(2,1)S(1)} %copy-done, bf16[256,3200]{1,0:T(8,128)(2,1)} %bitcast.147), kind=kOutput, calls=%fused_computation.24 | convolution fusion | flops 805961472 | bytes 5244928 | tf_op jit(solution)/shard_map/dot_general | solution.py:70
  59.5 2.4 %collective-permute-start.2 = (f32[8,16]{1,0:T(8,128)S(1)}, f32[8,16]{1,0:T(8,128)S(1)}, u32[]{:S(2)}, u32[]{:S(2)}) collective-permute-start(f32[8,16]{1,0:T(8,128)S(1)} %bitcast.156), channel_id=1, source_target_pairs={{0,1},{1,0},{2,3},{3,2},{4,5},{5,4},{6,7},{7,6},{8,9},{9,8},{10,11... | collective-permute-start | bytes 1544 | tf_op jit(solution)/shard_map/ppermute | solution.py:78
  62.7 12.3 %all-to-all-done.1 = bf16[8,16,3072]{2,1,0:T(8,128)(2,1)} async-done(((bf16[8,16,3072]{2,1,0:T(8,128)(2,1)}), bf16[8,16,3072]{2,1,0:T(8,128)(2,1)}, u32[]{:S(2)}, u32[]{:S(2)}) %all-to-all-start.1) | async-done | bytes 786464 | tf_op jit(solution)/shard_map/all_to_all | solution.py:58
  75.0 2.4 %collective-permute-start.4 = (f32[4,16]{1,0:T(4,128)S(1)}, f32[4,16]{1,0:T(4,128)S(1)}, u32[]{:S(2)}, u32[]{:S(2)}) collective-permute-start(f32[4,16]{1,0:T(4,128)S(1)} %slice_select_fusion), channel_id=1, source_target_pairs={{0,8},{2,10},{4,12},{6,14},{8,0},{10,2},{12,4},{14,6},{1,9},{3,11}... | collective-permute-start | bytes 776 | tf_op jit(solution)/shard_map/ppermute | solution.py:87
  77.4 1.3 %convert_reduce_fusion = f32[16,3072]{1,0:T(8,128)S(1)} fusion(bf16[8,16,3072]{2,1,0:T(8,128)(2,1)} %bitcast.38), kind=kLoop, calls=%fused_computation.8 | loop fusion | flops 737280 | bytes 983040 | tf_op jit(solution)/shard_map/reduce_sum | solution.py:90
  78.7 5.7 %collective-permute-done.4 = f32[4,16]{1,0:T(4,128)S(1)} collective-permute-done((f32[4,16]{1,0:T(4,128)S(1)}, f32[4,16]{1,0:T(4,128)S(1)}, u32[]{:S(2)}, u32[]{:S(2)}) %collective-permute-start.4) | collective-permute-done | bytes 288 | tf_op jit(solution)/shard_map/ppermute | solution.py:87
  84.4 2.4 %collective-permute-start.5 = (f32[2,16]{1,0:T(2,128)S(1)}, f32[2,16]{1,0:T(2,128)S(1)}, u32[]{:S(2)}, u32[]{:S(2)}) collective-permute-start(f32[2,16]{1,0:T(2,128)S(1)} %broadcast_select_fusion.2), channel_id=1, source_target_pairs={{0,4},{2,6},{4,0},{6,2},{8,12},{10,14},{12,8},{14,10},{1,5},{3,7},... | collective-permute-start | bytes 392 | tf_op jit(solution)/shard_map/ppermute | solution.py:87
  87.5 3.3 %collective-permute-done.5 = f32[2,16]{1,0:T(2,128)S(1)} collective-permute-done((f32[2,16]{1,0:T(2,128)S(1)}, f32[2,16]{1,0:T(2,128)S(1)}, u32[]{:S(2)}, u32[]{:S(2)}) %collective-permute-start.5) | collective-permute-done | bytes 160 | tf_op jit(solution)/shard_map/ppermute | solution.py:87
  90.8 2.4 %collective-permute-start.6 = (f32[1,16]{1,0:T(1,128)S(1)}, f32[1,16]{1,0:T(1,128)S(1)}, u32[]{:S(2)}, u32[]{:S(2)}) collective-permute-start(f32[1,16]{1,0:T(1,128)S(1)} %broadcast_select_fusion.3), channel_id=1, source_target_pairs={{0,2},{2,0},{4,6},{6,4},{8,10},{10,8},{12,14},{14,12},{1,3},{3,1},... | collective-permute-start | bytes 200 | tf_op jit(solution)/shard_map/ppermute | solution.py:87
  93.2 5.4 %collective-permute-start.3 = (bf16[1,16,3072]{2,1,0:T(8,128)(2,1)S(1)}, bf16[1,16,3072]{2,1,0:T(8,128)(2,1)S(1)}, u32[]{:S(2)}, u32[]{:S(2)}) collective-permute-start(bf16[1,16,3072]{2,1,0:T(8,128)(2,1)S(1)} %fusion.29), channel_id=1, source_target_pairs={{0,16},{16,32},{32,48},{48,64},{64,80},{80,96},{96,112},{112,128},... | collective-permute-start | bytes 294920 | tf_op jit(solution)/shard_map/ppermute | solution.py:10
  98.7 1.0 fusion.35
  99.7 1.9 %collective-permute-start.7 = (bf16[1,16,3072]{2,1,0:T(8,128)(2,1)S(1)}, bf16[1,16,3072]{2,1,0:T(8,128)(2,1)S(1)}, u32[]{:S(2)}, u32[]{:S(2)}) collective-permute-start(bf16[1,16,3072]{2,1,0:T(8,128)(2,1)S(1)} %fusion.35), channel_id=1, source_target_pairs={{16,0},{32,16},{48,32},{64,48},{80,64},{96,80},{112,96},{128,112},... | collective-permute-start | bytes 294920 | tf_op jit(solution)/shard_map/ppermute | solution.py:10
  101.7 7.9 %collective-permute-done.7 = bf16[1,16,3072]{2,1,0:T(8,128)(2,1)S(1)} collective-permute-done((bf16[1,16,3072]{2,1,0:T(8,128)(2,1)S(1)}, bf16[1,16,3072]{2,1,0:T(8,128)(2,1)S(1)}, u32[]{:S(2)}, u32[]{:S(2)}) %collective-permute-start.7) | collective-permute-done | bytes 98336 | tf_op jit(solution)/shard_map/ppermute | solution.py:10
  (69 shorter events, 13.2 us)
Async XLA Ops:
  0.6 14.0 %copy-start = (bf16[1,512,3072]{2,1,0:T(8,128)(2,1)S(1)}, bf16[1,512,3072]{2,1,0:T(8,128)(2,1)}, u32[]{:S(2)}) copy-start(bf16[1,512,3072]{2,1,0:T(8,128)(2,1)} %param.19) | copy-start | bytes 9437188
  0.6 14.0 %copy-start.5 = (bf16[1,256,512]{2,1,0:T(8,128)(2,1)S(1)}, bf16[1,256,512]{2,1,0:T(8,128)(2,1)}, u32[]{:S(2)}) copy-start(bf16[1,256,512]{2,1,0:T(8,128)(2,1)} %param.11) | copy-start | bytes 786436
  2.1 13.6 %copy-start.14 = (s32[16]{0:T(128)}, s32[16]{0:T(128)S(1)}, u32[]{:S(2)}) copy-start(s32[16]{0:T(128)S(1)} %broadcast_minimum_fusion.1) | copy-start | bytes 196
  3.1 2.5 %copy-start.11 = (f32[16]{0:T(128)}, f32[16]{0:T(128)S(1)}, u32[]{:S(2)}) copy-start(f32[16]{0:T(128)S(1)} %fusion.23) | copy-start | bytes 196
  3.2 2.4 %copy-start.12 = (f32[16]{0:T(128)}, f32[16]{0:T(128)S(1)}, u32[]{:S(2)}) copy-start(f32[16]{0:T(128)S(1)} %add_rsqrt_fusion) | copy-start | bytes 196
  5.6 10.1 %copy-start.8 = (bf16[16,8]{0,1:T(8,128)(2,1)}, bf16[16,8]{0,1:T(8,128)(2,1)S(1)}, u32[]{:S(2)}) copy-start(bf16[16,8]{0,1:T(8,128)(2,1)S(1)} %get-tuple-element.20) | copy-start | bytes 772
  7.6 31.0 %all-to-all-start = ((bf16[8,16,3200]{2,1,0:T(8,128)(2,1)}), bf16[8,16,3200]{2,1,0:T(8,128)(2,1)}, u32[]{:S(2)}, u32[]{:S(2)}) async-start(bf16[8,16,3200]{2,1,0:T(8,128)(2,1)} %broadcast_in_dim.6), calls=%async_computation | async-start | bytes 1638400 | tf_op jit(solution)/shard_map/all_to_all | solution.py:50
  15.7 1.2 %copy-start.1 = (bf16[256,3072]{1,0:T(8,128)(2,1)}, bf16[256,3072]{1,0:T(8,128)(2,1)S(1)}, u32[]{:S(2)}) copy-start(bf16[256,3072]{1,0:T(8,128)(2,1)S(1)} %convolution_convert_fusion) | copy-start | bytes 4718596
  15.7 4.0 %copy-start.6 = (bf16[1,3072,8]{1,2,0:T(8,128)(2,1)S(1)}, bf16[1,3072,8]{1,2,0:T(8,128)(2,1)}, u32[]{:S(2)}) copy-start(bf16[1,3072,8]{1,2,0:T(8,128)(2,1)} %param.18) | copy-start | bytes 147460
  15.7 4.0 %copy-start.3 = (bf16[1,16,3072]{2,1,0:T(8,128)(2,1)S(1)}, bf16[1,16,3072]{2,1,0:T(8,128)(2,1)}, u32[]{:S(2)}) copy-start(bf16[1,16,3072]{2,1,0:T(8,128)(2,1)} %param.13) | copy-start | bytes 294916
  15.7 4.0 %copy-start.13 = (f32[16]{0:T(128)S(1)}, f32[16]{0:T(128)}, u32[]{:S(2)}) copy-start(f32[16]{0:T(128)} %copy-done.12) | copy-start | bytes 196
  15.7 5.0 %copy-start.4 = (bf16[1,16,3072]{2,1,0:T(8,128)(2,1)S(1)}, bf16[1,16,3072]{2,1,0:T(8,128)(2,1)}, u32[]{:S(2)}) copy-start(bf16[1,16,3072]{2,1,0:T(8,128)(2,1)} %param.10) | copy-start | bytes 294916
  15.7 5.7 %copy-start.7 = (s32[1,256,2]{1,2,0:T(2,128)S(1)}, s32[1,256,2]{1,2,0:T(2,128)}, u32[]{:S(2)}) copy-start(s32[1,256,2]{1,2,0:T(2,128)} %param.15) | copy-start | bytes 6148
  16.8 2.9 %copy-start.15 = (s32[16]{0:T(128)S(1)}, s32[16]{0:T(128)}, u32[]{:S(2)}) copy-start(s32[16]{0:T(128)} %copy-done.14) | copy-start | bytes 196
  17.8 7.9 %collective-permute-start = (bf16[8,16,3072]{2,1,0:T(8,128)(2,1)}, bf16[8,16,3072]{2,1,0:T(8,128)(2,1)}, u32[]{:S(2)}, u32[]{:S(2)}) collective-permute-start(bf16[8,16,3072]{2,1,0:T(8,128)(2,1)} %fusion.7), channel_id=1, source_target_pairs={{0,1},{1,0},{2,3},{3,2},{4,5},{5,4},{6,7},{7,6},{8,9},{9,8},{10,11... | collective-permute-start | bytes 2359304 | tf_op jit(solution)/shard_map/ppermute | solution.py:55
  38.6 12.4 %collective-permute-start.1 = (bf16[8,1,16,3200]{3,2,0,1:T(8,128)(2,1)}, bf16[8,1,16,3200]{3,2,0,1:T(8,128)(2,1)}, u32[]{:S(2)}, u32[]{:S(2)}) collective-permute-start(bf16[8,1,16,3200]{3,2,0,1:T(8,128)(2,1)} %bitcast.18), channel_id=1, source_target_pairs={{0,1},{1,0},{2,3},{3,2},{4,5},{5,4},{6,7},{7,6},{8,9},{9,8},{10,11... | collective-permute-start | bytes 2457608 | tf_op jit(solution)/shard_map/ppermute | solution.py:60
  46.7 28.3 %all-to-all-start.1 = ((bf16[8,16,3072]{2,1,0:T(8,128)(2,1)}), bf16[8,16,3072]{2,1,0:T(8,128)(2,1)}, u32[]{:S(2)}, u32[]{:S(2)}) async-start(bf16[8,16,3072]{2,1,0:T(8,128)(2,1)} %fusion.5), calls=%async_computation.1 | async-start | bytes 1572864 | tf_op jit(solution)/shard_map/all_to_all | solution.py:58
  53.2 2.9 %copy-start.10 = (s32[256]{0:T(256)S(1)}, s32[256]{0:T(256)}, u32[]{:S(2)}) copy-start(s32[256]{0:T(256)} %broadcast_minimum_fusion) | copy-start | bytes 3076
  53.2 2.9 %copy-start.9 = (f32[256]{0:T(256)S(1)}, f32[256]{0:T(256)}, u32[]{:S(2)}) copy-start(f32[256]{0:T(256)} %fusion.40) | copy-start | bytes 3076
  53.4 1.2 %copy-start.2 = (bf16[8,2,16,3200]{3,2,1,0:T(8,128)(2,1)}, bf16[8,2,16,3200]{3,2,1,0:T(8,128)(2,1)S(1)}, u32[]{:S(2)}) copy-start(bf16[8,2,16,3200]{3,2,1,0:T(8,128)(2,1)S(1)} %copy.37) | copy-start | bytes 4915204
  59.5 3.2 %collective-permute-start.2 = (f32[8,16]{1,0:T(8,128)S(1)}, f32[8,16]{1,0:T(8,128)S(1)}, u32[]{:S(2)}, u32[]{:S(2)}) collective-permute-start(f32[8,16]{1,0:T(8,128)S(1)} %bitcast.156), channel_id=1, source_target_pairs={{0,1},{1,0},{2,3},{3,2},{4,5},{5,4},{6,7},{7,6},{8,9},{9,8},{10,11... | collective-permute-start | bytes 1544 | tf_op jit(solution)/shard_map/ppermute | solution.py:78
  75.0 9.4 %collective-permute-start.4 = (f32[4,16]{1,0:T(4,128)S(1)}, f32[4,16]{1,0:T(4,128)S(1)}, u32[]{:S(2)}, u32[]{:S(2)}) collective-permute-start(f32[4,16]{1,0:T(4,128)S(1)} %slice_select_fusion), channel_id=1, source_target_pairs={{0,8},{2,10},{4,12},{6,14},{8,0},{10,2},{12,4},{14,6},{1,9},{3,11}... | collective-permute-start | bytes 776 | tf_op jit(solution)/shard_map/ppermute | solution.py:87
  84.4 6.4 %collective-permute-start.5 = (f32[2,16]{1,0:T(2,128)S(1)}, f32[2,16]{1,0:T(2,128)S(1)}, u32[]{:S(2)}, u32[]{:S(2)}) collective-permute-start(f32[2,16]{1,0:T(2,128)S(1)} %broadcast_select_fusion.2), channel_id=1, source_target_pairs={{0,4},{2,6},{4,0},{6,2},{8,12},{10,14},{12,8},{14,10},{1,5},{3,7},... | collective-permute-start | bytes 392 | tf_op jit(solution)/shard_map/ppermute | solution.py:87
  90.8 7.9 %collective-permute-start.6 = (f32[1,16]{1,0:T(1,128)S(1)}, f32[1,16]{1,0:T(1,128)S(1)}, u32[]{:S(2)}, u32[]{:S(2)}) collective-permute-start(f32[1,16]{1,0:T(1,128)S(1)} %broadcast_select_fusion.3), channel_id=1, source_target_pairs={{0,2},{2,0},{4,6},{6,4},{8,10},{10,8},{12,14},{14,12},{1,3},{3,1},... | collective-permute-start | bytes 200 | tf_op jit(solution)/shard_map/ppermute | solution.py:87
  93.2 8.4 %collective-permute-start.3 = (bf16[1,16,3072]{2,1,0:T(8,128)(2,1)S(1)}, bf16[1,16,3072]{2,1,0:T(8,128)(2,1)S(1)}, u32[]{:S(2)}, u32[]{:S(2)}) collective-permute-start(bf16[1,16,3072]{2,1,0:T(8,128)(2,1)S(1)} %fusion.29), channel_id=1, source_target_pairs={{0,16},{16,32},{32,48},{48,64},{64,80},{80,96},{96,112},{112,128},... | collective-permute-start | bytes 294920 | tf_op jit(solution)/shard_map/ppermute | solution.py:10
  99.7 9.8 %collective-permute-start.7 = (bf16[1,16,3072]{2,1,0:T(8,128)(2,1)S(1)}, bf16[1,16,3072]{2,1,0:T(8,128)(2,1)S(1)}, u32[]{:S(2)}, u32[]{:S(2)}) collective-permute-start(bf16[1,16,3072]{2,1,0:T(8,128)(2,1)S(1)} %fusion.35), channel_id=1, source_target_pairs={{16,0},{32,16},{48,32},{64,48},{80,64},{96,80},{112,96},{128,112},... | collective-permute-start | bytes 294920 | tf_op jit(solution)/shard_map/ppermute | solution.py:10
